TPU v7x, 512 devices: a whole 4x8x8 slice. The times are simulated.
512 devices in a mesh: head: 16 (over y, core), seq: 32 (over z, x).
Axes of the slice: x: 4, y: 8, z: 8, core: 2. Of those that a mesh axis runs over, the one named last changes fastest.
Arguments:
- queries: bfloat16 [32768, 2048], P(('seq', 'head'))
- keys: bfloat16 [32768, 2048], P(('seq', 'head'))
- values: bfloat16 [32768, 2048], P(('seq', 'head')), may hold values from -6 to 6
- grad_out: bfloat16 [32768, 2048], P(('seq', 'head')), may hold values from -6 to 6
- random_blocks: int32 [256, 3], P('seq'), may hold values from 0 to 255, as said below
Outputs:
- attended: bfloat16 [32768, 2048], P(('seq', 'head'))
- grad_queries: bfloat16 [32768, 2048], P(('seq', 'head'))
- grad_keys: bfloat16 [32768, 2048], P(('seq', 'head'))
- grad_values: bfloat16 [32768, 2048], P(('seq', 'head'))
Inputs may be any that keep to these rules, and one draw needn't show every extreme that they name: `random_blocks`: within the rows of one sequence group (8 consecutive query blocks), at most 2 entries name blocks of any one group's range of 8 blocks, and in every group's rows one group's range is named exactly 2 times.
All inputs are finite; a program needn't handle non-finite values.
Results may differ from a plain program's by a relative error of at most 0.022.
Values may be sent and summed in bfloat16 or wider, within the bound.
No kernel may reach another device: no remote copies, remote signals or barrier semaphores. Data moves between devices by JAX's collectives and lax.ppermute only.
A program may use at most 192 MiB of HBM per device.

v0:
```python
import jax
import jax.numpy as jnp
from jax import lax
from jax.sharding import PartitionSpec as P

HD = 128
BLK = 128
RAND = 3


def with_halo(cells, sides, width):
    for axis, dim in sides:
        count = lax.axis_size(axis)
        ends = count - 1
        head = lax.slice_in_dim(cells, 0, width, axis=dim)
        tail = lax.slice_in_dim(cells, cells.shape[dim] - width, cells.shape[dim], axis=dim)
        cells = jnp.concatenate(
            [
                lax.ppermute(tail, axis, [(i, (i + 1) % count) for i in range(ends)]),
                cells,
                lax.ppermute(head, axis, [((i + 1) % count, i) for i in range(ends)]),
            ],
            axis=dim,
        )
    return cells


def row_width(count):
    return 4 if count % 4 == 0 else 1


def broadcast(value, axis):
    count = lax.axis_size(axis)
    me = lax.axis_index(axis)
    width = row_width(count)
    got = jnp.zeros_like(value)
    for row in range(1, count // width):
        got = got + lax.ppermute(value, axis, [(0, row * width)])
    value = jnp.where(me == 0, value, got)
    got = jnp.zeros_like(value)
    for col in range(1, width):
        pairs = [(row * width, row * width + col) for row in range(count // width)]
        got = got + lax.ppermute(value, axis, pairs)
    return jnp.where(me % width == 0, value, got)


def reduce_to_first(value, axis):
    count = lax.axis_size(axis)
    width = row_width(count)
    total = value
    for col in range(1, width):
        pairs = [(row * width + col, row * width) for row in range(count // width)]
        total = total + lax.ppermute(value, axis, pairs)
    value = total
    for row in range(1, count // width):
        total = total + lax.ppermute(value, axis, [(row * width, 0)])
    return total


def slot_places(owners, groups, capacity):
    owner_hits = (owners[:, None] == jnp.arange(groups, dtype=jnp.int32)[None, :]).astype(jnp.int32)
    earlier = jnp.cumsum(owner_hits, axis=0) - owner_hits
    return owners * capacity + jnp.sum(earlier * owner_hits, axis=1)


def request_table(list_rows, query_count, groups, capacity):
    flat_rows = list_rows.reshape(-1)
    places = slot_places(flat_rows // query_count, groups, capacity)
    matches = places[None, :] == jnp.arange(groups * capacity, dtype=jnp.int32)[:, None]
    table = jnp.sum(jnp.where(matches, (flat_rows % query_count)[None, :], 0), axis=1)
    return table.reshape(groups, capacity)


def window_valid(my_group, query_count, groups):
    block_ids = jnp.arange(query_count, dtype=jnp.int32)
    left_ok = jnp.logical_not(jnp.logical_and(my_group == 0, block_ids == 0))
    right_ok = jnp.logical_not(
        jnp.logical_and(my_group == groups - 1, block_ids == query_count - 1)
    )
    all_true = jnp.ones((query_count, BLK), dtype=bool)
    return jnp.concatenate(
        [
            all_true,
            all_true,
            left_ok[:, None] & all_true,
            all_true,
            right_ok[:, None] & all_true,
            jnp.ones((query_count, RAND * BLK), dtype=bool),
        ],
        axis=1,
    )


def against_keys(rows, global_part, window_part, remote_part):
    return jnp.concatenate(
        [
            jnp.einsum("qihd,jhd->qhij", rows, global_part, preferred_element_type=jnp.float32),
            jnp.einsum("qihd,qjhd->qhij", rows, window_part, preferred_element_type=jnp.float32),
            jnp.einsum("qihd,qjhd->qhij", rows, remote_part, preferred_element_type=jnp.float32),
        ],
        axis=-1,
    )


def split_keys(table):
    return (table[..., : 2 * BLK], table[..., 2 * BLK : 5 * BLK], table[..., 5 * BLK :])


def weigh_keys(table, global_part, window_part, remote_part):
    global_w, window_w, random_w = split_keys(table)
    return (
        jnp.einsum("qhij,jhd->qihd", global_w, global_part, preferred_element_type=jnp.float32)
        + jnp.einsum("qhij,qjhd->qihd", window_w, window_part, preferred_element_type=jnp.float32)
        + jnp.einsum("qhij,qjhd->qihd", random_w, remote_part, preferred_element_type=jnp.float32)
    )


def key_terms(table, rows):
    global_w, window_w, random_w = split_keys(table)
    return (
        jnp.einsum("qhij,qihd->jhd", global_w, rows, preferred_element_type=jnp.float32),
        jnp.einsum("qhij,qihd->qjhd", window_w, rows, preferred_element_type=jnp.float32),
        jnp.einsum("qhij,qihd->qjhd", random_w, rows, preferred_element_type=jnp.float32),
    )


def shards(queries, keys, values, grad_out, random_blocks):
    groups = lax.axis_size("seq")
    my_group = lax.axis_index("seq")
    head_q, head_k, head_v, head_g = lax.all_to_all(
        jnp.stack([queries, keys, values, grad_out]), "head", split_axis=2, concat_axis=1, tiled=True
    )
    group_tokens = head_q.shape[0]
    head_count = head_q.shape[1] // HD
    query_count = group_tokens // BLK
    capacity = max(2, 3 * query_count * RAND // (2 * groups))
    score_scale = HD ** (-0.5)
    ordered_table, head_k = lax.optimization_barrier(
        (request_table(random_blocks, query_count, groups, capacity), head_k)
    )
    key_value = jnp.stack([head_k, head_v])
    kv_blocks = key_value.reshape(2, query_count, BLK, head_count, HD)
    edged = with_halo(key_value, (("seq", 1),), BLK)
    edged = edged.reshape(2, query_count + 2, BLK, head_count, HD)
    window_kv = jnp.concatenate(
        [edged[:, 0:query_count], edged[:, 1 : query_count + 1], edged[:, 2 : query_count + 2]],
        axis=2,
    )
    global_kv = broadcast(kv_blocks[:, 0:2].reshape(2, 2 * BLK, head_count, HD), "seq")
    flat_ids = random_blocks.reshape(-1)
    places = slot_places(flat_ids // query_count, groups, capacity)
    table = ordered_table
    wanted = lax.all_to_all(
        table,
        "seq",
        split_axis=0,
        concat_axis=0,
        tiled=True,
    )
    served = jnp.take(kv_blocks, wanted.reshape(-1), axis=1)
    served = served.reshape(2, groups, capacity, BLK, head_count, HD)
    served, global_kv = lax.optimization_barrier((served, global_kv))
    fetched = lax.all_to_all(served, "seq", split_axis=1, concat_axis=1, tiled=True)
    chosen = jnp.take(fetched.reshape(2, groups * capacity, BLK, head_count, HD), places, axis=1)
    remote_kv = chosen.reshape(2, query_count, RAND * BLK, head_count, HD)
    query_blocks = head_q.reshape(query_count, BLK, head_count, HD)
    grad_blocks = head_g.reshape(query_count, BLK, head_count, HD)
    scores = score_scale * against_keys(query_blocks, global_kv[0], window_kv[0], remote_kv[0])
    valid = window_valid(my_group, query_count, groups)
    scores = jnp.where(valid[:, None, None, :], scores, -jnp.inf)
    row_max = jnp.max(scores, axis=-1, keepdims=True)
    exponent = jnp.exp(scores - row_max)
    attention_probs = exponent / jnp.sum(exponent, axis=-1, keepdims=True)
    weights = attention_probs.astype(jnp.bfloat16)
    attended = weigh_keys(weights, global_kv[1], window_kv[1], remote_kv[1]).astype(jnp.bfloat16)
    grad_prob = against_keys(grad_blocks, global_kv[1], window_kv[1], remote_kv[1])
    row_delta = jnp.sum(attention_probs * grad_prob, axis=-1, keepdims=True)
    grad_score = (score_scale * attention_probs * (grad_prob - row_delta)).astype(jnp.bfloat16)
    grad_q = weigh_keys(grad_score, global_kv[0], window_kv[0], remote_kv[0]).astype(jnp.bfloat16)
    key_global, key_window, key_random = key_terms(grad_score, query_blocks)
    value_global, value_window, value_random = key_terms(weights, grad_blocks)
    global_sum = reduce_to_first(jnp.stack([key_global, value_global]), "seq")
    window_grad = jnp.stack([key_window, value_window]).reshape(
        2, query_count, 3, BLK, head_count, HD
    )
    no_pad = (0, 0)
    extended = (
        jnp.pad(window_grad[:, :, 0], (no_pad, (0, 2), no_pad, no_pad, no_pad))
        + jnp.pad(window_grad[:, :, 1], (no_pad, (1, 1), no_pad, no_pad, no_pad))
        + jnp.pad(window_grad[:, :, 2], (no_pad, (2, 0), no_pad, no_pad, no_pad))
    )
    outward = jnp.concatenate([extended[:, 0], extended[:, query_count + 1]], axis=1)
    inward = with_halo(outward.astype(jnp.bfloat16), (("seq", 1),), BLK).astype(outward.dtype)
    own_grad = extended[:, 1 : query_count + 1]
    own_grad = own_grad.at[:, 0].add(inward[:, :BLK])
    own_grad = own_grad.at[:, query_count - 1].add(inward[:, 3 * BLK :])
    random_terms = (
        jnp.stack([key_random, value_random])
        .reshape(2, query_count * RAND, BLK, head_count, HD)
        .astype(jnp.bfloat16)
    )
    send_pick = (places[None, :] == jnp.arange(groups * capacity, dtype=jnp.int32)[:, None]).astype(
        jnp.bfloat16
    )
    outgoing = jnp.einsum(
        "pj,xjihd->xpihd", send_pick, random_terms, preferred_element_type=jnp.float32
    ).astype(jnp.bfloat16)
    incoming = lax.all_to_all(
        outgoing.reshape(2, groups, capacity, BLK, head_count, HD),
        "seq",
        split_axis=1,
        concat_axis=1,
        tiled=True,
    )
    take_pick = (
        wanted.reshape(-1)[None, :] == jnp.arange(query_count, dtype=jnp.int32)[:, None]
    ).astype(jnp.bfloat16)
    random_sum = jnp.einsum(
        "qp,xpihd->xqihd",
        take_pick,
        incoming.reshape(2, groups * capacity, BLK, head_count, HD),
        preferred_element_type=jnp.float32,
    )
    global_sum = global_sum.reshape(2, 2, BLK, head_count, HD)
    own_grad = own_grad.at[:, 0:2].add(jnp.where(my_group == 0, global_sum, 0.0))
    total_grad = own_grad + random_sum
    grad_k = total_grad[0].reshape(group_tokens, head_count * HD).astype(jnp.bfloat16)
    grad_v = total_grad[1].reshape(group_tokens, head_count * HD).astype(jnp.bfloat16)
    results = lax.all_to_all(
        jnp.stack([attended.reshape(group_tokens, head_count * HD),
                   grad_q.reshape(group_tokens, head_count * HD), grad_k, grad_v]),
        "head",
        split_axis=1,
        concat_axis=2,
        tiled=True,
    )
    return results[0], results[1], results[2], results[3]


def solution(mesh):
    placed = (
        P(("seq", "head"), None),
        P(("seq", "head"), None),
        P(("seq", "head"), None),
        P(("seq", "head"), None),
        P("seq", None),
    )
    return jax.shard_map(
        shards,
        mesh=mesh,
        in_specs=placed,
        out_specs=(
            P(("seq", "head"), None),
            P(("seq", "head"), None),
            P(("seq", "head"), None),
            P(("seq", "head"), None),
        ),
        check_vma=False,
    )
```

profile of v0, /device:TPU:1, one launch (start us, length us, event | category | flops | bytes accessed | tf_op | source)
XLA Modules:
  0.0 429.1 jit_solution(15551641921848663375)
XLA Ops:
  0.6 1.3 pad_maximum_fusion.3
  2.0 1.4 copy.158
  3.4 2.3 reshape.1021
  5.6 10.3 %all-to-all-start = ((bf16[16,2,16384]{2,1,0:T(2,128)(2,1)}), bf16[16,2,16384]{2,1,0:T(2,128)(2,1)S(1)}, u32[]{:S(2)}, u32[]{:S(2)}) async-start(bf16[16,2,16384]{2,1,0:T(2,128)(2,1)} %reshape.1021), calls=%async_computation | async-start | bytes 2097152 | tf_op jit(solution)/shard_map/all_to_all | solution.py:130
  17.3 26.7 %all-to-all-done = bf16[16,2,16384]{2,1,0:T(2,128)(2,1)S(1)} async-done(((bf16[16,2,16384]{2,1,0:T(2,128)(2,1)}), bf16[16,2,16384]{2,1,0:T(2,128)(2,1)S(1)}, u32[]{:S(2)}, u32[]{:S(2)}) %all-to-all-start) | async-done | bytes 1048608 | tf_op jit(solution)/shard_map/all_to_all | solution.py:130
  43.9 1.3 reshape.1022
  45.3 2.3 copy.159
  48.9 8.9 %collective-permute-start.6 = (bf16[2,256,1,128]{3,1,2,0:T(8,128)(2,1)S(1)}, bf16[2,256,1,128]{3,1,2,0:T(8,128)(2,1)S(1)}, u32[]{:S(2)}, u32[]{:S(2)}) collective-permute-start(bf16[2,256,1,128]{3,1,2,0:T(8,128)(2,1)S(1)} %bitcast.318), channel_id=1, source_target_pairs={{0,28},{32,60},{64,92},{96,124},{128,156},{160,188},{192,220},{224... | collective-permute-start | bytes 393224 | tf_op jit(solution)/shard_map/ppermute | solution.py:38
  57.8 1.3 collective-permute-start.5
  59.1 1.3 collective-permute-start.4
  60.4 1.3 collective-permute-start.3
  61.7 1.3 collective-permute-start.2
  63.0 3.8 all-to-all-start.1
  66.9 8.4 %all-to-all-done.1 = s32[32,1,2]{2,1,0:T(1,128)S(1)} async-done(((s32[32,1,2]{2,1,0:T(1,128)}), s32[32,1,2]{2,1,0:T(1,128)S(1)}, u32[]{:S(2)}, u32[]{:S(2)}) %all-to-all-start.1) | async-done | bytes 288 | tf_op jit(solution)/shard_map/all_to_all | solution.py:153
  76.8 2.3 collective-permute-start.1
  79.2 1.3 collective-permute-start
  80.6 3.1 gather_fusion
  83.6 2.7 copy.164
  86.5 1.3 collective-permute-start.9
  87.8 1.3 collective-permute-start.8
  89.1 1.3 collective-permute-start.7
  91.8 2.8 collective-permute-done.7
  94.6 2.5 copy.165
  97.1 4.9 %all-to-all-start.2 = ((bf16[2,32,2,128,1,128]{5,3,2,0,4,1:T(8,128)(2,1)}), bf16[2,32,2,128,1,128]{5,3,2,0,4,1:T(8,128)(2,1)}, u32[]{:S(2)}, u32[]{:S(2)}) async-start(bf16[2,32,2,128,1,128]{5,3,2,0,4,1:T(8,128)(2,1)} %copy.165), calls=%async_computation.2 | async-start | bytes 8388608 | tf_op jit(solution)/shard_map/all_to_all | solution.py:163
  102.3 3.9 collective-permute-start.10
  107.6 5.7 %collective-permute-done.10 = bf16[2,128,128]{2,1,0:T(8,128)(2,1)S(1)} collective-permute-done((bf16[2,128,128]{2,1,0:T(8,128)(2,1)S(1)}, bf16[2,128,128]{2,1,0:T(8,128)(2,1)S(1)}, u32[]{:S(2)}, u32[]{:S(2)}) %collective-permute-start.10) | collective-permute-done | bytes 65568 | tf_op jit(solution)/shard_map/ppermute | solution.py:19
  113.3 5.2 %collective-permute-done.11 = bf16[2,128,128]{2,1,0:T(8,128)(2,1)S(1)} collective-permute-done((bf16[2,128,128]{2,1,0:T(8,128)(2,1)S(1)}, bf16[2,128,128]{2,1,0:T(8,128)(2,1)S(1)}, u32[]{:S(2)}, u32[]{:S(2)}) %collective-permute-start.11) | collective-permute-done | bytes 65568 | tf_op jit(solution)/shard_map/ppermute | solution.py:21
  119.6 1.6 convolution_bitcast_fusion.3
  121.2 1.3 convolution_bitcast_fusion.8
  122.6 1.6 copy.168
  124.1 1.3 convolution_bitcast_fusion.7
  125.5 69.6 %all-to-all-done.2 = bf16[2,32,2,128,1,128]{5,3,2,0,4,1:T(8,128)(2,1)} async-done(((bf16[2,32,2,128,1,128]{5,3,2,0,4,1:T(8,128)(2,1)}), bf16[2,32,2,128,1,128]{5,3,2,0,4,1:T(8,128)(2,1)}, u32[]{:S(2)}, u32[]{:S(2)}) %all-to-all-start.2) | async-done | bytes 4194336 | tf_op jit(solution)/shard_map/all_to_all | solution.py:163
  195.1 4.8 %copy.166 = bf16[2,32,2,128,1,128]{5,3,2,1,0,4:T(8,128)(2,1)} copy(bf16[2,32,2,128,1,128]{5,3,2,0,4,1:T(8,128)(2,1)} %all-to-all-done.2) | data formatting | bytes 8388608 | tf_op jit(solution)/shard_map/all_to_all | solution.py:163
  199.9 4.2 gather_fusion.1
  204.1 1.6 bitcast_select_fusion
  207.8 1.4 fusion.2
  210.9 1.7 multiply_reduce_fusion
  212.6 3.0 multiply_convert_fusion
  215.6 1.7 fusion.8
  218.5 2.6 copy.188
  222.7 1.7 copy.189
  224.4 1.4 convolution_convert_fusion
  225.8 6.7 %copy.190 = bf16[2,32,2,128,1,128]{5,2,3,0,4,1:T(2,128)(2,1)} copy(bf16[2,32,2,128,1,128]{5,2,1,3,0,4:T(2,128)(2,1)S(1)} %bitcast.270) | data formatting | bytes 8388608 | tf_op jit(solution)/shard_map/reshape | solution.py:209
  232.4 15.9 %all-to-all-start.3 = ((bf16[2,32,2,128,1,128]{5,2,3,0,4,1:T(2,128)(2,1)}), bf16[2,32,2,128,1,128]{5,2,3,0,4,1:T(2,128)(2,1)}, u32[]{:S(2)}, u32[]{:S(2)}) async-start(bf16[2,32,2,128,1,128]{5,2,3,0,4,1:T(2,128)(2,1)} %copy.190), calls=%async_computation.3 | async-start | bytes 8388608 | tf_op jit(solution)/shard_map/all_to_all | solution.py:208
  248.5 1.4 convolution_bitcast_fusion.16
  253.5 1.5 collective-permute-start.14
  255.1 2.7 convolution_bitcast_fusion.1
  257.7 3.1 copy.171
  260.8 1.6 convolution_bitcast_fusion
  262.4 3.0 copy.173
  265.4 2.0 fusion.17
  268.0 4.6 %collective-permute-start.12 = (bf16[2,128,1,128]{3,1,0,2:T(8,128)(2,1)S(1)}, bf16[2,128,1,128]{3,1,0,2:T(8,128)(2,1)S(1)}, u32[]{:S(2)}, u32[]{:S(2)}) collective-permute-start(bf16[2,128,1,128]{3,1,0,2:T(8,128)(2,1)S(1)} %get-tuple-element.57), channel_id=1, source_target_pairs={{0,1},{1,2},{2,3},{3,4},{4,5},{5,6},{6,7},{7,8},{8,9},{9,10},{10,1... | collective-permute-start | bytes 196616 | tf_op jit(solution)/shard_map/ppermute | solution.py:19
  272.6 1.3 convolution_bitcast_fusion.13
  274.7 1.6 convolution_bitcast_fusion.9
  276.3 1.5 fusion.14
  277.8 9.9 %collective-permute-done.16 = f32[2,256,1,128]{3,1,2,0:T(8,128)} collective-permute-done((f32[2,256,1,128]{3,1,2,0:T(8,128)}, f32[2,256,1,128]{3,1,2,0:T(8,128)}, u32[]{:S(2)}, u32[]{:S(2)}) %collective-permute-start.16) | collective-permute-done | bytes 262176 | tf_op jit(solution)/shard_map/ppermute | solution.py:53
  296.5 1.5 collective-permute-done.13
  299.3 64.2 %collective-permute-done.23 = f32[2,256,1,128]{3,1,2,0:T(8,128)S(1)} collective-permute-done((f32[2,256,1,128]{3,1,2,0:T(8,128)S(1)}, f32[2,256,1,128]{3,1,2,0:T(8,128)S(1)}, u32[]{:S(2)}, u32[]{:S(2)}) %collective-permute-start.23) | collective-permute-done | bytes 262176 | tf_op jit(solution)/shard_map/ppermute | solution.py:56
  366.9 3.0 scatter-add.11
  369.9 2.9 collective-permute-done.18
  372.8 7.4 %collective-permute-done.17 = f32[2,256,1,128]{3,1,2,0:T(8,128)} collective-permute-done((f32[2,256,1,128]{3,1,2,0:T(8,128)S(1)}, f32[2,256,1,128]{3,1,2,0:T(8,128)}, u32[]{:S(2)}, u32[]{:S(2)}) %collective-permute-start.17) | collective-permute-done | bytes 262176 | tf_op jit(solution)/shard_map/ppermute | solution.py:56
  381.7 7.0 %copy.191 = bf16[2,32,2,128,1,128]{5,2,1,3,0,4:T(2,128)(2,1)S(1)} copy(bf16[2,32,2,128,1,128]{5,2,3,0,4,1:T(2,128)(2,1)} %all-to-all-done.3) | data formatting | bytes 8388608 | tf_op jit(solution)/shard_map/all_to_all | solution.py:208
  391.2 31.3 %all_to_all.49 = bf16[4,1024,128]{2,0,1:T(4,128)(2,1)S(1)} all-to-all(bf16[4,1024,128]{2,0,1:T(4,128)(2,1)S(1)} %copy.194), channel_id=1, replica_groups=mesh['head'=16,'seq'=32] {'head'}, dimensions={1} | all-to-all | bytes 2097152 | tf_op jit(solution)/shard_map/all_to_all | solution.py:229
  422.5 2.2 fusion.49
  (141 shorter events, 41.4 us)
Async XLA Ops:
  3.4 12.6 %copy-start.16 = (s32[8,3]{0,1:T(4,128)S(1)}, s32[8,3]{0,1:T(4,128)}, u32[]{:S(2)}) copy-start(s32[8,3]{0,1:T(4,128)} %param.15) | copy-start | bytes 292
  5.6 38.3 %all-to-all-start = ((bf16[16,2,16384]{2,1,0:T(2,128)(2,1)}), bf16[16,2,16384]{2,1,0:T(2,128)(2,1)S(1)}, u32[]{:S(2)}, u32[]{:S(2)}) async-start(bf16[16,2,16384]{2,1,0:T(2,128)(2,1)} %reshape.1021), calls=%async_computation | async-start | bytes 2097152 | tf_op jit(solution)/shard_map/all_to_all | solution.py:130
  48.8 157.0 %copy-start.4 = (bf16[1,16,64,128]{3,2,1,0:T(8,128)(2,1)}, bf16[1,16,64,128]{3,2,1,0:T(8,128)(2,1)S(1)}, u32[]{:S(2)}) copy-start(bf16[1,16,64,128]{3,2,1,0:T(8,128)(2,1)S(1)} %get-tuple-element.67) | copy-start | bytes 786436
  48.9 27.9 %collective-permute-start.6 = (bf16[2,256,1,128]{3,1,2,0:T(8,128)(2,1)S(1)}, bf16[2,256,1,128]{3,1,2,0:T(8,128)(2,1)S(1)}, u32[]{:S(2)}, u32[]{:S(2)}) collective-permute-start(bf16[2,256,1,128]{3,1,2,0:T(8,128)(2,1)S(1)} %bitcast.318), channel_id=1, source_target_pairs={{0,28},{32,60},{64,92},{96,124},{128,156},{160,188},{192,220},{224... | collective-permute-start | bytes 393224 | tf_op jit(solution)/shard_map/ppermute | solution.py:38
  57.8 21.3 %collective-permute-start.5 = (bf16[2,256,1,128]{3,1,2,0:T(8,128)(2,1)S(1)}, bf16[2,256,1,128]{3,1,2,0:T(8,128)(2,1)S(1)}, u32[]{:S(2)}, u32[]{:S(2)}) collective-permute-start(bf16[2,256,1,128]{3,1,2,0:T(8,128)(2,1)S(1)} %bitcast.319), channel_id=1, source_target_pairs={{0,24},{32,56},{64,88},{96,120},{128,152},{160,184},{192,216},{224... | collective-permute-start | bytes 393224 | tf_op jit(solution)/shard_map/ppermute | solution.py:38
  59.1 27.3 %collective-permute-start.4 = (bf16[2,256,1,128]{3,1,2,0:T(8,128)(2,1)S(1)}, bf16[2,256,1,128]{3,1,2,0:T(8,128)(2,1)S(1)}, u32[]{:S(2)}, u32[]{:S(2)}) collective-permute-start(bf16[2,256,1,128]{3,1,2,0:T(8,128)(2,1)S(1)} %bitcast.320), channel_id=1, source_target_pairs={{0,20},{32,52},{64,84},{96,116},{128,148},{160,180},{192,212},{224... | collective-permute-start | bytes 393224 | tf_op jit(solution)/shard_map/ppermute | solution.py:38
  60.4 26.0 %collective-permute-start.3 = (bf16[2,256,1,128]{3,1,2,0:T(8,128)(2,1)S(1)}, bf16[2,256,1,128]{3,1,2,0:T(8,128)(2,1)S(1)}, u32[]{:S(2)}, u32[]{:S(2)}) collective-permute-start(bf16[2,256,1,128]{3,1,2,0:T(8,128)(2,1)S(1)} %bitcast.321), channel_id=1, source_target_pairs={{0,16},{32,48},{64,80},{96,112},{128,144},{160,176},{192,208},{224... | collective-permute-start | bytes 393224 | tf_op jit(solution)/shard_map/ppermute | solution.py:38
  61.7 24.7 %collective-permute-start.2 = (bf16[2,256,1,128]{3,1,2,0:T(8,128)(2,1)S(1)}, bf16[2,256,1,128]{3,1,2,0:T(8,128)(2,1)S(1)}, u32[]{:S(2)}, u32[]{:S(2)}) collective-permute-start(bf16[2,256,1,128]{3,1,2,0:T(8,128)(2,1)S(1)} %bitcast.322), channel_id=1, source_target_pairs={{0,12},{32,44},{64,76},{96,108},{128,140},{160,172},{192,204},{224... | collective-permute-start | bytes 393224 | tf_op jit(solution)/shard_map/ppermute | solution.py:38
  63.0 12.3 %all-to-all-start.1 = ((s32[32,1,2]{2,1,0:T(1,128)}), s32[32,1,2]{2,1,0:T(1,128)S(1)}, u32[]{:S(2)}, u32[]{:S(2)}) async-start(s32[32,1,2]{2,1,0:T(1,128)} %bitcast.112), calls=%async_computation.1 | async-start | bytes 32768 | tf_op jit(solution)/shard_map/all_to_all | solution.py:153
  76.8 9.6 %collective-permute-start.1 = (bf16[2,256,1,128]{3,1,2,0:T(8,128)(2,1)S(1)}, bf16[2,256,1,128]{3,1,2,0:T(8,128)(2,1)S(1)}, u32[]{:S(2)}, u32[]{:S(2)}) collective-permute-start(bf16[2,256,1,128]{3,1,2,0:T(8,128)(2,1)S(1)} %bitcast.323), channel_id=1, source_target_pairs={{0,8},{32,40},{64,72},{96,104},{128,136},{160,168},{192,200},{224,... | collective-permute-start | bytes 393224 | tf_op jit(solution)/shard_map/ppermute | solution.py:38
  79.2 7.3 %collective-permute-start = (bf16[2,256,1,128]{3,1,2,0:T(8,128)(2,1)S(1)}, bf16[2,256,1,128]{3,1,2,0:T(8,128)(2,1)S(1)}, u32[]{:S(2)}, u32[]{:S(2)}) collective-permute-start(bf16[2,256,1,128]{3,1,2,0:T(8,128)(2,1)S(1)} %bitcast.324), channel_id=1, source_target_pairs={{0,4},{32,36},{64,68},{96,100},{128,132},{160,164},{192,196},{224,... | collective-permute-start | bytes 393224 | tf_op jit(solution)/shard_map/ppermute | solution.py:38
  86.5 4.4 %collective-permute-start.9 = (bf16[2,256,1,128]{3,1,2,0:T(8,128)(2,1)S(1)}, bf16[2,256,1,128]{3,1,2,0:T(8,128)(2,1)S(1)}, u32[]{:S(2)}, u32[]{:S(2)}) collective-permute-start(bf16[2,256,1,128]{3,1,2,0:T(8,128)(2,1)S(1)} %add_select_fusion.2), channel_id=1, source_target_pairs={{0,3},{4,7},{8,11},{12,15},{16,19},{20,23},{24,27},{28,31},{32,35}... | collective-permute-start | bytes 393224 | tf_op jit(solution)/shard_map/ppermute | solution.py:43
  87.8 4.0 collective-permute-start.8
  89.1 5.5 %collective-permute-start.7 = (bf16[2,256,1,128]{3,1,2,0:T(8,128)(2,1)S(1)}, bf16[2,256,1,128]{3,1,2,0:T(8,128)(2,1)S(1)}, u32[]{:S(2)}, u32[]{:S(2)}) collective-permute-start(bf16[2,256,1,128]{3,1,2,0:T(8,128)(2,1)S(1)} %add_select_fusion.2), channel_id=1, source_target_pairs={{0,1},{4,5},{8,9},{12,13},{16,17},{20,21},{24,25},{28,29},{32,33},... | collective-permute-start | bytes 393224 | tf_op jit(solution)/shard_map/ppermute | solution.py:43
  97.1 97.9 %all-to-all-start.2 = ((bf16[2,32,2,128,1,128]{5,3,2,0,4,1:T(8,128)(2,1)}), bf16[2,32,2,128,1,128]{5,3,2,0,4,1:T(8,128)(2,1)}, u32[]{:S(2)}, u32[]{:S(2)}) async-start(bf16[2,32,2,128,1,128]{5,3,2,0,4,1:T(8,128)(2,1)} %copy.165), calls=%async_computation.2 | async-start | bytes 8388608 | tf_op jit(solution)/shard_map/all_to_all | solution.py:163
  102.3 11.0 %collective-permute-start.10 = (bf16[2,128,128]{2,1,0:T(8,128)(2,1)S(1)}, bf16[2,128,128]{2,1,0:T(8,128)(2,1)S(1)}, u32[]{:S(2)}, u32[]{:S(2)}) collective-permute-start(bf16[2,128,128]{2,1,0:T(8,128)(2,1)S(1)} %get-tuple-element.74), channel_id=1, source_target_pairs={{0,1},{1,2},{2,3},{3,4},{4,5},{5,6},{6,7},{7,8},{8,9},{9,10},{10,1... | collective-permute-start | bytes 196616 | tf_op jit(solution)/shard_map/ppermute | solution.py:19
  106.3 12.3 %collective-permute-start.11 = (bf16[2,128,128]{2,1,0:T(8,128)(2,1)S(1)}, bf16[2,128,128]{2,1,0:T(8,128)(2,1)S(1)}, u32[]{:S(2)}, u32[]{:S(2)}) collective-permute-start(bf16[2,128,128]{2,1,0:T(8,128)(2,1)S(1)} %get-tuple-element.75), channel_id=1, source_target_pairs={{1,0},{2,1},{3,2},{4,3},{5,4},{6,5},{7,6},{8,7},{9,8},{10,9},{11,1... | collective-permute-start | bytes 196616 | tf_op jit(solution)/shard_map/ppermute | solution.py:21
  119.1 2.1 copy-start.1
  205.9 0.9 copy-start.8
  205.9 3.3 copy-start.10
  209.2 1.4 copy-start.3
  209.2 1.7 copy-start.7
  212.6 3.1 copy-start.5
  215.6 5.5 %copy-start = (bf16[8,1,128,1024]{3,2,0,1:T(8,128)(2,1)S(1)}, bf16[8,1,128,1024]{3,2,0,1:T(8,128)(2,1)}, u32[]{:S(2)}) copy-start(bf16[8,1,128,1024]{3,2,0,1:T(8,128)(2,1)} %get-tuple-element.51) | copy-start | bytes 6291460
  222.7 1.7 copy-start.12
  232.4 16.0 %copy-start.6 = (bf16[1,16,64,128]{3,2,1,0:T(8,128)(2,1)S(1)}, bf16[1,16,64,128]{3,2,1,0:T(8,128)(2,1)}, u32[]{:S(2)}) copy-start(bf16[1,16,64,128]{3,2,1,0:T(8,128)(2,1)} %copy-done.4) | copy-start | bytes 786436
  232.4 149.2 %all-to-all-start.3 = ((bf16[2,32,2,128,1,128]{5,2,3,0,4,1:T(2,128)(2,1)}), bf16[2,32,2,128,1,128]{5,2,3,0,4,1:T(2,128)(2,1)}, u32[]{:S(2)}, u32[]{:S(2)}) async-start(bf16[2,32,2,128,1,128]{5,2,3,0,4,1:T(2,128)(2,1)} %copy.190), calls=%async_computation.3 | async-start | bytes 8388608 | tf_op jit(solution)/shard_map/all_to_all | solution.py:208
  250.9 26.8 %collective-permute-start.15 = (f32[2,256,1,128]{3,1,2,0:T(8,128)}, f32[2,256,1,128]{3,1,2,0:T(8,128)S(1)}, u32[]{:S(2)}, u32[]{:S(2)}) collective-permute-start(f32[2,256,1,128]{3,1,2,0:T(8,128)} %pad_maximum_fusion.7), channel_id=1, source_target_pairs={{2,0},{6,4},{10,8},{14,12},{18,16},{22,20},{26,24},{30,28},{34,32}... | collective-permute-start | bytes 786440 | tf_op jit(solution)/shard_map/ppermute | solution.py:53
  252.2 35.5 %collective-permute-start.16 = (f32[2,256,1,128]{3,1,2,0:T(8,128)}, f32[2,256,1,128]{3,1,2,0:T(8,128)}, u32[]{:S(2)}, u32[]{:S(2)}) collective-permute-start(f32[2,256,1,128]{3,1,2,0:T(8,128)} %pad_maximum_fusion.7), channel_id=1, source_target_pairs={{3,0},{7,4},{11,8},{15,12},{19,16},{23,20},{27,24},{31,28},{35,32}... | collective-permute-start | bytes 786440 | tf_op jit(solution)/shard_map/ppermute | solution.py:53
  253.5 34.2 %collective-permute-start.14 = (f32[2,256,1,128]{3,1,2,0:T(8,128)}, f32[2,256,1,128]{3,1,2,0:T(8,128)}, u32[]{:S(2)}, u32[]{:S(2)}) collective-permute-start(f32[2,256,1,128]{3,1,2,0:T(8,128)} %pad_maximum_fusion.7), channel_id=1, source_target_pairs={{1,0},{5,4},{9,8},{13,12},{17,16},{21,20},{25,24},{29,28},{33,32},... | collective-permute-start | bytes 786440 | tf_op jit(solution)/shard_map/ppermute | solution.py:53
  267.9 6.3 %copy-start.11 = (bf16[1,24,128,1,128]{4,2,0,1,3:T(8,128)(2,1)S(1)}, bf16[1,24,128,1,128]{4,2,0,1,3:T(8,128)(2,1)}, u32[]{:S(2)}) copy-start(bf16[1,24,128,1,128]{4,2,0,1,3:T(8,128)(2,1)} %copy-done.10) | copy-start | bytes 2359300
  268.0 6.7 %copy-start.9 = (bf16[1,24,128,1,128]{4,2,0,1,3:T(8,128)(2,1)S(1)}, bf16[1,24,128,1,128]{4,2,0,1,3:T(8,128)(2,1)}, u32[]{:S(2)}) copy-start(bf16[1,24,128,1,128]{4,2,0,1,3:T(8,128)(2,1)} %copy-done.8) | copy-start | bytes 2359300
  268.0 27.2 %collective-permute-start.12 = (bf16[2,128,1,128]{3,1,0,2:T(8,128)(2,1)S(1)}, bf16[2,128,1,128]{3,1,0,2:T(8,128)(2,1)S(1)}, u32[]{:S(2)}, u32[]{:S(2)}) collective-permute-start(bf16[2,128,1,128]{3,1,0,2:T(8,128)(2,1)S(1)} %get-tuple-element.57), channel_id=1, source_target_pairs={{0,1},{1,2},{2,3},{3,4},{4,5},{5,6},{6,7},{7,8},{8,9},{9,10},{10,1... | collective-permute-start | bytes 196616 | tf_op jit(solution)/shard_map/ppermute | solution.py:19
  274.3 2.0 copy-start.2
  288.8 74.6 %collective-permute-start.23 = (f32[2,256,1,128]{3,1,2,0:T(8,128)S(1)}, f32[2,256,1,128]{3,1,2,0:T(8,128)S(1)}, u32[]{:S(2)}, u32[]{:S(2)}) collective-permute-start(f32[2,256,1,128]{3,1,2,0:T(8,128)S(1)} %add_add_fusion), channel_id=1, source_target_pairs={{28,0},{60,32},{92,64},{124,96},{156,128},{188,160},{220,192},{252... | collective-permute-start | bytes 786440 | tf_op jit(solution)/shard_map/ppermute | solution.py:56
  290.1 74.6 %collective-permute-start.22 = (f32[2,256,1,128]{3,1,2,0:T(8,128)S(1)}, f32[2,256,1,128]{3,1,2,0:T(8,128)S(1)}, u32[]{:S(2)}, u32[]{:S(2)}) collective-permute-start(f32[2,256,1,128]{3,1,2,0:T(8,128)S(1)} %add_add_fusion), channel_id=1, source_target_pairs={{24,0},{56,32},{88,64},{120,96},{152,128},{184,160},{216,192},{248... | collective-permute-start | bytes 786440 | tf_op jit(solution)/shard_map/ppermute | solution.py:56
  292.6 5.4 %collective-permute-start.13 = (bf16[2,128,1,128]{3,1,0,2:T(8,128)(2,1)S(1)}, bf16[2,128,1,128]{3,1,0,2:T(8,128)(2,1)S(1)}, u32[]{:S(2)}, u32[]{:S(2)}) collective-permute-start(bf16[2,128,1,128]{3,1,0,2:T(8,128)(2,1)S(1)} %get-tuple-element.58), channel_id=1, source_target_pairs={{1,0},{2,1},{3,2},{4,3},{5,4},{6,5},{7,6},{8,7},{9,8},{10,9},{11,1... | collective-permute-start | bytes 196616 | tf_op jit(solution)/shard_map/ppermute | solution.py:21
  293.9 76.0 %collective-permute-start.21 = (f32[2,256,1,128]{3,1,2,0:T(8,128)S(1)}, f32[2,256,1,128]{3,1,2,0:T(8,128)S(1)}, u32[]{:S(2)}, u32[]{:S(2)}) collective-permute-start(f32[2,256,1,128]{3,1,2,0:T(8,128)S(1)} %add_add_fusion), channel_id=1, source_target_pairs={{20,0},{52,32},{84,64},{116,96},{148,128},{180,160},{212,192},{244... | collective-permute-start | bytes 786440 | tf_op jit(solution)/shard_map/ppermute | solution.py:56
  295.2 74.7 %collective-permute-start.20 = (f32[2,256,1,128]{3,1,2,0:T(8,128)S(1)}, f32[2,256,1,128]{3,1,2,0:T(8,128)S(1)}, u32[]{:S(2)}, u32[]{:S(2)}) collective-permute-start(f32[2,256,1,128]{3,1,2,0:T(8,128)S(1)} %add_add_fusion), channel_id=1, source_target_pairs={{16,0},{48,32},{80,64},{112,96},{144,128},{176,160},{208,192},{240... | collective-permute-start | bytes 786440 | tf_op jit(solution)/shard_map/ppermute | solution.py:56
  298.0 71.9 %collective-permute-start.19 = (f32[2,256,1,128]{3,1,2,0:T(8,128)S(1)}, f32[2,256,1,128]{3,1,2,0:T(8,128)S(1)}, u32[]{:S(2)}, u32[]{:S(2)}) collective-permute-start(f32[2,256,1,128]{3,1,2,0:T(8,128)S(1)} %add_add_fusion), channel_id=1, source_target_pairs={{12,0},{44,32},{76,64},{108,96},{140,128},{172,160},{204,192},{236... | collective-permute-start | bytes 786440 | tf_op jit(solution)/shard_map/ppermute | solution.py:56
  363.4 9.3 %collective-permute-start.18 = (f32[2,256,1,128]{3,1,2,0:T(8,128)S(1)}, f32[2,256,1,128]{3,1,2,0:T(8,128)}, u32[]{:S(2)}, u32[]{:S(2)}) collective-permute-start(f32[2,256,1,128]{3,1,2,0:T(8,128)S(1)} %add_add_fusion), channel_id=1, source_target_pairs={{8,0},{40,32},{72,64},{104,96},{136,128},{168,160},{200,192},{232,... | collective-permute-start | bytes 786440 | tf_op jit(solution)/shard_map/ppermute | solution.py:56
  364.7 1.3 copy-start.14
  364.8 15.4 %collective-permute-start.17 = (f32[2,256,1,128]{3,1,2,0:T(8,128)S(1)}, f32[2,256,1,128]{3,1,2,0:T(8,128)}, u32[]{:S(2)}, u32[]{:S(2)}) collective-permute-start(f32[2,256,1,128]{3,1,2,0:T(8,128)S(1)} %add_add_fusion), channel_id=1, source_target_pairs={{4,0},{36,32},{68,64},{100,96},{132,128},{164,160},{196,192},{228,... | collective-permute-start | bytes 786440 | tf_op jit(solution)/shard_map/ppermute | solution.py:56
  366.1 14.1 %copy-start.15 = (f32[2,256,1,128]{3,1,2,0:T(8,128)S(1)}, f32[2,256,1,128]{3,1,2,0:T(8,128)}, u32[]{:S(2)}) copy-start(f32[2,256,1,128]{3,1,2,0:T(8,128)} %copy-done.14) | copy-start | bytes 786436
  389.3 1.0 copy-start.13
where the time goes:
time: 431 us; the launch traced here: 429 us
  waiting for transfers between devices  205 us (48%)
  starting transfers between devices  80.8 us (19%)
  local copies, waits for them, and re-layouts  70.7 us (16%)
  blocking collectives  31.3 us (7%)
  matrix products  22 us (5%)
  other arithmetic  17.4 us (4%)
    ppermute x7, waiting for transfers between devices, reduce_to_first(): total = total + lax.ppermute(value, axis, [(row * width, 0)])  74.4 us
    all_to_all x1, waiting for transfers between devices, shards(): lax.all_to_all(served, 'seq', split_axis=1, concat_axis=1, tiled=True)  69.6 us
    all_to_all x1, blocking collectives, shards(): lax.all_to_all(jnp.stack([attended.reshape(group_tokens, head_count * HD)...  31.3 us
    all_to_all x1, waiting for transfers between devices, shards(): lax.all_to_all(jnp.stack([queries, keys, values, grad_out]), 'head', spli...  26.7 us
    ppermute x7, starting transfers between devices, broadcast(): got = got + lax.ppermute(value, axis, [(0, row * width)])  17.8 us
    all_to_all x1, starting transfers between devices, shards(): lax.all_to_all(outgoing.reshape(2, groups, capacity, BLK, head_count, HD)...  15.9 us
    all_to_all x1, starting transfers between devices, shards(): lax.all_to_all(jnp.stack([queries, keys, values, grad_out]), 'head', spli...  10.3 us
    unnamed x46, local copies, waits for them, and re-layouts  9.97 us
  transfers between devices with their start and end apart: 28, of which 12 were waited for; matrix products, arithmetic and copies ran while one was open for 10% of the time, Pallas kernels for 0%

commit v1 on v0

--- a/solution.py
+++ b/solution.py
@@ -157,12 +157,12 @@
         concat_axis=0,
         tiled=True,
     )
-    served = jnp.take(kv_blocks, wanted.reshape(-1), axis=1)
-    served = served.reshape(2, groups, capacity, BLK, head_count, HD)
+    served = jnp.take(jnp.swapaxes(kv_blocks, 0, 1), wanted.reshape(-1), axis=0)
+    served = served.reshape(groups, capacity, 2, BLK, head_count, HD)
     served, global_kv = lax.optimization_barrier((served, global_kv))
-    fetched = lax.all_to_all(served, "seq", split_axis=1, concat_axis=1, tiled=True)
-    chosen = jnp.take(fetched.reshape(2, groups * capacity, BLK, head_count, HD), places, axis=1)
-    remote_kv = chosen.reshape(2, query_count, RAND * BLK, head_count, HD)
+    fetched = lax.all_to_all(served, "seq", split_axis=0, concat_axis=0, tiled=True)
+    chosen = jnp.take(fetched.reshape(groups * capacity, 2, BLK, head_count, HD), places, axis=0)
+    remote_kv = jnp.swapaxes(chosen, 0, 1).reshape(2, query_count, RAND * BLK, head_count, HD)
     query_blocks = head_q.reshape(query_count, BLK, head_count, HD)
     grad_blocks = head_g.reshape(query_count, BLK, head_count, HD)
     scores = score_scale * against_keys(query_blocks, global_kv[0], window_kv[0], remote_kv[0])
@@ -194,31 +194,31 @@
     own_grad = extended[:, 1 : query_count + 1]
     own_grad = own_grad.at[:, 0].add(inward[:, :BLK])
     own_grad = own_grad.at[:, query_count - 1].add(inward[:, 3 * BLK :])
-    random_terms = (
-        jnp.stack([key_random, value_random])
-        .reshape(2, query_count * RAND, BLK, head_count, HD)
-        .astype(jnp.bfloat16)
-    )
+    random_terms = jnp.stack(
+        [key_random.reshape(query_count * RAND, BLK, head_count, HD),
+         value_random.reshape(query_count * RAND, BLK, head_count, HD)],
+        axis=1,
+    ).astype(jnp.bfloat16)
     send_pick = (places[None, :] == jnp.arange(groups * capacity, dtype=jnp.int32)[:, None]).astype(
         jnp.bfloat16
     )
     outgoing = jnp.einsum(
-        "pj,xjihd->xpihd", send_pick, random_terms, preferred_element_type=jnp.float32
+        "pj,jxihd->pxihd", send_pick, random_terms, preferred_element_type=jnp.float32
     ).astype(jnp.bfloat16)
     incoming = lax.all_to_all(
-        outgoing.reshape(2, groups, capacity, BLK, head_count, HD),
+        outgoing.reshape(groups, capacity, 2, BLK, head_count, HD),
         "seq",
-        split_axis=1,
-        concat_axis=1,
+        split_axis=0,
+        concat_axis=0,
         tiled=True,
     )
     take_pick = (
         wanted.reshape(-1)[None, :] == jnp.arange(query_count, dtype=jnp.int32)[:, None]
     ).astype(jnp.bfloat16)
     random_sum = jnp.einsum(
-        "qp,xpihd->xqihd",
+        "qp,pxihd->xqihd",
         take_pick,
-        incoming.reshape(2, groups * capacity, BLK, head_count, HD),
+        incoming.reshape(groups * capacity, 2, BLK, head_count, HD),
         preferred_element_type=jnp.float32,
     )
     global_sum = global_sum.reshape(2, 2, BLK, head_count, HD)

time: 431 us -> 422 us (0.979)
  local copies, waits for them, and re-layouts: 70.7 us -> 60.7 us
    all_to_all x2 -> x1, local copies, waits for them, and re-layouts: 11.8 us -> 6.97 us  [shards(): lax.all_to_all(outgoing.reshape(groups, capacity, 2, BLK, head_count, HD)...]
    gather x3 -> x2, local copies, waits for them, and re-layouts: 9.95 us -> 7.21 us  [the longest x1 4.15 us: shards(): jnp.take(fetched.reshape(groups * capacity, 2, BLK, head_count, HD), plac...]
  transfers between devices with their start and end apart: 28 -> 28, of which waited for: 12 -> 11; matrix products, arithmetic and copies ran while one was open for 10% -> 11% of each run, Pallas kernels for 0% -> 0%
where the time goes in v1:
time: 422 us; the launch traced here: 420 us
  waiting for transfers between devices  203 us (48%)
  starting transfers between devices  80.6 us (19%)
  local copies, waits for them, and re-layouts  60.7 us (14%)
  blocking collectives  31.3 us (7%)
  matrix products  22 us (5%)
  other arithmetic  21.6 us (5%)
    ppermute x7, waiting for transfers between devices, reduce_to_first(): total = total + lax.ppermute(value, axis, [(row * width, 0)])  74.4 us
    all_to_all x1, waiting for transfers between devices, shards(): lax.all_to_all(served, 'seq', split_axis=0, concat_axis=0, tiled=True)  71.3 us
    all_to_all x1, blocking collectives, shards(): lax.all_to_all(jnp.stack([attended.reshape(group_tokens, head_count * HD)...  31.3 us
    all_to_all x1, waiting for transfers between devices, shards(): lax.all_to_all(jnp.stack([queries, keys, values, grad_out]), 'head', spli...  26.7 us
    ppermute x7, starting transfers between devices, broadcast(): got = got + lax.ppermute(value, axis, [(0, row * width)])  17.8 us
    all_to_all x1, starting transfers between devices, shards(): lax.all_to_all(outgoing.reshape(groups, capacity, 2, BLK, head_count, HD)...  16.6 us
    all_to_all x1, starting transfers between devices, shards(): lax.all_to_all(jnp.stack([queries, keys, values, grad_out]), 'head', spli...  10.3 us
    unnamed x46, local copies, waits for them, and re-layouts  9.97 us
  transfers between devices with their start and end apart: 28, of which 11 were waited for; matrix products, arithmetic and copies ran while one was open for 11% of the time, Pallas kernels for 0%

profile of v1, /device:TPU:1, one launch (start us, length us, event | category | flops | bytes accessed | tf_op | source)
XLA Modules:
  0.0 420.4 jit_solution(16069299775341391652)
XLA Ops:
  0.6 1.3 pad_maximum_fusion.3
  2.0 1.4 copy.114
  3.4 2.3 reshape.1020
  5.6 10.3 %all-to-all-start = ((bf16[16,2,16384]{2,1,0:T(2,128)(2,1)}), bf16[16,2,16384]{2,1,0:T(2,128)(2,1)S(1)}, u32[]{:S(2)}, u32[]{:S(2)}) async-start(bf16[16,2,16384]{2,1,0:T(2,128)(2,1)} %reshape.1020), calls=%async_computation | async-start | bytes 2097152 | tf_op jit(solution)/shard_map/all_to_all | solution.py:130
  17.3 26.7 %all-to-all-done = bf16[16,2,16384]{2,1,0:T(2,128)(2,1)S(1)} async-done(((bf16[16,2,16384]{2,1,0:T(2,128)(2,1)}), bf16[16,2,16384]{2,1,0:T(2,128)(2,1)S(1)}, u32[]{:S(2)}, u32[]{:S(2)}) %all-to-all-start) | async-done | bytes 1048608 | tf_op jit(solution)/shard_map/all_to_all | solution.py:130
  43.9 1.3 reshape.1021
  45.3 2.3 copy.115
  48.9 8.9 %collective-permute-start.6 = (bf16[2,256,1,128]{3,1,2,0:T(8,128)(2,1)S(1)}, bf16[2,256,1,128]{3,1,2,0:T(8,128)(2,1)S(1)}, u32[]{:S(2)}, u32[]{:S(2)}) collective-permute-start(bf16[2,256,1,128]{3,1,2,0:T(8,128)(2,1)S(1)} %bitcast.317), channel_id=1, source_target_pairs={{0,28},{32,60},{64,92},{96,124},{128,156},{160,188},{192,220},{224... | collective-permute-start | bytes 393224 | tf_op jit(solution)/shard_map/ppermute | solution.py:38
  57.8 1.3 collective-permute-start.5
  59.1 1.3 collective-permute-start.4
  60.4 1.3 collective-permute-start.3
  61.7 1.3 collective-permute-start.2
  63.0 3.8 all-to-all-start.1
  66.9 8.4 %all-to-all-done.1 = s32[32,1,2]{2,1,0:T(1,128)S(1)} async-done(((s32[32,1,2]{2,1,0:T(1,128)}), s32[32,1,2]{2,1,0:T(1,128)S(1)}, u32[]{:S(2)}, u32[]{:S(2)}) %all-to-all-start.1) | async-done | bytes 288 | tf_op jit(solution)/shard_map/all_to_all | solution.py:153
  76.8 2.3 collective-permute-start.1
  79.2 1.3 collective-permute-start
  80.6 3.1 gather_fusion
  84.7 1.3 collective-permute-start.9
  86.0 1.3 collective-permute-start.8
  87.3 1.3 collective-permute-start.7
  88.6 4.7 %broadcast_select_fusion = bf16[32,2,2,128,1,128]{5,3,2,1,4,0:T(8,128)(2,1)} fusion(bf16[32,2,2,128,1,128]{5,3,2,1,4,0:T(8,128)(2,1)} %bitcast.273, pred[32,2]{1,0:T(8,128)(4,1)S(1)} %copy.119), kind=kLoop, calls=%fused_computation.8 | loop fusion | flops 2097152 | bytes 8388672 | tf_op jit(solution)/shard_map/jit(_take)/select_n | solution.py:160
  93.3 4.9 %all-to-all-start.2 = ((bf16[32,2,2,128,1,128]{5,3,2,1,4,0:T(8,128)(2,1)}), bf16[32,2,2,128,1,128]{5,3,2,1,4,0:T(8,128)(2,1)}, u32[]{:S(2)}, u32[]{:S(2)}) async-start(bf16[32,2,2,128,1,128]{5,3,2,1,4,0:T(8,128)(2,1)} %broadcast_select_fusion), calls=%async_computation.2 | async-start | bytes 8388608 | tf_op jit(solution)/shard_map/all_to_all | solution.py:163
  98.5 3.0 collective-permute-start.10
  101.6 1.3 collective-permute-start.11
  102.9 5.1 %collective-permute-done.10 = bf16[2,128,128]{2,1,0:T(8,128)(2,1)S(1)} collective-permute-done((bf16[2,128,128]{2,1,0:T(8,128)(2,1)S(1)}, bf16[2,128,128]{2,1,0:T(8,128)(2,1)S(1)}, u32[]{:S(2)}, u32[]{:S(2)}) %collective-permute-start.10) | collective-permute-done | bytes 65568 | tf_op jit(solution)/shard_map/ppermute | solution.py:19
  108.0 4.4 %collective-permute-done.11 = bf16[2,128,128]{2,1,0:T(8,128)(2,1)S(1)} collective-permute-done((bf16[2,128,128]{2,1,0:T(8,128)(2,1)S(1)}, bf16[2,128,128]{2,1,0:T(8,128)(2,1)S(1)}, u32[]{:S(2)}, u32[]{:S(2)}) %collective-permute-start.11) | collective-permute-done | bytes 65568 | tf_op jit(solution)/shard_map/ppermute | solution.py:21
  113.4 1.6 convolution_bitcast_fusion.3
  115.0 1.3 convolution_bitcast_fusion.8
  116.4 1.6 copy.122
  117.9 1.3 convolution_bitcast_fusion.7
  119.2 71.3 %all-to-all-done.2 = bf16[32,2,2,128,1,128]{5,3,2,1,4,0:T(8,128)(2,1)} async-done(((bf16[32,2,2,128,1,128]{5,3,2,1,4,0:T(8,128)(2,1)}), bf16[32,2,2,128,1,128]{5,3,2,1,4,0:T(8,128)(2,1)}, u32[]{:S(2)}, u32[]{:S(2)}) %all-to-all-start.2) | async-done | bytes 4194336 | tf_op jit(solution)/shard_map/all_to_all | solution.py:163
  190.5 4.2 gather_fusion.1
  194.7 1.6 fusion.6
  198.4 1.4 fusion.2
  201.5 1.7 multiply_reduce_fusion
  203.2 3.0 multiply_convert_fusion
  206.2 1.7 fusion.9
  209.1 2.6 copy.142
  213.3 1.7 copy.143
  215.0 1.4 convolution_convert_fusion
  216.3 6.7 %copy.144 = bf16[32,2,2,128,1,128]{5,1,3,2,4,0:T(2,128)(2,1)} copy(bf16[32,2,2,128,1,128]{5,1,0,3,2,4:T(2,128)(2,1)S(1)} %bitcast.271) | data formatting | bytes 8388608 | tf_op jit(solution)/shard_map/reshape | solution.py:209
  223.0 16.6 %all-to-all-start.3 = ((bf16[32,2,2,128,1,128]{5,1,3,2,4,0:T(2,128)(2,1)}), bf16[32,2,2,128,1,128]{5,1,3,2,4,0:T(2,128)(2,1)}, u32[]{:S(2)}, u32[]{:S(2)}) async-start(bf16[32,2,2,128,1,128]{5,1,3,2,4,0:T(2,128)(2,1)} %copy.144), calls=%async_computation.3 | async-start | bytes 8388608 | tf_op jit(solution)/shard_map/all_to_all | solution.py:208
  239.8 1.4 convolution_bitcast_fusion.16
  244.8 1.5 collective-permute-start.14
  246.3 2.7 convolution_bitcast_fusion.1
  249.0 3.1 copy.125
  252.1 1.6 convolution_bitcast_fusion
  253.6 3.0 copy.127
  256.7 2.0 fusion.18
  259.3 4.6 %collective-permute-start.12 = (bf16[2,128,1,128]{3,1,0,2:T(8,128)(2,1)S(1)}, bf16[2,128,1,128]{3,1,0,2:T(8,128)(2,1)S(1)}, u32[]{:S(2)}, u32[]{:S(2)}) collective-permute-start(bf16[2,128,1,128]{3,1,0,2:T(8,128)(2,1)S(1)} %get-tuple-element.57), channel_id=1, source_target_pairs={{0,1},{1,2},{2,3},{3,4},{4,5},{5,6},{6,7},{7,8},{8,9},{9,10},{10,1... | collective-permute-start | bytes 196616 | tf_op jit(solution)/shard_map/ppermute | solution.py:19
  263.9 1.3 convolution_bitcast_fusion.13
  266.0 1.6 convolution_bitcast_fusion.9
  267.5 1.5 fusion.15
  269.1 10.0 %collective-permute-done.16 = f32[2,256,1,128]{3,1,2,0:T(8,128)} collective-permute-done((f32[2,256,1,128]{3,1,2,0:T(8,128)}, f32[2,256,1,128]{3,1,2,0:T(8,128)}, u32[]{:S(2)}, u32[]{:S(2)}) %collective-permute-start.16) | collective-permute-done | bytes 262176 | tf_op jit(solution)/shard_map/ppermute | solution.py:53
  280.1 1.3 collective-permute-start.23
  281.4 1.3 collective-permute-start.22
  287.8 1.5 collective-permute-done.13
  290.6 64.1 %collective-permute-done.23 = f32[2,256,1,128]{3,1,2,0:T(8,128)S(1)} collective-permute-done((f32[2,256,1,128]{3,1,2,0:T(8,128)S(1)}, f32[2,256,1,128]{3,1,2,0:T(8,128)S(1)}, u32[]{:S(2)}, u32[]{:S(2)}) %collective-permute-start.23) | collective-permute-done | bytes 262176 | tf_op jit(solution)/shard_map/ppermute | solution.py:56
  358.2 3.0 scatter-add.11
  361.2 2.9 collective-permute-done.18
  364.1 7.4 %collective-permute-done.17 = f32[2,256,1,128]{3,1,2,0:T(8,128)} collective-permute-done((f32[2,256,1,128]{3,1,2,0:T(8,128)S(1)}, f32[2,256,1,128]{3,1,2,0:T(8,128)}, u32[]{:S(2)}, u32[]{:S(2)}) %collective-permute-start.17) | collective-permute-done | bytes 262176 | tf_op jit(solution)/shard_map/ppermute | solution.py:56
  373.0 7.0 %copy.145 = bf16[32,2,2,128,1,128]{5,1,0,3,2,4:T(2,128)(2,1)S(1)} copy(bf16[32,2,2,128,1,128]{5,1,3,2,4,0:T(2,128)(2,1)} %all-to-all-done.3) | data formatting | bytes 8388608 | tf_op jit(solution)/shard_map/all_to_all | solution.py:208
  382.5 31.3 %all_to_all.49 = bf16[4,1024,128]{2,0,1:T(4,128)(2,1)S(1)} all-to-all(bf16[4,1024,128]{2,0,1:T(4,128)(2,1)S(1)} %copy.148), channel_id=1, replica_groups=mesh['head'=16,'seq'=32] {'head'}, dimensions={1} | all-to-all | bytes 2097152 | tf_op jit(solution)/shard_map/all_to_all | solution.py:229
  413.8 2.2 fusion.50
  (138 shorter events, 37.2 us)
Async XLA Ops:
  3.4 12.6 %copy-start.16 = (s32[8,3]{0,1:T(4,128)S(1)}, s32[8,3]{0,1:T(4,128)}, u32[]{:S(2)}) copy-start(s32[8,3]{0,1:T(4,128)} %param.15) | copy-start | bytes 292
  5.6 38.3 %all-to-all-start = ((bf16[16,2,16384]{2,1,0:T(2,128)(2,1)}), bf16[16,2,16384]{2,1,0:T(2,128)(2,1)S(1)}, u32[]{:S(2)}, u32[]{:S(2)}) async-start(bf16[16,2,16384]{2,1,0:T(2,128)(2,1)} %reshape.1020), calls=%async_computation | async-start | bytes 2097152 | tf_op jit(solution)/shard_map/all_to_all | solution.py:130
  48.8 147.6 %copy-start.4 = (bf16[1,16,64,128]{3,2,1,0:T(8,128)(2,1)}, bf16[1,16,64,128]{3,2,1,0:T(8,128)(2,1)S(1)}, u32[]{:S(2)}) copy-start(bf16[1,16,64,128]{3,2,1,0:T(8,128)(2,1)S(1)} %get-tuple-element.67) | copy-start | bytes 786436
  48.9 27.9 %collective-permute-start.6 = (bf16[2,256,1,128]{3,1,2,0:T(8,128)(2,1)S(1)}, bf16[2,256,1,128]{3,1,2,0:T(8,128)(2,1)S(1)}, u32[]{:S(2)}, u32[]{:S(2)}) collective-permute-start(bf16[2,256,1,128]{3,1,2,0:T(8,128)(2,1)S(1)} %bitcast.317), channel_id=1, source_target_pairs={{0,28},{32,60},{64,92},{96,124},{128,156},{160,188},{192,220},{224... | collective-permute-start | bytes 393224 | tf_op jit(solution)/shard_map/ppermute | solution.py:38
  57.8 21.3 %collective-permute-start.5 = (bf16[2,256,1,128]{3,1,2,0:T(8,128)(2,1)S(1)}, bf16[2,256,1,128]{3,1,2,0:T(8,128)(2,1)S(1)}, u32[]{:S(2)}, u32[]{:S(2)}) collective-permute-start(bf16[2,256,1,128]{3,1,2,0:T(8,128)(2,1)S(1)} %bitcast.318), channel_id=1, source_target_pairs={{0,24},{32,56},{64,88},{96,120},{128,152},{160,184},{192,216},{224... | collective-permute-start | bytes 393224 | tf_op jit(solution)/shard_map/ppermute | solution.py:38
  59.1 24.5 %collective-permute-start.4 = (bf16[2,256,1,128]{3,1,2,0:T(8,128)(2,1)S(1)}, bf16[2,256,1,128]{3,1,2,0:T(8,128)(2,1)S(1)}, u32[]{:S(2)}, u32[]{:S(2)}) collective-permute-start(bf16[2,256,1,128]{3,1,2,0:T(8,128)(2,1)S(1)} %bitcast.319), channel_id=1, source_target_pairs={{0,20},{32,52},{64,84},{96,116},{128,148},{160,180},{192,212},{224... | collective-permute-start | bytes 393224 | tf_op jit(solution)/shard_map/ppermute | solution.py:38
  60.4 23.2 %collective-permute-start.3 = (bf16[2,256,1,128]{3,1,2,0:T(8,128)(2,1)S(1)}, bf16[2,256,1,128]{3,1,2,0:T(8,128)(2,1)S(1)}, u32[]{:S(2)}, u32[]{:S(2)}) collective-permute-start(bf16[2,256,1,128]{3,1,2,0:T(8,128)(2,1)S(1)} %bitcast.320), channel_id=1, source_target_pairs={{0,16},{32,48},{64,80},{96,112},{128,144},{160,176},{192,208},{224... | collective-permute-start | bytes 393224 | tf_op jit(solution)/shard_map/ppermute | solution.py:38
  61.7 21.9 %collective-permute-start.2 = (bf16[2,256,1,128]{3,1,2,0:T(8,128)(2,1)S(1)}, bf16[2,256,1,128]{3,1,2,0:T(8,128)(2,1)S(1)}, u32[]{:S(2)}, u32[]{:S(2)}) collective-permute-start(bf16[2,256,1,128]{3,1,2,0:T(8,128)(2,1)S(1)} %bitcast.321), channel_id=1, source_target_pairs={{0,12},{32,44},{64,76},{96,108},{128,140},{160,172},{192,204},{224... | collective-permute-start | bytes 393224 | tf_op jit(solution)/shard_map/ppermute | solution.py:38
  63.0 12.3 %all-to-all-start.1 = ((s32[32,1,2]{2,1,0:T(1,128)}), s32[32,1,2]{2,1,0:T(1,128)S(1)}, u32[]{:S(2)}, u32[]{:S(2)}) async-start(s32[32,1,2]{2,1,0:T(1,128)} %bitcast.111), calls=%async_computation.1 | async-start | bytes 32768 | tf_op jit(solution)/shard_map/all_to_all | solution.py:153
  76.8 6.9 %collective-permute-start.1 = (bf16[2,256,1,128]{3,1,2,0:T(8,128)(2,1)S(1)}, bf16[2,256,1,128]{3,1,2,0:T(8,128)(2,1)S(1)}, u32[]{:S(2)}, u32[]{:S(2)}) collective-permute-start(bf16[2,256,1,128]{3,1,2,0:T(8,128)(2,1)S(1)} %bitcast.322), channel_id=1, source_target_pairs={{0,8},{32,40},{64,72},{96,104},{128,136},{160,168},{192,200},{224,... | collective-permute-start | bytes 393224 | tf_op jit(solution)/shard_map/ppermute | solution.py:38
  79.2 5.5 %collective-permute-start = (bf16[2,256,1,128]{3,1,2,0:T(8,128)(2,1)S(1)}, bf16[2,256,1,128]{3,1,2,0:T(8,128)(2,1)S(1)}, u32[]{:S(2)}, u32[]{:S(2)}) collective-permute-start(bf16[2,256,1,128]{3,1,2,0:T(8,128)(2,1)S(1)} %bitcast.323), channel_id=1, source_target_pairs={{0,4},{32,36},{64,68},{96,100},{128,132},{160,164},{192,196},{224,... | collective-permute-start | bytes 393224 | tf_op jit(solution)/shard_map/ppermute | solution.py:38
  84.7 8.6 %collective-permute-start.9 = (bf16[2,256,1,128]{3,1,2,0:T(8,128)(2,1)S(1)}, bf16[2,256,1,128]{3,1,2,0:T(8,128)(2,1)S(1)}, u32[]{:S(2)}, u32[]{:S(2)}) collective-permute-start(bf16[2,256,1,128]{3,1,2,0:T(8,128)(2,1)S(1)} %add_select_fusion.2), channel_id=1, source_target_pairs={{0,3},{4,7},{8,11},{12,15},{16,19},{20,23},{24,27},{28,31},{32,35}... | collective-permute-start | bytes 393224 | tf_op jit(solution)/shard_map/ppermute | solution.py:43
  86.0 7.3 %collective-permute-start.8 = (bf16[2,256,1,128]{3,1,2,0:T(8,128)(2,1)S(1)}, bf16[2,256,1,128]{3,1,2,0:T(8,128)(2,1)S(1)}, u32[]{:S(2)}, u32[]{:S(2)}) collective-permute-start(bf16[2,256,1,128]{3,1,2,0:T(8,128)(2,1)S(1)} %add_select_fusion.2), channel_id=1, source_target_pairs={{0,2},{4,6},{8,10},{12,14},{16,18},{20,22},{24,26},{28,30},{32,34}... | collective-permute-start | bytes 393224 | tf_op jit(solution)/shard_map/ppermute | solution.py:43
  87.3 6.0 %collective-permute-start.7 = (bf16[2,256,1,128]{3,1,2,0:T(8,128)(2,1)S(1)}, bf16[2,256,1,128]{3,1,2,0:T(8,128)(2,1)S(1)}, u32[]{:S(2)}, u32[]{:S(2)}) collective-permute-start(bf16[2,256,1,128]{3,1,2,0:T(8,128)(2,1)S(1)} %add_select_fusion.2), channel_id=1, source_target_pairs={{0,1},{4,5},{8,9},{12,13},{16,17},{20,21},{24,25},{28,29},{32,33},... | collective-permute-start | bytes 393224 | tf_op jit(solution)/shard_map/ppermute | solution.py:43
  93.3 97.2 %all-to-all-start.2 = ((bf16[32,2,2,128,1,128]{5,3,2,1,4,0:T(8,128)(2,1)}), bf16[32,2,2,128,1,128]{5,3,2,1,4,0:T(8,128)(2,1)}, u32[]{:S(2)}, u32[]{:S(2)}) async-start(bf16[32,2,2,128,1,128]{5,3,2,1,4,0:T(8,128)(2,1)} %broadcast_select_fusion), calls=%async_computation.2 | async-start | bytes 8388608 | tf_op jit(solution)/shard_map/all_to_all | solution.py:163
  98.5 9.4 %collective-permute-start.10 = (bf16[2,128,128]{2,1,0:T(8,128)(2,1)S(1)}, bf16[2,128,128]{2,1,0:T(8,128)(2,1)S(1)}, u32[]{:S(2)}, u32[]{:S(2)}) collective-permute-start(bf16[2,128,128]{2,1,0:T(8,128)(2,1)S(1)} %get-tuple-element.74), channel_id=1, source_target_pairs={{0,1},{1,2},{2,3},{3,4},{4,5},{5,6},{6,7},{7,8},{8,9},{9,10},{10,1... | collective-permute-start | bytes 196616 | tf_op jit(solution)/shard_map/ppermute | solution.py:19
  101.6 10.8 %collective-permute-start.11 = (bf16[2,128,128]{2,1,0:T(8,128)(2,1)S(1)}, bf16[2,128,128]{2,1,0:T(8,128)(2,1)S(1)}, u32[]{:S(2)}, u32[]{:S(2)}) collective-permute-start(bf16[2,128,128]{2,1,0:T(8,128)(2,1)S(1)} %get-tuple-element.75), channel_id=1, source_target_pairs={{1,0},{2,1},{3,2},{4,3},{5,4},{6,5},{7,6},{8,7},{9,8},{10,9},{11,1... | collective-permute-start | bytes 196616 | tf_op jit(solution)/shard_map/ppermute | solution.py:21
  112.9 2.1 copy-start.1
  196.4 0.9 copy-start.8
  196.5 3.3 copy-start.10
  199.8 1.4 copy-start.3
  199.8 1.7 copy-start.7
  203.1 3.1 copy-start.5
  206.2 5.5 %copy-start = (bf16[8,1,128,1024]{3,2,0,1:T(8,128)(2,1)S(1)}, bf16[8,1,128,1024]{3,2,0,1:T(8,128)(2,1)}, u32[]{:S(2)}) copy-start(bf16[8,1,128,1024]{3,2,0,1:T(8,128)(2,1)} %get-tuple-element.51) | copy-start | bytes 6291460
  213.3 1.7 copy-start.12
  223.0 16.7 %copy-start.6 = (bf16[1,16,64,128]{3,2,1,0:T(8,128)(2,1)S(1)}, bf16[1,16,64,128]{3,2,1,0:T(8,128)(2,1)}, u32[]{:S(2)}) copy-start(bf16[1,16,64,128]{3,2,1,0:T(8,128)(2,1)} %copy-done.4) | copy-start | bytes 786436
  223.0 149.9 %all-to-all-start.3 = ((bf16[32,2,2,128,1,128]{5,1,3,2,4,0:T(2,128)(2,1)}), bf16[32,2,2,128,1,128]{5,1,3,2,4,0:T(2,128)(2,1)}, u32[]{:S(2)}, u32[]{:S(2)}) async-start(bf16[32,2,2,128,1,128]{5,1,3,2,4,0:T(2,128)(2,1)} %copy.144), calls=%async_computation.3 | async-start | bytes 8388608 | tf_op jit(solution)/shard_map/all_to_all | solution.py:208
  242.2 26.8 %collective-permute-start.15 = (f32[2,256,1,128]{3,1,2,0:T(8,128)}, f32[2,256,1,128]{3,1,2,0:T(8,128)S(1)}, u32[]{:S(2)}, u32[]{:S(2)}) collective-permute-start(f32[2,256,1,128]{3,1,2,0:T(8,128)} %pad_maximum_fusion.7), channel_id=1, source_target_pairs={{2,0},{6,4},{10,8},{14,12},{18,16},{22,20},{26,24},{30,28},{34,32}... | collective-permute-start | bytes 786440 | tf_op jit(solution)/shard_map/ppermute | solution.py:53
  243.5 35.5 %collective-permute-start.16 = (f32[2,256,1,128]{3,1,2,0:T(8,128)}, f32[2,256,1,128]{3,1,2,0:T(8,128)}, u32[]{:S(2)}, u32[]{:S(2)}) collective-permute-start(f32[2,256,1,128]{3,1,2,0:T(8,128)} %pad_maximum_fusion.7), channel_id=1, source_target_pairs={{3,0},{7,4},{11,8},{15,12},{19,16},{23,20},{27,24},{31,28},{35,32}... | collective-permute-start | bytes 786440 | tf_op jit(solution)/shard_map/ppermute | solution.py:53
  244.8 34.2 %collective-permute-start.14 = (f32[2,256,1,128]{3,1,2,0:T(8,128)}, f32[2,256,1,128]{3,1,2,0:T(8,128)}, u32[]{:S(2)}, u32[]{:S(2)}) collective-permute-start(f32[2,256,1,128]{3,1,2,0:T(8,128)} %pad_maximum_fusion.7), channel_id=1, source_target_pairs={{1,0},{5,4},{9,8},{13,12},{17,16},{21,20},{25,24},{29,28},{33,32},... | collective-permute-start | bytes 786440 | tf_op jit(solution)/shard_map/ppermute | solution.py:53
  259.2 6.3 %copy-start.11 = (bf16[1,24,128,1,128]{4,2,0,1,3:T(8,128)(2,1)S(1)}, bf16[1,24,128,1,128]{4,2,0,1,3:T(8,128)(2,1)}, u32[]{:S(2)}) copy-start(bf16[1,24,128,1,128]{4,2,0,1,3:T(8,128)(2,1)} %copy-done.10) | copy-start | bytes 2359300
  259.3 6.7 %copy-start.9 = (bf16[1,24,128,1,128]{4,2,0,1,3:T(8,128)(2,1)S(1)}, bf16[1,24,128,1,128]{4,2,0,1,3:T(8,128)(2,1)}, u32[]{:S(2)}) copy-start(bf16[1,24,128,1,128]{4,2,0,1,3:T(8,128)(2,1)} %copy-done.8) | copy-start | bytes 2359300
  259.3 27.2 %collective-permute-start.12 = (bf16[2,128,1,128]{3,1,0,2:T(8,128)(2,1)S(1)}, bf16[2,128,1,128]{3,1,0,2:T(8,128)(2,1)S(1)}, u32[]{:S(2)}, u32[]{:S(2)}) collective-permute-start(bf16[2,128,1,128]{3,1,0,2:T(8,128)(2,1)S(1)} %get-tuple-element.57), channel_id=1, source_target_pairs={{0,1},{1,2},{2,3},{3,4},{4,5},{5,6},{6,7},{7,8},{8,9},{9,10},{10,1... | collective-permute-start | bytes 196616 | tf_op jit(solution)/shard_map/ppermute | solution.py:19
  265.6 2.0 copy-start.2
  280.1 74.6 %collective-permute-start.23 = (f32[2,256,1,128]{3,1,2,0:T(8,128)S(1)}, f32[2,256,1,128]{3,1,2,0:T(8,128)S(1)}, u32[]{:S(2)}, u32[]{:S(2)}) collective-permute-start(f32[2,256,1,128]{3,1,2,0:T(8,128)S(1)} %add_add_fusion), channel_id=1, source_target_pairs={{28,0},{60,32},{92,64},{124,96},{156,128},{188,160},{220,192},{252... | collective-permute-start | bytes 786440 | tf_op jit(solution)/shard_map/ppermute | solution.py:56
  281.4 74.6 %collective-permute-start.22 = (f32[2,256,1,128]{3,1,2,0:T(8,128)S(1)}, f32[2,256,1,128]{3,1,2,0:T(8,128)S(1)}, u32[]{:S(2)}, u32[]{:S(2)}) collective-permute-start(f32[2,256,1,128]{3,1,2,0:T(8,128)S(1)} %add_add_fusion), channel_id=1, source_target_pairs={{24,0},{56,32},{88,64},{120,96},{152,128},{184,160},{216,192},{248... | collective-permute-start | bytes 786440 | tf_op jit(solution)/shard_map/ppermute | solution.py:56
  283.9 5.4 %collective-permute-start.13 = (bf16[2,128,1,128]{3,1,0,2:T(8,128)(2,1)S(1)}, bf16[2,128,1,128]{3,1,0,2:T(8,128)(2,1)S(1)}, u32[]{:S(2)}, u32[]{:S(2)}) collective-permute-start(bf16[2,128,1,128]{3,1,0,2:T(8,128)(2,1)S(1)} %get-tuple-element.58), channel_id=1, source_target_pairs={{1,0},{2,1},{3,2},{4,3},{5,4},{6,5},{7,6},{8,7},{9,8},{10,9},{11,1... | collective-permute-start | bytes 196616 | tf_op jit(solution)/shard_map/ppermute | solution.py:21
  285.2 76.0 %collective-permute-start.21 = (f32[2,256,1,128]{3,1,2,0:T(8,128)S(1)}, f32[2,256,1,128]{3,1,2,0:T(8,128)S(1)}, u32[]{:S(2)}, u32[]{:S(2)}) collective-permute-start(f32[2,256,1,128]{3,1,2,0:T(8,128)S(1)} %add_add_fusion), channel_id=1, source_target_pairs={{20,0},{52,32},{84,64},{116,96},{148,128},{180,160},{212,192},{244... | collective-permute-start | bytes 786440 | tf_op jit(solution)/shard_map/ppermute | solution.py:56
  286.5 74.7 %collective-permute-start.20 = (f32[2,256,1,128]{3,1,2,0:T(8,128)S(1)}, f32[2,256,1,128]{3,1,2,0:T(8,128)S(1)}, u32[]{:S(2)}, u32[]{:S(2)}) collective-permute-start(f32[2,256,1,128]{3,1,2,0:T(8,128)S(1)} %add_add_fusion), channel_id=1, source_target_pairs={{16,0},{48,32},{80,64},{112,96},{144,128},{176,160},{208,192},{240... | collective-permute-start | bytes 786440 | tf_op jit(solution)/shard_map/ppermute | solution.py:56
  289.3 71.9 %collective-permute-start.19 = (f32[2,256,1,128]{3,1,2,0:T(8,128)S(1)}, f32[2,256,1,128]{3,1,2,0:T(8,128)S(1)}, u32[]{:S(2)}, u32[]{:S(2)}) collective-permute-start(f32[2,256,1,128]{3,1,2,0:T(8,128)S(1)} %add_add_fusion), channel_id=1, source_target_pairs={{12,0},{44,32},{76,64},{108,96},{140,128},{172,160},{204,192},{236... | collective-permute-start | bytes 786440 | tf_op jit(solution)/shard_map/ppermute | solution.py:56
  354.7 9.3 %collective-permute-start.18 = (f32[2,256,1,128]{3,1,2,0:T(8,128)S(1)}, f32[2,256,1,128]{3,1,2,0:T(8,128)}, u32[]{:S(2)}, u32[]{:S(2)}) collective-permute-start(f32[2,256,1,128]{3,1,2,0:T(8,128)S(1)} %add_add_fusion), channel_id=1, source_target_pairs={{8,0},{40,32},{72,64},{104,96},{136,128},{168,160},{200,192},{232,... | collective-permute-start | bytes 786440 | tf_op jit(solution)/shard_map/ppermute | solution.py:56
  356.0 1.3 copy-start.14
  356.0 15.4 %collective-permute-start.17 = (f32[2,256,1,128]{3,1,2,0:T(8,128)S(1)}, f32[2,256,1,128]{3,1,2,0:T(8,128)}, u32[]{:S(2)}, u32[]{:S(2)}) collective-permute-start(f32[2,256,1,128]{3,1,2,0:T(8,128)S(1)} %add_add_fusion), channel_id=1, source_target_pairs={{4,0},{36,32},{68,64},{100,96},{132,128},{164,160},{196,192},{228,... | collective-permute-start | bytes 786440 | tf_op jit(solution)/shard_map/ppermute | solution.py:56
  357.4 14.1 %copy-start.15 = (f32[2,256,1,128]{3,1,2,0:T(8,128)S(1)}, f32[2,256,1,128]{3,1,2,0:T(8,128)}, u32[]{:S(2)}) copy-start(f32[2,256,1,128]{3,1,2,0:T(8,128)} %copy-done.14) | copy-start | bytes 786436
  380.6 1.0 copy-start.13

commit v2 on v1

--- a/solution.py
+++ b/solution.py
@@ -94,9 +94,9 @@
 def against_keys(rows, global_part, window_part, remote_part):
     return jnp.concatenate(
         [
-            jnp.einsum("qihd,jhd->qhij", rows, global_part, preferred_element_type=jnp.float32),
-            jnp.einsum("qihd,qjhd->qhij", rows, window_part, preferred_element_type=jnp.float32),
-            jnp.einsum("qihd,qjhd->qhij", rows, remote_part, preferred_element_type=jnp.float32),
+            jnp.einsum("hqid,hjd->hqij", rows, global_part, preferred_element_type=jnp.float32),
+            jnp.einsum("hqid,hqjd->hqij", rows, window_part, preferred_element_type=jnp.float32),
+            jnp.einsum("hqid,hqjd->hqij", rows, remote_part, preferred_element_type=jnp.float32),
         ],
         axis=-1,
     )
@@ -109,19 +109,29 @@
 def weigh_keys(table, global_part, window_part, remote_part):
     global_w, window_w, random_w = split_keys(table)
     return (
-        jnp.einsum("qhij,jhd->qihd", global_w, global_part, preferred_element_type=jnp.float32)
-        + jnp.einsum("qhij,qjhd->qihd", window_w, window_part, preferred_element_type=jnp.float32)
-        + jnp.einsum("qhij,qjhd->qihd", random_w, remote_part, preferred_element_type=jnp.float32)
+        jnp.einsum("hqij,hjd->hqid", global_w, global_part, preferred_element_type=jnp.float32)
+        + jnp.einsum("hqij,hqjd->hqid", window_w, window_part, preferred_element_type=jnp.float32)
+        + jnp.einsum("hqij,hqjd->hqid", random_w, remote_part, preferred_element_type=jnp.float32)
     )
 
 
 def key_terms(table, rows):
     global_w, window_w, random_w = split_keys(table)
     return (
-        jnp.einsum("qhij,qihd->jhd", global_w, rows, preferred_element_type=jnp.float32),
-        jnp.einsum("qhij,qihd->qjhd", window_w, rows, preferred_element_type=jnp.float32),
-        jnp.einsum("qhij,qihd->qjhd", random_w, rows, preferred_element_type=jnp.float32),
-    )
+        jnp.einsum("hqij,hqid->hjd", global_w, rows, preferred_element_type=jnp.float32),
+        jnp.einsum("hqij,hqid->hqjd", window_w, rows, preferred_element_type=jnp.float32),
+        jnp.einsum("hqij,hqid->hqjd", random_w, rows, preferred_element_type=jnp.float32),
+    )
+
+
+def by_head(table, head_count):
+    tokens = table.shape[0]
+    return jnp.transpose(table.reshape(tokens, head_count, HD), (1, 0, 2))
+
+
+def by_token(table):
+    head_count, tokens = table.shape[0], table.shape[1]
+    return jnp.transpose(table, (1, 0, 2)).reshape(tokens, head_count * HD)
 
 
 def shards(queries, keys, values, grad_out, random_blocks):
@@ -138,36 +148,31 @@
     ordered_table, head_k = lax.optimization_barrier(
         (request_table(random_blocks, query_count, groups, capacity), head_k)
     )
-    key_value = jnp.stack([head_k, head_v])
-    kv_blocks = key_value.reshape(2, query_count, BLK, head_count, HD)
-    edged = with_halo(key_value, (("seq", 1),), BLK)
-    edged = edged.reshape(2, query_count + 2, BLK, head_count, HD)
+    key_value = jnp.stack([by_head(head_k, head_count), by_head(head_v, head_count)])
+    kv_blocks = key_value.reshape(2, head_count, query_count, BLK, HD)
+    edged = with_halo(key_value, (("seq", 2),), BLK)
+    edged = edged.reshape(2, head_count, query_count + 2, BLK, HD)
     window_kv = jnp.concatenate(
-        [edged[:, 0:query_count], edged[:, 1 : query_count + 1], edged[:, 2 : query_count + 2]],
-        axis=2,
-    )
-    global_kv = broadcast(kv_blocks[:, 0:2].reshape(2, 2 * BLK, head_count, HD), "seq")
+        [edged[:, :, 0:query_count], edged[:, :, 1 : query_count + 1], edged[:, :, 2 : query_count + 2]],
+        axis=3,
+    )
+    global_kv = broadcast(kv_blocks[:, :, 0:2].reshape(2, head_count, 2 * BLK, HD), "seq")
     flat_ids = random_blocks.reshape(-1)
     places = slot_places(flat_ids // query_count, groups, capacity)
-    table = ordered_table
-    wanted = lax.all_to_all(
-        table,
-        "seq",
-        split_axis=0,
-        concat_axis=0,
-        tiled=True,
-    )
-    served = jnp.take(jnp.swapaxes(kv_blocks, 0, 1), wanted.reshape(-1), axis=0)
-    served = served.reshape(groups, capacity, 2, BLK, head_count, HD)
+    wanted = lax.all_to_all(ordered_table, "seq", split_axis=0, concat_axis=0, tiled=True)
+    served = jnp.take(jnp.transpose(kv_blocks, (2, 0, 1, 3, 4)), wanted.reshape(-1), axis=0)
+    served = served.reshape(groups, capacity, 2, head_count, BLK, HD)
     served, global_kv = lax.optimization_barrier((served, global_kv))
     fetched = lax.all_to_all(served, "seq", split_axis=0, concat_axis=0, tiled=True)
-    chosen = jnp.take(fetched.reshape(groups * capacity, 2, BLK, head_count, HD), places, axis=0)
-    remote_kv = jnp.swapaxes(chosen, 0, 1).reshape(2, query_count, RAND * BLK, head_count, HD)
-    query_blocks = head_q.reshape(query_count, BLK, head_count, HD)
-    grad_blocks = head_g.reshape(query_count, BLK, head_count, HD)
+    chosen = jnp.take(fetched.reshape(groups * capacity, 2, head_count, BLK, HD), places, axis=0)
+    remote_kv = jnp.transpose(
+        chosen.reshape(query_count, RAND, 2, head_count, BLK, HD), (2, 3, 0, 1, 4, 5)
+    ).reshape(2, head_count, query_count, RAND * BLK, HD)
+    query_blocks = by_head(head_q, head_count).reshape(head_count, query_count, BLK, HD)
+    grad_blocks = by_head(head_g, head_count).reshape(head_count, query_count, BLK, HD)
     scores = score_scale * against_keys(query_blocks, global_kv[0], window_kv[0], remote_kv[0])
     valid = window_valid(my_group, query_count, groups)
-    scores = jnp.where(valid[:, None, None, :], scores, -jnp.inf)
+    scores = jnp.where(valid[None, :, None, :], scores, -jnp.inf)
     row_max = jnp.max(scores, axis=-1, keepdims=True)
     exponent = jnp.exp(scores - row_max)
     attention_probs = exponent / jnp.sum(exponent, axis=-1, keepdims=True)
@@ -181,32 +186,31 @@
     value_global, value_window, value_random = key_terms(weights, grad_blocks)
     global_sum = reduce_to_first(jnp.stack([key_global, value_global]), "seq")
     window_grad = jnp.stack([key_window, value_window]).reshape(
-        2, query_count, 3, BLK, head_count, HD
+        2, head_count, query_count, 3, BLK, HD
     )
     no_pad = (0, 0)
     extended = (
-        jnp.pad(window_grad[:, :, 0], (no_pad, (0, 2), no_pad, no_pad, no_pad))
-        + jnp.pad(window_grad[:, :, 1], (no_pad, (1, 1), no_pad, no_pad, no_pad))
-        + jnp.pad(window_grad[:, :, 2], (no_pad, (2, 0), no_pad, no_pad, no_pad))
-    )
-    outward = jnp.concatenate([extended[:, 0], extended[:, query_count + 1]], axis=1)
-    inward = with_halo(outward.astype(jnp.bfloat16), (("seq", 1),), BLK).astype(outward.dtype)
-    own_grad = extended[:, 1 : query_count + 1]
-    own_grad = own_grad.at[:, 0].add(inward[:, :BLK])
-    own_grad = own_grad.at[:, query_count - 1].add(inward[:, 3 * BLK :])
-    random_terms = jnp.stack(
-        [key_random.reshape(query_count * RAND, BLK, head_count, HD),
-         value_random.reshape(query_count * RAND, BLK, head_count, HD)],
-        axis=1,
+        jnp.pad(window_grad[:, :, :, 0], (no_pad, no_pad, (0, 2), no_pad, no_pad))
+        + jnp.pad(window_grad[:, :, :, 1], (no_pad, no_pad, (1, 1), no_pad, no_pad))
+        + jnp.pad(window_grad[:, :, :, 2], (no_pad, no_pad, (2, 0), no_pad, no_pad))
+    )
+    outward = jnp.concatenate([extended[:, :, 0], extended[:, :, query_count + 1]], axis=2)
+    inward = with_halo(outward.astype(jnp.bfloat16), (("seq", 2),), BLK).astype(outward.dtype)
+    own_grad = extended[:, :, 1 : query_count + 1]
+    own_grad = own_grad.at[:, :, 0].add(inward[:, :, :BLK])
+    own_grad = own_grad.at[:, :, query_count - 1].add(inward[:, :, 3 * BLK :])
+    random_terms = jnp.transpose(
+        jnp.stack([key_random, value_random]).reshape(2, head_count, query_count * RAND, BLK, HD),
+        (2, 0, 1, 3, 4),
     ).astype(jnp.bfloat16)
     send_pick = (places[None, :] == jnp.arange(groups * capacity, dtype=jnp.int32)[:, None]).astype(
         jnp.bfloat16
     )
     outgoing = jnp.einsum(
-        "pj,jxihd->pxihd", send_pick, random_terms, preferred_element_type=jnp.float32
+        "pj,jxhid->pxhid", send_pick, random_terms, preferred_element_type=jnp.float32
     ).astype(jnp.bfloat16)
     incoming = lax.all_to_all(
-        outgoing.reshape(groups, capacity, 2, BLK, head_count, HD),
+        outgoing.reshape(groups, capacity, 2, head_count, BLK, HD),
         "seq",
         split_axis=0,
         concat_axis=0,
@@ -216,19 +220,18 @@
         wanted.reshape(-1)[None, :] == jnp.arange(query_count, dtype=jnp.int32)[:, None]
     ).astype(jnp.bfloat16)
     random_sum = jnp.einsum(
-        "qp,pxihd->xqihd",
+        "qp,pxhid->xhqid",
         take_pick,
-        incoming.reshape(groups * capacity, 2, BLK, head_count, HD),
+        incoming.reshape(groups * capacity, 2, head_count, BLK, HD),
         preferred_element_type=jnp.float32,
     )
-    global_sum = global_sum.reshape(2, 2, BLK, head_count, HD)
-    own_grad = own_grad.at[:, 0:2].add(jnp.where(my_group == 0, global_sum, 0.0))
-    total_grad = own_grad + random_sum
-    grad_k = total_grad[0].reshape(group_tokens, head_count * HD).astype(jnp.bfloat16)
-    grad_v = total_grad[1].reshape(group_tokens, head_count * HD).astype(jnp.bfloat16)
+    global_sum = global_sum.reshape(2, head_count, 2, BLK, HD)
+    own_grad = own_grad.at[:, :, 0:2].add(jnp.where(my_group == 0, global_sum, 0.0))
+    total_grad = (own_grad + random_sum).astype(jnp.bfloat16)
+    flat = (head_count, group_tokens, HD)
     results = lax.all_to_all(
-        jnp.stack([attended.reshape(group_tokens, head_count * HD),
-                   grad_q.reshape(group_tokens, head_count * HD), grad_k, grad_v]),
+        jnp.stack([by_token(attended.reshape(flat)), by_token(grad_q.reshape(flat)),
+                   by_token(total_grad[0].reshape(flat)), by_token(total_grad[1].reshape(flat))]),
         "head",
         split_axis=1,
         concat_axis=2,

time: 422 us -> 410 us (0.972)
  waiting for transfers between devices: 203 us -> 221 us
  local copies, waits for them, and re-layouts: 60.7 us -> 48.9 us
  matrix products: 22 us -> 12.3 us
  other arithmetic: 21.6 us -> 16.7 us
    ppermute x3, waiting for transfers between devices: 9.96 us -> 25.3 us  [reduce_to_first(): total = total + lax.ppermute(value, axis, pairs)]
    transpose x5 -> x0, local copies, waits for them, and re-layouts: 9.97 us -> none  [the longest x2 6.08 us: key_terms(): jnp.einsum('qhij,qihd->qjhd', window_w, rows, preferred_element_type=jnp....]
    dot_general x20, matrix products: 22 us -> 12.3 us  [the longest x2 2.11 us: against_keys(): jnp.einsum('hqid,hqjd->hqij', rows, window_part, preferred_element_type=j...]
    unnamed x46 -> x38, local copies, waits for them, and re-layouts: 9.97 us -> 11.4 us
  transfers between devices with their start and end apart: 28 -> 28, of which waited for: 11 -> 11; matrix products, arithmetic and copies ran while one was open for 11% -> 6% of each run, Pallas kernels for 0% -> 0%
where the time goes in v2:
time: 410 us; the launch traced here: 409 us
  waiting for transfers between devices  221 us (54%)
  starting transfers between devices  77.6 us (19%)
  local copies, waits for them, and re-layouts  48.9 us (12%)
  blocking collectives  31.3 us (8%)
  other arithmetic  16.7 us (4%)
  matrix products  12.3 us (3%)
    ppermute x7, waiting for transfers between devices, reduce_to_first(): total = total + lax.ppermute(value, axis, [(row * width, 0)])  76.3 us
    all_to_all x1, waiting for transfers between devices, shards(): lax.all_to_all(served, 'seq', split_axis=0, concat_axis=0, tiled=True)  73.5 us
    all_to_all x1, blocking collectives, shards(): lax.all_to_all(jnp.stack([by_token(attended.reshape(flat)), by_token(grad...  31.3 us
    all_to_all x1, waiting for transfers between devices, shards(): lax.all_to_all(jnp.stack([queries, keys, values, grad_out]), 'head', spli...  26.7 us
    ppermute x3, waiting for transfers between devices, reduce_to_first(): total = total + lax.ppermute(value, axis, pairs)  25.3 us
    ppermute x7, starting transfers between devices, broadcast(): got = got + lax.ppermute(value, axis, [(0, row * width)])  17.8 us
    all_to_all x1, starting transfers between devices, shards(): lax.all_to_all(outgoing.reshape(groups, capacity, 2, head_count, BLK, HD)...  14.2 us
    unnamed x38, local copies, waits for them, and re-layouts  11.4 us
  transfers between devices with their start and end apart: 28, of which 11 were waited for; matrix products, arithmetic and copies ran while one was open for 6% of the time, Pallas kernels for 0%

profile of v2, /device:TPU:1, one launch (start us, length us, event | category | flops | bytes accessed | tf_op | source)
XLA Modules:
  0.0 409.1 jit_solution(8591512427415898953)
XLA Ops:
  0.6 1.3 pad_maximum_fusion.3
  2.0 1.4 copy.106
  3.4 2.3 reshape.1010
  5.6 10.3 %all-to-all-start = ((bf16[16,2,16384]{2,1,0:T(2,128)(2,1)}), bf16[16,2,16384]{2,1,0:T(2,128)(2,1)S(1)}, u32[]{:S(2)}, u32[]{:S(2)}) async-start(bf16[16,2,16384]{2,1,0:T(2,128)(2,1)} %reshape.1010), calls=%async_computation | async-start | bytes 2097152 | tf_op jit(solution)/shard_map/all_to_all | solution.py:140
  17.3 26.7 %all-to-all-done = bf16[16,2,16384]{2,1,0:T(2,128)(2,1)S(1)} async-done(((bf16[16,2,16384]{2,1,0:T(2,128)(2,1)}), bf16[16,2,16384]{2,1,0:T(2,128)(2,1)S(1)}, u32[]{:S(2)}, u32[]{:S(2)}) %all-to-all-start) | async-done | bytes 1048608 | tf_op jit(solution)/shard_map/all_to_all | solution.py:140
  43.9 1.3 reshape.1011
  45.3 2.3 copy.107
  47.6 1.3 fusion.48
  48.9 8.9 %collective-permute-start.6 = (bf16[2,1,256,128]{3,2,1,0:T(8,128)(2,1)S(1)}, bf16[2,1,256,128]{3,2,1,0:T(8,128)(2,1)S(1)}, u32[]{:S(2)}, u32[]{:S(2)}) collective-permute-start(bf16[2,1,256,128]{3,2,1,0:T(8,128)(2,1)S(1)} %bitcast.254), channel_id=1, source_target_pairs={{0,28},{32,60},{64,92},{96,124},{128,156},{160,188},{192,220},{224... | collective-permute-start | bytes 393224 | tf_op jit(solution)/shard_map/ppermute | solution.py:38
  57.8 1.3 collective-permute-start.5
  59.1 1.3 collective-permute-start.4
  60.4 1.3 collective-permute-start.3
  61.7 1.3 collective-permute-start.2
  63.0 3.8 all-to-all-start.1
  66.9 8.4 %all-to-all-done.1 = s32[32,1,2]{2,1,0:T(1,128)S(1)} async-done(((s32[32,1,2]{2,1,0:T(1,128)}), s32[32,1,2]{2,1,0:T(1,128)S(1)}, u32[]{:S(2)}, u32[]{:S(2)}) %all-to-all-start.1) | async-done | bytes 288 | tf_op jit(solution)/shard_map/all_to_all | solution.py:162
  76.8 2.3 collective-permute-start.1
  79.2 1.3 collective-permute-start
  80.6 3.0 gather_fusion
  83.7 1.0 collective-permute-done
  84.7 1.3 collective-permute-start.9
  86.0 1.3 collective-permute-start.8
  87.3 1.3 collective-permute-start.7
  88.6 4.6 %broadcast_select_fusion = bf16[32,2,2,1,128,128]{5,4,2,1,3,0:T(8,128)(2,1)} fusion(bf16[32,2,2,1,128,128]{5,4,2,1,3,0:T(8,128)(2,1)} %bitcast.210, pred[32,2]{1,0:T(8,128)(4,1)S(1)} %copy.112), kind=kLoop, calls=%fused_computation.8 | loop fusion | flops 2097152 | bytes 8388672 | tf_op jit(solution)/shard_map/jit(_take)/select_n | solution.py:163
  93.3 4.9 %all-to-all-start.2 = ((bf16[32,2,2,1,128,128]{5,4,2,1,3,0:T(8,128)(2,1)}), bf16[32,2,2,1,128,128]{5,4,2,1,3,0:T(8,128)(2,1)}, u32[]{:S(2)}, u32[]{:S(2)}) async-start(bf16[32,2,2,1,128,128]{5,4,2,1,3,0:T(8,128)(2,1)} %broadcast_select_fusion), calls=%async_computation.2 | async-start | bytes 8388608 | tf_op jit(solution)/shard_map/all_to_all | solution.py:166
  98.6 3.0 collective-permute-start.10
  101.7 1.5 collective-permute-start.11
  103.1 4.8 %collective-permute-done.10 = bf16[2,1,128,128]{3,2,0,1:T(8,128)(2,1)S(1)} collective-permute-done((bf16[2,1,128,128]{3,2,0,1:T(8,128)(2,1)S(1)}, bf16[2,1,128,128]{3,2,0,1:T(8,128)(2,1)S(1)}, u32[]{:S(2)}, u32[]{:S(2)}) %collective-permute-start.10) | collective-permute-done | bytes 65568 | tf_op jit(solution)/shard_map/ppermute | solution.py:19
  107.9 4.7 %collective-permute-done.11 = bf16[2,1,128,128]{3,2,0,1:T(8,128)(2,1)S(1)} collective-permute-done((bf16[2,1,128,128]{3,2,0,1:T(8,128)(2,1)S(1)}, bf16[2,1,128,128]{3,2,0,1:T(8,128)(2,1)S(1)}, u32[]{:S(2)}, u32[]{:S(2)}) %collective-permute-start.11) | collective-permute-done | bytes 65568 | tf_op jit(solution)/shard_map/ppermute | solution.py:21
  113.7 1.6 convolution_bitcast_fusion.1
  115.6 1.3 convolution_bitcast_fusion.5
  116.9 73.5 %all-to-all-done.2 = bf16[32,2,2,1,128,128]{5,4,2,1,3,0:T(8,128)(2,1)} async-done(((bf16[32,2,2,1,128,128]{5,4,2,1,3,0:T(8,128)(2,1)}), bf16[32,2,2,1,128,128]{5,4,2,1,3,0:T(8,128)(2,1)}, u32[]{:S(2)}, u32[]{:S(2)}) %all-to-all-start.2) | async-done | bytes 4194336 | tf_op jit(solution)/shard_map/all_to_all | solution.py:166
  190.4 4.1 %gather_fusion.1 = bf16[24,2,128,128]{3,2,1,0:T(8,128)(2,1)} fusion(bf16[64,2,128,128]{3,2,1,0:T(8,128)(2,1)} %bitcast.26, s32[1024]{0:T(1024)S(1)} %pad_clamp_fusion), kind=kCustom, calls=%fused_computation.1 | custom fusion | bytes 3145824 | tf_op jit(solution)/shard_map/jit(_take)/gather | solution.py:167
  194.6 1.6 fusion.5
  198.2 1.2 fusion.2
  200.0 0.9 copy-done.6
  201.2 1.7 multiply_reduce_fusion
  202.9 1.8 multiply_convert_fusion
  207.2 1.4 convolution_convert_fusion
  208.5 6.7 %copy.133 = bf16[32,2,2,1,128,128]{5,1,4,2,3,0:T(2,128)(2,1)} copy(bf16[32,2,2,1,128,128]{5,1,0,4,2,3:T(2,128)(2,1)S(1)} %bitcast.208) | data formatting | bytes 8388608 | tf_op jit(solution)/shard_map/reshape | solution.py:213
  215.2 14.2 %all-to-all-start.3 = ((bf16[32,2,2,1,128,128]{5,1,4,2,3,0:T(2,128)(2,1)}), bf16[32,2,2,1,128,128]{5,1,4,2,3,0:T(2,128)(2,1)}, u32[]{:S(2)}, u32[]{:S(2)}) async-start(bf16[32,2,2,1,128,128]{5,1,4,2,3,0:T(2,128)(2,1)} %copy.133), calls=%async_computation.3 | async-start | bytes 8388608 | tf_op jit(solution)/shard_map/all_to_all | solution.py:212
  229.6 1.5 convolution_bitcast_fusion.8
  231.5 1.3 collective-permute-start.15
  232.8 1.3 collective-permute-start.16
  234.1 1.3 collective-permute-start.14
  239.0 0.9 copy-done.11
  240.3 8.4 %collective-permute-done.15 = f32[2,1,256,128]{3,2,1,0:T(8,128)S(1)} collective-permute-done((f32[2,1,256,128]{3,2,1,0:T(8,128)S(1)}, f32[2,1,256,128]{3,2,1,0:T(8,128)S(1)}, u32[]{:S(2)}, u32[]{:S(2)}) %collective-permute-start.15) | collective-permute-done | bytes 262176 | tf_op jit(solution)/shard_map/ppermute | solution.py:53
  248.7 17.0 %collective-permute-done.16 = f32[2,1,256,128]{3,2,1,0:T(8,128)S(1)} collective-permute-done((f32[2,1,256,128]{3,2,1,0:T(8,128)S(1)}, f32[2,1,256,128]{3,2,1,0:T(8,128)S(1)}, u32[]{:S(2)}, u32[]{:S(2)}) %collective-permute-start.16) | collective-permute-done | bytes 262176 | tf_op jit(solution)/shard_map/ppermute | solution.py:53
  265.7 1.3 collective-permute-start.23
  267.0 1.3 collective-permute-start.22
  268.8 1.3 collective-permute-start.13
  270.1 4.0 collective-permute-start.12
  274.3 1.3 collective-permute-start.21
  275.6 1.3 collective-permute-start.20
  276.9 1.3 collective-permute-start.19
  278.2 66.1 %collective-permute-done.23 = f32[2,1,256,128]{3,2,1,0:T(8,128)S(1)} collective-permute-done((f32[2,1,256,128]{3,2,1,0:T(8,128)S(1)}, f32[2,1,256,128]{3,2,1,0:T(8,128)S(1)}, u32[]{:S(2)}, u32[]{:S(2)}) %collective-permute-start.23) | collective-permute-done | bytes 262176 | tf_op jit(solution)/shard_map/ppermute | solution.py:56
  344.3 1.3 collective-permute-start.18
  345.6 1.3 collective-permute-start.17
  347.8 3.0 scatter-add.11
  350.8 2.8 collective-permute-done.18
  353.6 7.4 %collective-permute-done.17 = f32[2,1,256,128]{3,2,1,0:T(8,128)} collective-permute-done((f32[2,1,256,128]{3,2,1,0:T(8,128)S(1)}, f32[2,1,256,128]{3,2,1,0:T(8,128)}, u32[]{:S(2)}, u32[]{:S(2)}) %collective-permute-start.17) | collective-permute-done | bytes 262176 | tf_op jit(solution)/shard_map/ppermute | solution.py:56
  361.0 1.1 add_select_fusion
  362.5 7.0 %copy.134 = bf16[32,2,2,1,128,128]{5,1,0,4,2,3:T(2,128)(2,1)S(1)} copy(bf16[32,2,2,1,128,128]{5,1,4,2,3,0:T(2,128)(2,1)} %all-to-all-done.3) | data formatting | bytes 8388608 | tf_op jit(solution)/shard_map/all_to_all | solution.py:212
  371.2 31.3 %all_to_all.49 = bf16[4,1024,128]{2,0,1:T(4,128)(2,1)S(1)} all-to-all(bf16[4,1024,128]{2,0,1:T(4,128)(2,1)S(1)} %copy.137), channel_id=1, replica_groups=mesh['head'=16,'seq'=32] {'head'}, dimensions={1} | all-to-all | bytes 2097152 | tf_op jit(solution)/shard_map/all_to_all | solution.py:232
  402.5 2.2 fusion.47
  (127 shorter events, 22.4 us)
Async XLA Ops:
  3.4 12.6 %copy-start.12 = (s32[8,3]{0,1:T(4,128)S(1)}, s32[8,3]{0,1:T(4,128)}, u32[]{:S(2)}) copy-start(s32[8,3]{0,1:T(4,128)} %param.15) | copy-start | bytes 292
  5.6 38.3 %all-to-all-start = ((bf16[16,2,16384]{2,1,0:T(2,128)(2,1)}), bf16[16,2,16384]{2,1,0:T(2,128)(2,1)S(1)}, u32[]{:S(2)}, u32[]{:S(2)}) async-start(bf16[16,2,16384]{2,1,0:T(2,128)(2,1)} %reshape.1010), calls=%async_computation | async-start | bytes 2097152 | tf_op jit(solution)/shard_map/all_to_all | solution.py:140
  48.9 27.9 %collective-permute-start.6 = (bf16[2,1,256,128]{3,2,1,0:T(8,128)(2,1)S(1)}, bf16[2,1,256,128]{3,2,1,0:T(8,128)(2,1)S(1)}, u32[]{:S(2)}, u32[]{:S(2)}) collective-permute-start(bf16[2,1,256,128]{3,2,1,0:T(8,128)(2,1)S(1)} %bitcast.254), channel_id=1, source_target_pairs={{0,28},{32,60},{64,92},{96,124},{128,156},{160,188},{192,220},{224... | collective-permute-start | bytes 393224 | tf_op jit(solution)/shard_map/ppermute | solution.py:38
  57.8 21.3 %collective-permute-start.5 = (bf16[2,1,256,128]{3,2,1,0:T(8,128)(2,1)S(1)}, bf16[2,1,256,128]{3,2,1,0:T(8,128)(2,1)S(1)}, u32[]{:S(2)}, u32[]{:S(2)}) collective-permute-start(bf16[2,1,256,128]{3,2,1,0:T(8,128)(2,1)S(1)} %bitcast.255), channel_id=1, source_target_pairs={{0,24},{32,56},{64,88},{96,120},{128,152},{160,184},{192,216},{224... | collective-permute-start | bytes 393224 | tf_op jit(solution)/shard_map/ppermute | solution.py:38
  59.1 24.5 %collective-permute-start.4 = (bf16[2,1,256,128]{3,2,1,0:T(8,128)(2,1)S(1)}, bf16[2,1,256,128]{3,2,1,0:T(8,128)(2,1)S(1)}, u32[]{:S(2)}, u32[]{:S(2)}) collective-permute-start(bf16[2,1,256,128]{3,2,1,0:T(8,128)(2,1)S(1)} %bitcast.256), channel_id=1, source_target_pairs={{0,20},{32,52},{64,84},{96,116},{128,148},{160,180},{192,212},{224... | collective-permute-start | bytes 393224 | tf_op jit(solution)/shard_map/ppermute | solution.py:38
  60.4 23.2 %collective-permute-start.3 = (bf16[2,1,256,128]{3,2,1,0:T(8,128)(2,1)S(1)}, bf16[2,1,256,128]{3,2,1,0:T(8,128)(2,1)S(1)}, u32[]{:S(2)}, u32[]{:S(2)}) collective-permute-start(bf16[2,1,256,128]{3,2,1,0:T(8,128)(2,1)S(1)} %bitcast.257), channel_id=1, source_target_pairs={{0,16},{32,48},{64,80},{96,112},{128,144},{160,176},{192,208},{224... | collective-permute-start | bytes 393224 | tf_op jit(solution)/shard_map/ppermute | solution.py:38
  61.7 21.9 %collective-permute-start.2 = (bf16[2,1,256,128]{3,2,1,0:T(8,128)(2,1)S(1)}, bf16[2,1,256,128]{3,2,1,0:T(8,128)(2,1)S(1)}, u32[]{:S(2)}, u32[]{:S(2)}) collective-permute-start(bf16[2,1,256,128]{3,2,1,0:T(8,128)(2,1)S(1)} %bitcast.258), channel_id=1, source_target_pairs={{0,12},{32,44},{64,76},{96,108},{128,140},{160,172},{192,204},{224... | collective-permute-start | bytes 393224 | tf_op jit(solution)/shard_map/ppermute | solution.py:38
  63.0 12.3 %all-to-all-start.1 = ((s32[32,1,2]{2,1,0:T(1,128)}), s32[32,1,2]{2,1,0:T(1,128)S(1)}, u32[]{:S(2)}, u32[]{:S(2)}) async-start(s32[32,1,2]{2,1,0:T(1,128)} %bitcast.86), calls=%async_computation.1 | async-start | bytes 32768 | tf_op jit(solution)/shard_map/all_to_all | solution.py:162
  76.8 6.9 %collective-permute-start.1 = (bf16[2,1,256,128]{3,2,1,0:T(8,128)(2,1)S(1)}, bf16[2,1,256,128]{3,2,1,0:T(8,128)(2,1)S(1)}, u32[]{:S(2)}, u32[]{:S(2)}) collective-permute-start(bf16[2,1,256,128]{3,2,1,0:T(8,128)(2,1)S(1)} %bitcast.259), channel_id=1, source_target_pairs={{0,8},{32,40},{64,72},{96,104},{128,136},{160,168},{192,200},{224,... | collective-permute-start | bytes 393224 | tf_op jit(solution)/shard_map/ppermute | solution.py:38
  79.2 5.5 %collective-permute-start = (bf16[2,1,256,128]{3,2,1,0:T(8,128)(2,1)S(1)}, bf16[2,1,256,128]{3,2,1,0:T(8,128)(2,1)S(1)}, u32[]{:S(2)}, u32[]{:S(2)}) collective-permute-start(bf16[2,1,256,128]{3,2,1,0:T(8,128)(2,1)S(1)} %bitcast.260), channel_id=1, source_target_pairs={{0,4},{32,36},{64,68},{96,100},{128,132},{160,164},{192,196},{224,... | collective-permute-start | bytes 393224 | tf_op jit(solution)/shard_map/ppermute | solution.py:38
  84.7 8.6 %collective-permute-start.9 = (bf16[2,1,256,128]{3,2,1,0:T(8,128)(2,1)S(1)}, bf16[2,1,256,128]{3,2,1,0:T(8,128)(2,1)S(1)}, u32[]{:S(2)}, u32[]{:S(2)}) collective-permute-start(bf16[2,1,256,128]{3,2,1,0:T(8,128)(2,1)S(1)} %add_select_fusion.2), channel_id=1, source_target_pairs={{0,3},{4,7},{8,11},{12,15},{16,19},{20,23},{24,27},{28,31},{32,35}... | collective-permute-start | bytes 393224 | tf_op jit(solution)/shard_map/ppermute | solution.py:43
  86.0 7.3 %collective-permute-start.8 = (bf16[2,1,256,128]{3,2,1,0:T(8,128)(2,1)S(1)}, bf16[2,1,256,128]{3,2,1,0:T(8,128)(2,1)S(1)}, u32[]{:S(2)}, u32[]{:S(2)}) collective-permute-start(bf16[2,1,256,128]{3,2,1,0:T(8,128)(2,1)S(1)} %add_select_fusion.2), channel_id=1, source_target_pairs={{0,2},{4,6},{8,10},{12,14},{16,18},{20,22},{24,26},{28,30},{32,34}... | collective-permute-start | bytes 393224 | tf_op jit(solution)/shard_map/ppermute | solution.py:43
  87.3 6.0 %collective-permute-start.7 = (bf16[2,1,256,128]{3,2,1,0:T(8,128)(2,1)S(1)}, bf16[2,1,256,128]{3,2,1,0:T(8,128)(2,1)S(1)}, u32[]{:S(2)}, u32[]{:S(2)}) collective-permute-start(bf16[2,1,256,128]{3,2,1,0:T(8,128)(2,1)S(1)} %add_select_fusion.2), channel_id=1, source_target_pairs={{0,1},{4,5},{8,9},{12,13},{16,17},{20,21},{24,25},{28,29},{32,33},... | collective-permute-start | bytes 393224 | tf_op jit(solution)/shard_map/ppermute | solution.py:43
  93.3 97.1 %all-to-all-start.2 = ((bf16[32,2,2,1,128,128]{5,4,2,1,3,0:T(8,128)(2,1)}), bf16[32,2,2,1,128,128]{5,4,2,1,3,0:T(8,128)(2,1)}, u32[]{:S(2)}, u32[]{:S(2)}) async-start(bf16[32,2,2,1,128,128]{5,4,2,1,3,0:T(8,128)(2,1)} %broadcast_select_fusion), calls=%async_computation.2 | async-start | bytes 8388608 | tf_op jit(solution)/shard_map/all_to_all | solution.py:166
  98.6 9.3 %collective-permute-start.10 = (bf16[2,1,128,128]{3,2,0,1:T(8,128)(2,1)S(1)}, bf16[2,1,128,128]{3,2,0,1:T(8,128)(2,1)S(1)}, u32[]{:S(2)}, u32[]{:S(2)}) collective-permute-start(bf16[2,1,128,128]{3,2,0,1:T(8,128)(2,1)S(1)} %get-tuple-element.70), channel_id=1, source_target_pairs={{0,1},{1,2},{2,3},{3,4},{4,5},{5,6},{6,7},{7,8},{8,9},{9,10},{10,1... | collective-permute-start | bytes 196616 | tf_op jit(solution)/shard_map/ppermute | solution.py:19
  101.7 11.0 %collective-permute-start.11 = (bf16[2,1,128,128]{3,2,0,1:T(8,128)(2,1)S(1)}, bf16[2,1,128,128]{3,2,0,1:T(8,128)(2,1)S(1)}, u32[]{:S(2)}, u32[]{:S(2)}) collective-permute-start(bf16[2,1,128,128]{3,2,0,1:T(8,128)(2,1)S(1)} %get-tuple-element.71), channel_id=1, source_target_pairs={{1,0},{2,1},{3,2},{4,3},{5,4},{6,5},{7,6},{8,7},{9,8},{10,9},{11,1... | collective-permute-start | bytes 196616 | tf_op jit(solution)/shard_map/ppermute | solution.py:21
  113.2 2.1 copy-start.4
  196.3 0.9 copy-start.10
  196.3 3.1 copy-start.8
  199.5 1.4 copy-start.6
  199.5 1.7 copy-start.7
  204.6 1.4 copy-start
  204.6 2.0 copy-start.2
  215.2 15.9 %copy-start.1 = (bf16[1,8,128,1024]{3,2,1,0:T(8,128)(2,1)S(1)}, bf16[1,8,128,1024]{3,2,1,0:T(8,128)(2,1)}, u32[]{:S(2)}) copy-start(bf16[1,8,128,1024]{3,2,1,0:T(8,128)(2,1)} %copy-done) | copy-start | bytes 6291460
  215.2 147.3 %all-to-all-start.3 = ((bf16[32,2,2,1,128,128]{5,1,4,2,3,0:T(2,128)(2,1)}), bf16[32,2,2,1,128,128]{5,1,4,2,3,0:T(2,128)(2,1)}, u32[]{:S(2)}, u32[]{:S(2)}) async-start(bf16[32,2,2,1,128,128]{5,1,4,2,3,0:T(2,128)(2,1)} %copy.133), calls=%async_computation.3 | async-start | bytes 8388608 | tf_op jit(solution)/shard_map/all_to_all | solution.py:212
  229.6 5.8 %copy-start.3 = (bf16[1,8,128,1024]{3,2,1,0:T(8,128)(2,1)S(1)}, bf16[1,8,128,1024]{3,2,1,0:T(8,128)(2,1)}, u32[]{:S(2)}) copy-start(bf16[1,8,128,1024]{3,2,1,0:T(8,128)(2,1)} %copy-done.2) | copy-start | bytes 6291460
  231.5 17.2 %collective-permute-start.15 = (f32[2,1,256,128]{3,2,1,0:T(8,128)S(1)}, f32[2,1,256,128]{3,2,1,0:T(8,128)S(1)}, u32[]{:S(2)}, u32[]{:S(2)}) collective-permute-start(f32[2,1,256,128]{3,2,1,0:T(8,128)S(1)} %pad_maximum_fusion.7), channel_id=1, source_target_pairs={{2,0},{6,4},{10,8},{14,12},{18,16},{22,20},{26,24},{30,28},{34,32}... | collective-permute-start | bytes 786440 | tf_op jit(solution)/shard_map/ppermute | solution.py:53
  232.8 32.8 %collective-permute-start.16 = (f32[2,1,256,128]{3,2,1,0:T(8,128)S(1)}, f32[2,1,256,128]{3,2,1,0:T(8,128)S(1)}, u32[]{:S(2)}, u32[]{:S(2)}) collective-permute-start(f32[2,1,256,128]{3,2,1,0:T(8,128)S(1)} %pad_maximum_fusion.7), channel_id=1, source_target_pairs={{3,0},{7,4},{11,8},{15,12},{19,16},{23,20},{27,24},{31,28},{35,32}... | collective-permute-start | bytes 786440 | tf_op jit(solution)/shard_map/ppermute | solution.py:53
  234.1 31.5 %collective-permute-start.14 = (f32[2,1,256,128]{3,2,1,0:T(8,128)S(1)}, f32[2,1,256,128]{3,2,1,0:T(8,128)S(1)}, u32[]{:S(2)}, u32[]{:S(2)}) collective-permute-start(f32[2,1,256,128]{3,2,1,0:T(8,128)S(1)} %pad_maximum_fusion.7), channel_id=1, source_target_pairs={{1,0},{5,4},{9,8},{13,12},{17,16},{21,20},{25,24},{29,28},{33,32},... | collective-permute-start | bytes 786440 | tf_op jit(solution)/shard_map/ppermute | solution.py:53
  236.6 1.4 copy-start.5
  238.8 1.1 copy-start.11
  239.9 28.4 %copy-start.9 = (bf16[1,1,8,3,128,128]{5,4,3,2,1,0:T(8,128)(2,1)S(1)}, bf16[1,1,8,3,128,128]{5,4,3,2,1,0:T(8,128)(2,1)}, u32[]{:S(2)}) copy-start(bf16[1,1,8,3,128,128]{5,4,3,2,1,0:T(8,128)(2,1)} %copy-done.8) | copy-start | bytes 2359300
  265.7 78.6 %collective-permute-start.23 = (f32[2,1,256,128]{3,2,1,0:T(8,128)S(1)}, f32[2,1,256,128]{3,2,1,0:T(8,128)S(1)}, u32[]{:S(2)}, u32[]{:S(2)}) collective-permute-start(f32[2,1,256,128]{3,2,1,0:T(8,128)S(1)} %add_add_fusion), channel_id=1, source_target_pairs={{28,0},{60,32},{92,64},{124,96},{156,128},{188,160},{220,192},{252... | collective-permute-start | bytes 786440 | tf_op jit(solution)/shard_map/ppermute | solution.py:56
  267.0 78.6 %collective-permute-start.22 = (f32[2,1,256,128]{3,2,1,0:T(8,128)S(1)}, f32[2,1,256,128]{3,2,1,0:T(8,128)S(1)}, u32[]{:S(2)}, u32[]{:S(2)}) collective-permute-start(f32[2,1,256,128]{3,2,1,0:T(8,128)S(1)} %add_add_fusion), channel_id=1, source_target_pairs={{24,0},{56,32},{88,64},{120,96},{152,128},{184,160},{216,192},{248... | collective-permute-start | bytes 786440 | tf_op jit(solution)/shard_map/ppermute | solution.py:56
  268.8 6.8 %collective-permute-start.13 = (bf16[2,1,128,128]{3,2,0,1:T(8,128)(2,1)S(1)}, bf16[2,1,128,128]{3,2,0,1:T(8,128)(2,1)S(1)}, u32[]{:S(2)}, u32[]{:S(2)}) collective-permute-start(bf16[2,1,128,128]{3,2,0,1:T(8,128)(2,1)S(1)} %bitcast.270), channel_id=1, source_target_pairs={{1,0},{2,1},{3,2},{4,3},{5,4},{6,5},{7,6},{8,7},{9,8},{10,9},{11,1... | collective-permute-start | bytes 196616 | tf_op jit(solution)/shard_map/ppermute | solution.py:21
  270.1 6.8 %collective-permute-start.12 = (bf16[2,1,128,128]{3,2,0,1:T(8,128)(2,1)S(1)}, bf16[2,1,128,128]{3,2,0,1:T(8,128)(2,1)S(1)}, u32[]{:S(2)}, u32[]{:S(2)}) collective-permute-start(bf16[2,1,128,128]{3,2,0,1:T(8,128)(2,1)S(1)} %bitcast.268), channel_id=1, source_target_pairs={{0,1},{1,2},{2,3},{3,4},{4,5},{5,6},{6,7},{7,8},{8,9},{9,10},{10,1... | collective-permute-start | bytes 196616 | tf_op jit(solution)/shard_map/ppermute | solution.py:19
  274.3 76.5 %collective-permute-start.21 = (f32[2,1,256,128]{3,2,1,0:T(8,128)S(1)}, f32[2,1,256,128]{3,2,1,0:T(8,128)S(1)}, u32[]{:S(2)}, u32[]{:S(2)}) collective-permute-start(f32[2,1,256,128]{3,2,1,0:T(8,128)S(1)} %add_add_fusion), channel_id=1, source_target_pairs={{20,0},{52,32},{84,64},{116,96},{148,128},{180,160},{212,192},{244... | collective-permute-start | bytes 786440 | tf_op jit(solution)/shard_map/ppermute | solution.py:56
  275.6 75.2 %collective-permute-start.20 = (f32[2,1,256,128]{3,2,1,0:T(8,128)S(1)}, f32[2,1,256,128]{3,2,1,0:T(8,128)S(1)}, u32[]{:S(2)}, u32[]{:S(2)}) collective-permute-start(f32[2,1,256,128]{3,2,1,0:T(8,128)S(1)} %add_add_fusion), channel_id=1, source_target_pairs={{16,0},{48,32},{80,64},{112,96},{144,128},{176,160},{208,192},{240... | collective-permute-start | bytes 786440 | tf_op jit(solution)/shard_map/ppermute | solution.py:56
  276.9 73.9 %collective-permute-start.19 = (f32[2,1,256,128]{3,2,1,0:T(8,128)S(1)}, f32[2,1,256,128]{3,2,1,0:T(8,128)S(1)}, u32[]{:S(2)}, u32[]{:S(2)}) collective-permute-start(f32[2,1,256,128]{3,2,1,0:T(8,128)S(1)} %add_add_fusion), channel_id=1, source_target_pairs={{12,0},{44,32},{76,64},{108,96},{140,128},{172,160},{204,192},{236... | collective-permute-start | bytes 786440 | tf_op jit(solution)/shard_map/ppermute | solution.py:56
  344.3 9.3 %collective-permute-start.18 = (f32[2,1,256,128]{3,2,1,0:T(8,128)S(1)}, f32[2,1,256,128]{3,2,1,0:T(8,128)}, u32[]{:S(2)}, u32[]{:S(2)}) collective-permute-start(f32[2,1,256,128]{3,2,1,0:T(8,128)S(1)} %add_add_fusion), channel_id=1, source_target_pairs={{8,0},{40,32},{72,64},{104,96},{136,128},{168,160},{200,192},{232,... | collective-permute-start | bytes 786440 | tf_op jit(solution)/shard_map/ppermute | solution.py:56
  345.6 15.4 %collective-permute-start.17 = (f32[2,1,256,128]{3,2,1,0:T(8,128)S(1)}, f32[2,1,256,128]{3,2,1,0:T(8,128)}, u32[]{:S(2)}, u32[]{:S(2)}) collective-permute-start(f32[2,1,256,128]{3,2,1,0:T(8,128)S(1)} %add_add_fusion), channel_id=1, source_target_pairs={{4,0},{36,32},{68,64},{100,96},{132,128},{164,160},{196,192},{228,... | collective-permute-start | bytes 786440 | tf_op jit(solution)/shard_map/ppermute | solution.py:56

commit v3 on v2

--- a/solution.py
+++ b/solution.py
@@ -162,7 +162,7 @@
     wanted = lax.all_to_all(ordered_table, "seq", split_axis=0, concat_axis=0, tiled=True)
     served = jnp.take(jnp.transpose(kv_blocks, (2, 0, 1, 3, 4)), wanted.reshape(-1), axis=0)
     served = served.reshape(groups, capacity, 2, head_count, BLK, HD)
-    served, global_kv = lax.optimization_barrier((served, global_kv))
+    served, global_kv, window_kv = lax.optimization_barrier((served, global_kv, window_kv))
     fetched = lax.all_to_all(served, "seq", split_axis=0, concat_axis=0, tiled=True)
     chosen = jnp.take(fetched.reshape(groups * capacity, 2, head_count, BLK, HD), places, axis=0)
     remote_kv = jnp.transpose(
@@ -196,9 +196,6 @@
     )
     outward = jnp.concatenate([extended[:, :, 0], extended[:, :, query_count + 1]], axis=2)
     inward = with_halo(outward.astype(jnp.bfloat16), (("seq", 2),), BLK).astype(outward.dtype)
-    own_grad = extended[:, :, 1 : query_count + 1]
-    own_grad = own_grad.at[:, :, 0].add(inward[:, :, :BLK])
-    own_grad = own_grad.at[:, :, query_count - 1].add(inward[:, :, 3 * BLK :])
     random_terms = jnp.transpose(
         jnp.stack([key_random, value_random]).reshape(2, head_count, query_count * RAND, BLK, HD),
         (2, 0, 1, 3, 4),
@@ -209,6 +206,7 @@
     outgoing = jnp.einsum(
         "pj,jxhid->pxhid", send_pick, random_terms, preferred_element_type=jnp.float32
     ).astype(jnp.bfloat16)
+    outgoing, inward, global_sum = lax.optimization_barrier((outgoing, inward, global_sum))
     incoming = lax.all_to_all(
         outgoing.reshape(groups, capacity, 2, head_count, BLK, HD),
         "seq",
@@ -225,6 +223,9 @@
         incoming.reshape(groups * capacity, 2, head_count, BLK, HD),
         preferred_element_type=jnp.float32,
     )
+    own_grad = extended[:, :, 1 : query_count + 1]
+    own_grad = own_grad.at[:, :, 0].add(inward[:, :, :BLK])
+    own_grad = own_grad.at[:, :, query_count - 1].add(inward[:, :, 3 * BLK :])
     global_sum = global_sum.reshape(2, head_count, 2, BLK, HD)
     own_grad = own_grad.at[:, :, 0:2].add(jnp.where(my_group == 0, global_sum, 0.0))
     total_grad = (own_grad + random_sum).astype(jnp.bfloat16)

time: 410 us -> 434 us (1.059)
  waiting for transfers between devices: 221 us -> 237 us
    all_to_all x1, waiting for transfers between devices: 0.01 us -> 82.3 us  [shards(): lax.all_to_all(outgoing.reshape(groups, capacity, 2, head_count, BLK, HD)...]
    ppermute x7, waiting for transfers between devices: 76.3 us -> 15 us  [reduce_to_first(): total = total + lax.ppermute(value, axis, [(row * width, 0)])]
    all_to_all x1, waiting for transfers between devices: 73.5 us -> 86.8 us  [shards(): lax.all_to_all(served, 'seq', split_axis=0, concat_axis=0, tiled=True)]
    ppermute x3, waiting for transfers between devices: 25.3 us -> 12.3 us  [reduce_to_first(): total = total + lax.ppermute(value, axis, pairs)]
    all_to_all x1, starting transfers between devices: 14.2 us -> 5.09 us  [shards(): lax.all_to_all(outgoing.reshape(groups, capacity, 2, head_count, BLK, HD)...]
    ppermute x7, waiting for transfers between devices: 0.99 us -> 7.02 us  [broadcast(): got = got + lax.ppermute(value, axis, [(0, row * width)])]
    ppermute x7, starting transfers between devices: 17.8 us -> 22.6 us  [broadcast(): got = got + lax.ppermute(value, axis, [(0, row * width)])]
    ppermute x2, waiting for transfers between devices: 4.78 us -> 0.01 us  [with_halo(): lax.ppermute(tail, axis, [(i, (i + 1) % count) for i in range(ends)])]
  transfers between devices with their start and end apart: 28 -> 28, of which waited for: 11 -> 14; matrix products, arithmetic and copies ran while one was open for 6% -> 8% of each run, Pallas kernels for 0% -> 0%
where the time goes in v3:
time: 434 us; the launch traced here: 432 us
  waiting for transfers between devices  237 us (55%)
  starting transfers between devices  74.3 us (17%)
  local copies, waits for them, and re-layouts  52.1 us (12%)
  blocking collectives  34 us (8%)
  other arithmetic  17.6 us (4%)
  matrix products  15.7 us (4%)
    all_to_all x1, waiting for transfers between devices, shards(): lax.all_to_all(served, 'seq', split_axis=0, concat_axis=0, tiled=True)  86.8 us
    all_to_all x1, waiting for transfers between devices, shards(): lax.all_to_all(outgoing.reshape(groups, capacity, 2, head_count, BLK, HD)...  82.3 us
    all_to_all x1, blocking collectives, shards(): lax.all_to_all(jnp.stack([by_token(attended.reshape(flat)), by_token(grad...  34 us
    all_to_all x1, waiting for transfers between devices, shards(): lax.all_to_all(jnp.stack([queries, keys, values, grad_out]), 'head', spli...  26.6 us
    ppermute x7, starting transfers between devices, broadcast(): got = got + lax.ppermute(value, axis, [(0, row * width)])  22.6 us
    ppermute x7, waiting for transfers between devices, reduce_to_first(): total = total + lax.ppermute(value, axis, [(row * width, 0)])  15 us
    ppermute x3, waiting for transfers between devices, reduce_to_first(): total = total + lax.ppermute(value, axis, pairs)  12.3 us
    unnamed x60, local copies, waits for them, and re-layouts  11.9 us
  transfers between devices with their start and end apart: 28, of which 14 were waited for; matrix products, arithmetic and copies ran while one was open for 8% of the time, Pallas kernels for 0%

profile of v3, /device:TPU:1, one launch (start us, length us, event | category | flops | bytes accessed | tf_op | source)
XLA Modules:
  0.0 432.1 jit_solution(15619300704526994053)
XLA Ops:
  0.6 1.3 pad_maximum_fusion.3
  2.0 1.4 copy.106
  3.4 2.3 reshape.1009
  5.6 10.3 %all-to-all-start = ((bf16[16,2,16384]{2,1,0:T(2,128)(2,1)}), bf16[16,2,16384]{2,1,0:T(2,128)(2,1)S(1)}, u32[]{:S(2)}, u32[]{:S(2)}) async-start(bf16[16,2,16384]{2,1,0:T(2,128)(2,1)} %reshape.1009), calls=%async_computation | async-start | bytes 2097152 | tf_op jit(solution)/shard_map/all_to_all | solution.py:140
  17.3 26.6 %all-to-all-done = bf16[16,2,16384]{2,1,0:T(2,128)(2,1)S(1)} async-done(((bf16[16,2,16384]{2,1,0:T(2,128)(2,1)}), bf16[16,2,16384]{2,1,0:T(2,128)(2,1)S(1)}, u32[]{:S(2)}, u32[]{:S(2)}) %all-to-all-start) | async-done | bytes 1048608 | tf_op jit(solution)/shard_map/all_to_all | solution.py:140
  43.9 1.3 reshape.1010
  45.3 2.3 copy.107
  47.6 1.3 fusion.54
  48.9 8.9 %collective-permute-start.6 = (bf16[2,1,256,128]{3,2,1,0:T(8,128)(2,1)S(1)}, bf16[2,1,256,128]{3,2,1,0:T(8,128)(2,1)S(1)}, u32[]{:S(2)}, u32[]{:S(2)}) collective-permute-start(bf16[2,1,256,128]{3,2,1,0:T(8,128)(2,1)S(1)} %bitcast.255), channel_id=1, source_target_pairs={{0,28},{32,60},{64,92},{96,124},{128,156},{160,188},{192,220},{224... | collective-permute-start | bytes 393224 | tf_op jit(solution)/shard_map/ppermute | solution.py:38
  57.8 1.3 collective-permute-start.5
  59.1 1.3 collective-permute-start.4
  60.5 3.8 all-to-all-start.1
  64.4 3.0 collective-permute-start.10
  67.4 1.3 collective-permute-start.11
  68.7 4.1 all-to-all-done.1
  74.4 3.1 gather_fusion
  77.5 4.6 %broadcast_select_fusion = bf16[32,2,2,1,128,128]{5,4,2,1,3,0:T(8,128)(2,1)} fusion(bf16[32,2,2,1,128,128]{5,4,2,1,3,0:T(8,128)(2,1)} %bitcast.210, pred[32,2]{1,0:T(8,128)(4,1)S(1)} %copy.112), kind=kLoop, calls=%fused_computation.9 | loop fusion | flops 2097152 | bytes 8388672 | tf_op jit(solution)/shard_map/jit(_take)/select_n | solution.py:163
  82.0 7.2 %collective-permute-start.3 = (bf16[2,1,256,128]{3,2,1,0:T(8,128)(2,1)S(1)}, bf16[2,1,256,128]{3,2,1,0:T(8,128)(2,1)S(1)}, u32[]{:S(2)}, u32[]{:S(2)}) collective-permute-start(bf16[2,1,256,128]{3,2,1,0:T(8,128)(2,1)S(1)} %bitcast.258), channel_id=1, source_target_pairs={{0,16},{32,48},{64,80},{96,112},{128,144},{160,176},{192,208},{224... | collective-permute-start | bytes 393224 | tf_op jit(solution)/shard_map/ppermute | solution.py:38
  89.2 1.3 collective-permute-start.2
  90.6 1.3 collective-permute-start.1
  91.9 1.3 collective-permute-start
  93.6 1.4 collective-permute-done.2
  95.0 2.8 collective-permute-done.1
  97.8 2.8 collective-permute-done
  100.7 1.3 collective-permute-start.9
  102.0 1.3 collective-permute-start.8
  103.3 1.3 collective-permute-start.7
  105.9 2.7 collective-permute-done.7
  108.6 5.9 %all-to-all-start.2 = ((bf16[32,2,2,1,128,128]{5,4,2,1,3,0:T(8,128)(2,1)}), bf16[32,2,2,1,128,128]{5,4,2,1,3,0:T(8,128)(2,1)}, u32[]{:S(2)}, u32[]{:S(2)}) async-start(bf16[32,2,2,1,128,128]{5,4,2,1,3,0:T(8,128)(2,1)} %broadcast_select_fusion), calls=%async_computation.2 | async-start | bytes 8388608 | tf_op jit(solution)/shard_map/all_to_all | solution.py:166
  115.2 1.3 convolution_bitcast_fusion.5
  116.6 1.6 convolution_bitcast_fusion.3
  118.2 1.6 convolution_bitcast_fusion.1
  119.8 86.8 %all-to-all-done.2 = bf16[32,2,2,1,128,128]{5,4,2,1,3,0:T(8,128)(2,1)} async-done(((bf16[32,2,2,1,128,128]{5,4,2,1,3,0:T(8,128)(2,1)}), bf16[32,2,2,1,128,128]{5,4,2,1,3,0:T(8,128)(2,1)}, u32[]{:S(2)}, u32[]{:S(2)}) %all-to-all-start.2) | async-done | bytes 4194336 | tf_op jit(solution)/shard_map/all_to_all | solution.py:166
  206.6 4.1 gather_fusion.1
  210.7 1.6 fusion.5
  216.4 1.7 multiply_reduce_fusion
  218.1 1.8 multiply_convert_fusion
  220.6 1.3 collective-permute-start.15
  221.9 1.3 collective-permute-start.16
  223.2 1.5 collective-permute-start.14
  226.5 3.7 collective-permute-done.15
  230.3 8.5 %collective-permute-done.16 = f32[2,1,256,128]{3,2,1,0:T(8,128)S(1)} collective-permute-done((f32[2,1,256,128]{3,2,1,0:T(8,128)S(1)}, f32[2,1,256,128]{3,2,1,0:T(8,128)S(1)}, u32[]{:S(2)}, u32[]{:S(2)}) %collective-permute-start.16) | collective-permute-done | bytes 262176 | tf_op jit(solution)/shard_map/ppermute | solution.py:53
  238.9 1.3 collective-permute-start.23
  240.2 1.3 collective-permute-start.22
  243.1 1.3 collective-permute-start.13
  244.4 4.0 collective-permute-start.12
  248.4 1.3 collective-permute-start.21
  249.7 1.3 collective-permute-start.20
  251.0 1.3 collective-permute-start.19
  252.3 2.7 collective-permute-done.23
  255.0 1.3 collective-permute-start.18
  256.3 1.3 collective-permute-start.17
  257.6 3.4 convert_bitcast_fusion
  261.8 3.9 collective-permute-done.21
  265.7 2.9 collective-permute-done.18
  268.6 5.6 %collective-permute-done.17 = f32[2,1,256,128]{3,2,1,0:T(8,128)S(1)} collective-permute-done((f32[2,1,256,128]{3,2,1,0:T(8,128)S(1)}, f32[2,1,256,128]{3,2,1,0:T(8,128)S(1)}, u32[]{:S(2)}, u32[]{:S(2)}) %collective-permute-start.17) | collective-permute-done | bytes 262176 | tf_op jit(solution)/shard_map/ppermute | solution.py:56
  274.3 8.7 %copy.133 = bf16[32,2,2,1,128,128]{5,1,4,2,3,0:T(2,128)(2,1)} copy(bf16[32,2,2,1,128,128]{5,1,0,4,2,3:T(2,128)(2,1)} %bitcast.208) | data formatting | bytes 8388608 | tf_op jit(solution)/shard_map/reshape | solution.py:211
  283.1 5.1 %all-to-all-start.3 = ((bf16[32,2,2,1,128,128]{5,1,4,2,3,0:T(2,128)(2,1)}), bf16[32,2,2,1,128,128]{5,1,4,2,3,0:T(2,128)(2,1)}, u32[]{:S(2)}, u32[]{:S(2)}) async-start(bf16[32,2,2,1,128,128]{5,1,4,2,3,0:T(2,128)(2,1)} %copy.133), calls=%async_computation.3 | async-start | bytes 8388608 | tf_op jit(solution)/shard_map/all_to_all | solution.py:210
  289.0 1.8 copy-done.3
  296.3 3.0 scatter-add.11
  299.7 82.3 %all-to-all-done.3 = bf16[32,2,2,1,128,128]{5,1,4,2,3,0:T(2,128)(2,1)} async-done(((bf16[32,2,2,1,128,128]{5,1,4,2,3,0:T(2,128)(2,1)}), bf16[32,2,2,1,128,128]{5,1,4,2,3,0:T(2,128)(2,1)}, u32[]{:S(2)}, u32[]{:S(2)}) %all-to-all-start.3) | async-done | bytes 4194336 | tf_op jit(solution)/shard_map/all_to_all | solution.py:210
  382.0 7.0 %copy.134 = bf16[32,2,2,1,128,128]{5,1,0,4,2,3:T(2,128)(2,1)S(1)} copy(bf16[32,2,2,1,128,128]{5,1,4,2,3,0:T(2,128)(2,1)} %all-to-all-done.3) | data formatting | bytes 8388608 | tf_op jit(solution)/shard_map/all_to_all | solution.py:210
  391.6 34.0 %all_to_all.49 = bf16[4,1024,128]{2,0,1:T(4,128)(2,1)S(1)} all-to-all(bf16[4,1024,128]{2,0,1:T(4,128)(2,1)S(1)} %copy.137), channel_id=1, replica_groups=mesh['head'=16,'seq'=32] {'head'}, dimensions={1} | all-to-all | bytes 2097152 | tf_op jit(solution)/shard_map/all_to_all | solution.py:233
  425.6 2.2 fusion.53
  (153 shorter events, 28.0 us)
Async XLA Ops:
  3.4 12.6 %copy-start.19 = (s32[8,3]{0,1:T(4,128)S(1)}, s32[8,3]{0,1:T(4,128)}, u32[]{:S(2)}) copy-start(s32[8,3]{0,1:T(4,128)} %param.15) | copy-start | bytes 292
  5.6 38.3 %all-to-all-start = ((bf16[16,2,16384]{2,1,0:T(2,128)(2,1)}), bf16[16,2,16384]{2,1,0:T(2,128)(2,1)S(1)}, u32[]{:S(2)}, u32[]{:S(2)}) async-start(bf16[16,2,16384]{2,1,0:T(2,128)(2,1)} %reshape.1009), calls=%async_computation | async-start | bytes 2097152 | tf_op jit(solution)/shard_map/all_to_all | solution.py:140
  16.0 1.2 copy-start.16
  16.4 0.8 copy-start.20
  16.5 0.8 copy-start.22
  48.9 41.7 %collective-permute-start.6 = (bf16[2,1,256,128]{3,2,1,0:T(8,128)(2,1)S(1)}, bf16[2,1,256,128]{3,2,1,0:T(8,128)(2,1)S(1)}, u32[]{:S(2)}, u32[]{:S(2)}) collective-permute-start(bf16[2,1,256,128]{3,2,1,0:T(8,128)(2,1)S(1)} %bitcast.255), channel_id=1, source_target_pairs={{0,28},{32,60},{64,92},{96,124},{128,156},{160,188},{192,220},{224... | collective-permute-start | bytes 393224 | tf_op jit(solution)/shard_map/ppermute | solution.py:38
  57.8 34.1 %collective-permute-start.5 = (bf16[2,1,256,128]{3,2,1,0:T(8,128)(2,1)S(1)}, bf16[2,1,256,128]{3,2,1,0:T(8,128)(2,1)S(1)}, u32[]{:S(2)}, u32[]{:S(2)}) collective-permute-start(bf16[2,1,256,128]{3,2,1,0:T(8,128)(2,1)S(1)} %bitcast.256), channel_id=1, source_target_pairs={{0,24},{32,56},{64,88},{96,120},{128,152},{160,184},{192,216},{224... | collective-permute-start | bytes 393224 | tf_op jit(solution)/shard_map/ppermute | solution.py:38
  59.1 34.5 %collective-permute-start.4 = (bf16[2,1,256,128]{3,2,1,0:T(8,128)(2,1)S(1)}, bf16[2,1,256,128]{3,2,1,0:T(8,128)(2,1)S(1)}, u32[]{:S(2)}, u32[]{:S(2)}) collective-permute-start(bf16[2,1,256,128]{3,2,1,0:T(8,128)(2,1)S(1)} %bitcast.257), channel_id=1, source_target_pairs={{0,20},{32,52},{64,84},{96,116},{128,148},{160,180},{192,212},{224... | collective-permute-start | bytes 393224 | tf_op jit(solution)/shard_map/ppermute | solution.py:38
  60.5 12.3 %all-to-all-start.1 = ((s32[32,1,2]{2,1,0:T(1,128)}), s32[32,1,2]{2,1,0:T(1,128)S(1)}, u32[]{:S(2)}, u32[]{:S(2)}) async-start(s32[32,1,2]{2,1,0:T(1,128)} %bitcast.87), calls=%async_computation.1 | async-start | bytes 32768 | tf_op jit(solution)/shard_map/all_to_all | solution.py:162
  64.4 17.7 %collective-permute-start.10 = (bf16[2,1,128,128]{3,2,0,1:T(8,128)(2,1)S(1)}, bf16[2,1,128,128]{3,2,0,1:T(8,128)(2,1)S(1)}, u32[]{:S(2)}, u32[]{:S(2)}) collective-permute-start(bf16[2,1,128,128]{3,2,0,1:T(8,128)(2,1)S(1)} %get-tuple-element.78), channel_id=1, source_target_pairs={{0,1},{1,2},{2,3},{3,4},{4,5},{5,6},{6,7},{7,8},{8,9},{9,10},{10,1... | collective-permute-start | bytes 196616 | tf_op jit(solution)/shard_map/ppermute | solution.py:19
  67.4 21.8 %collective-permute-start.11 = (bf16[2,1,128,128]{3,2,0,1:T(8,128)(2,1)S(1)}, bf16[2,1,128,128]{3,2,0,1:T(8,128)(2,1)S(1)}, u32[]{:S(2)}, u32[]{:S(2)}) collective-permute-start(bf16[2,1,128,128]{3,2,0,1:T(8,128)(2,1)S(1)} %get-tuple-element.79), channel_id=1, source_target_pairs={{1,0},{2,1},{3,2},{4,3},{5,4},{6,5},{7,6},{8,7},{9,8},{10,9},{11,1... | collective-permute-start | bytes 196616 | tf_op jit(solution)/shard_map/ppermute | solution.py:21
  82.0 11.6 %collective-permute-start.3 = (bf16[2,1,256,128]{3,2,1,0:T(8,128)(2,1)S(1)}, bf16[2,1,256,128]{3,2,1,0:T(8,128)(2,1)S(1)}, u32[]{:S(2)}, u32[]{:S(2)}) collective-permute-start(bf16[2,1,256,128]{3,2,1,0:T(8,128)(2,1)S(1)} %bitcast.258), channel_id=1, source_target_pairs={{0,16},{32,48},{64,80},{96,112},{128,144},{160,176},{192,208},{224... | collective-permute-start | bytes 393224 | tf_op jit(solution)/shard_map/ppermute | solution.py:38
  89.2 5.8 %collective-permute-start.2 = (bf16[2,1,256,128]{3,2,1,0:T(8,128)(2,1)S(1)}, bf16[2,1,256,128]{3,2,1,0:T(8,128)(2,1)S(1)}, u32[]{:S(2)}, u32[]{:S(2)}) collective-permute-start(bf16[2,1,256,128]{3,2,1,0:T(8,128)(2,1)S(1)} %bitcast.259), channel_id=1, source_target_pairs={{0,12},{32,44},{64,76},{96,108},{128,140},{160,172},{192,204},{224... | collective-permute-start | bytes 393224 | tf_op jit(solution)/shard_map/ppermute | solution.py:38
  90.6 7.2 %collective-permute-start.1 = (bf16[2,1,256,128]{3,2,1,0:T(8,128)(2,1)S(1)}, bf16[2,1,256,128]{3,2,1,0:T(8,128)(2,1)S(1)}, u32[]{:S(2)}, u32[]{:S(2)}) collective-permute-start(bf16[2,1,256,128]{3,2,1,0:T(8,128)(2,1)S(1)} %bitcast.260), channel_id=1, source_target_pairs={{0,8},{32,40},{64,72},{96,104},{128,136},{160,168},{192,200},{224,... | collective-permute-start | bytes 393224 | tf_op jit(solution)/shard_map/ppermute | solution.py:38
  91.9 8.7 %collective-permute-start = (bf16[2,1,256,128]{3,2,1,0:T(8,128)(2,1)S(1)}, bf16[2,1,256,128]{3,2,1,0:T(8,128)(2,1)S(1)}, u32[]{:S(2)}, u32[]{:S(2)}) collective-permute-start(bf16[2,1,256,128]{3,2,1,0:T(8,128)(2,1)S(1)} %bitcast.261), channel_id=1, source_target_pairs={{0,4},{32,36},{64,68},{96,100},{128,132},{160,164},{192,196},{224,... | collective-permute-start | bytes 393224 | tf_op jit(solution)/shard_map/ppermute | solution.py:38
  100.7 5.2 %collective-permute-start.9 = (bf16[2,1,256,128]{3,2,1,0:T(8,128)(2,1)S(1)}, bf16[2,1,256,128]{3,2,1,0:T(8,128)(2,1)S(1)}, u32[]{:S(2)}, u32[]{:S(2)}) collective-permute-start(bf16[2,1,256,128]{3,2,1,0:T(8,128)(2,1)S(1)} %add_select_fusion.1), channel_id=1, source_target_pairs={{0,3},{4,7},{8,11},{12,15},{16,19},{20,23},{24,27},{28,31},{32,35}... | collective-permute-start | bytes 393224 | tf_op jit(solution)/shard_map/ppermute | solution.py:43
  102.0 3.9 collective-permute-start.8
  103.3 5.2 %collective-permute-start.7 = (bf16[2,1,256,128]{3,2,1,0:T(8,128)(2,1)S(1)}, bf16[2,1,256,128]{3,2,1,0:T(8,128)(2,1)S(1)}, u32[]{:S(2)}, u32[]{:S(2)}) collective-permute-start(bf16[2,1,256,128]{3,2,1,0:T(8,128)(2,1)S(1)} %add_select_fusion.1), channel_id=1, source_target_pairs={{0,1},{4,5},{8,9},{12,13},{16,17},{20,21},{24,25},{28,29},{32,33},... | collective-permute-start | bytes 393224 | tf_op jit(solution)/shard_map/ppermute | solution.py:43
  108.5 6.0 %copy-start.17 = (s32[8,3]{1,0:T(8,128)S(1)}, s32[8,3]{1,0:T(8,128)}, u32[]{:S(2)}) copy-start(s32[8,3]{1,0:T(8,128)} %copy-done.16) | copy-start | bytes 292
  108.6 6.0 %copy-start.21 = (s32[24]{0:T(128)S(1)}, s32[24]{0:T(128)}, u32[]{:S(2)}) copy-start(s32[24]{0:T(128)} %copy-done.20) | copy-start | bytes 292
  108.6 98.0 %all-to-all-start.2 = ((bf16[32,2,2,1,128,128]{5,4,2,1,3,0:T(8,128)(2,1)}), bf16[32,2,2,1,128,128]{5,4,2,1,3,0:T(8,128)(2,1)}, u32[]{:S(2)}, u32[]{:S(2)}) async-start(bf16[32,2,2,1,128,128]{5,4,2,1,3,0:T(8,128)(2,1)} %broadcast_select_fusion), calls=%async_computation.2 | async-start | bytes 8388608 | tf_op jit(solution)/shard_map/all_to_all | solution.py:166
  115.2 2.9 copy-start.4
  212.5 1.0 copy-start.10
  212.5 2.3 copy-start.8
  214.7 1.4 copy-start.6
  214.8 1.7 copy-start.7
  219.9 6.2 %copy-start.2 = (bf16[1,8,128,1024]{3,2,1,0:T(8,128)(2,1)}, bf16[1,8,128,1024]{3,2,1,0:T(8,128)(2,1)S(1)}, u32[]{:S(2)}) copy-start(bf16[1,8,128,1024]{3,2,1,0:T(8,128)(2,1)S(1)} %get-tuple-element.56) | copy-start | bytes 6291460
  219.9 21.6 %copy-start = (bf16[1,8,128,1024]{3,2,1,0:T(8,128)(2,1)}, bf16[1,8,128,1024]{3,2,1,0:T(8,128)(2,1)S(1)}, u32[]{:S(2)}) copy-start(bf16[1,8,128,1024]{3,2,1,0:T(8,128)(2,1)S(1)} %get-tuple-element.57) | copy-start | bytes 6291460
  220.6 9.6 %collective-permute-start.15 = (f32[2,1,256,128]{3,2,1,0:T(8,128)S(1)}, f32[2,1,256,128]{3,2,1,0:T(8,128)S(1)}, u32[]{:S(2)}, u32[]{:S(2)}) collective-permute-start(f32[2,1,256,128]{3,2,1,0:T(8,128)S(1)} %pad_maximum_fusion.7), channel_id=1, source_target_pairs={{2,0},{6,4},{10,8},{14,12},{18,16},{22,20},{26,24},{30,28},{34,32}... | collective-permute-start | bytes 786440 | tf_op jit(solution)/shard_map/ppermute | solution.py:53
  221.9 16.9 %collective-permute-start.16 = (f32[2,1,256,128]{3,2,1,0:T(8,128)S(1)}, f32[2,1,256,128]{3,2,1,0:T(8,128)S(1)}, u32[]{:S(2)}, u32[]{:S(2)}) collective-permute-start(f32[2,1,256,128]{3,2,1,0:T(8,128)S(1)} %pad_maximum_fusion.7), channel_id=1, source_target_pairs={{3,0},{7,4},{11,8},{15,12},{19,16},{23,20},{27,24},{31,28},{35,32}... | collective-permute-start | bytes 786440 | tf_op jit(solution)/shard_map/ppermute | solution.py:53
  223.2 15.6 %collective-permute-start.14 = (f32[2,1,256,128]{3,2,1,0:T(8,128)S(1)}, f32[2,1,256,128]{3,2,1,0:T(8,128)S(1)}, u32[]{:S(2)}, u32[]{:S(2)}) collective-permute-start(f32[2,1,256,128]{3,2,1,0:T(8,128)S(1)} %pad_maximum_fusion.7), channel_id=1, source_target_pairs={{1,0},{5,4},{9,8},{13,12},{17,16},{21,20},{25,24},{29,28},{33,32},... | collective-permute-start | bytes 786440 | tf_op jit(solution)/shard_map/ppermute | solution.py:53
  238.9 16.1 %collective-permute-start.23 = (f32[2,1,256,128]{3,2,1,0:T(8,128)S(1)}, f32[2,1,256,128]{3,2,1,0:T(8,128)S(1)}, u32[]{:S(2)}, u32[]{:S(2)}) collective-permute-start(f32[2,1,256,128]{3,2,1,0:T(8,128)S(1)} %add_add_fusion.1), channel_id=1, source_target_pairs={{28,0},{60,32},{92,64},{124,96},{156,128},{188,160},{220,192},{252... | collective-permute-start | bytes 786440 | tf_op jit(solution)/shard_map/ppermute | solution.py:56
  240.2 16.1 %collective-permute-start.22 = (f32[2,1,256,128]{3,2,1,0:T(8,128)S(1)}, f32[2,1,256,128]{3,2,1,0:T(8,128)S(1)}, u32[]{:S(2)}, u32[]{:S(2)}) collective-permute-start(f32[2,1,256,128]{3,2,1,0:T(8,128)S(1)} %add_add_fusion.1), channel_id=1, source_target_pairs={{24,0},{56,32},{88,64},{120,96},{152,128},{184,160},{216,192},{248... | collective-permute-start | bytes 786440 | tf_op jit(solution)/shard_map/ppermute | solution.py:56
  243.0 14.5 %copy-start.23 = (s32[24]{0:T(128)S(1)}, s32[24]{0:T(128)}, u32[]{:S(2)}) copy-start(s32[24]{0:T(128)} %copy-done.22) | copy-start | bytes 292
  243.1 6.6 %collective-permute-start.13 = (bf16[2,1,128,128]{3,2,0,1:T(8,128)(2,1)S(1)}, bf16[2,1,128,128]{3,2,0,1:T(8,128)(2,1)S(1)}, u32[]{:S(2)}, u32[]{:S(2)}) collective-permute-start(bf16[2,1,128,128]{3,2,0,1:T(8,128)(2,1)S(1)} %bitcast.270), channel_id=1, source_target_pairs={{1,0},{2,1},{3,2},{4,3},{5,4},{6,5},{7,6},{8,7},{9,8},{10,9},{11,1... | collective-permute-start | bytes 196616 | tf_op jit(solution)/shard_map/ppermute | solution.py:21
  244.4 6.6 %collective-permute-start.12 = (bf16[2,1,128,128]{3,2,0,1:T(8,128)(2,1)S(1)}, bf16[2,1,128,128]{3,2,0,1:T(8,128)(2,1)S(1)}, u32[]{:S(2)}, u32[]{:S(2)}) collective-permute-start(bf16[2,1,128,128]{3,2,0,1:T(8,128)(2,1)S(1)} %bitcast.268), channel_id=1, source_target_pairs={{0,1},{1,2},{2,3},{3,4},{4,5},{5,6},{6,7},{7,8},{8,9},{9,10},{10,1... | collective-permute-start | bytes 196616 | tf_op jit(solution)/shard_map/ppermute | solution.py:19
  248.4 17.3 %collective-permute-start.21 = (f32[2,1,256,128]{3,2,1,0:T(8,128)S(1)}, f32[2,1,256,128]{3,2,1,0:T(8,128)S(1)}, u32[]{:S(2)}, u32[]{:S(2)}) collective-permute-start(f32[2,1,256,128]{3,2,1,0:T(8,128)S(1)} %add_add_fusion.1), channel_id=1, source_target_pairs={{20,0},{52,32},{84,64},{116,96},{148,128},{180,160},{212,192},{244... | collective-permute-start | bytes 786440 | tf_op jit(solution)/shard_map/ppermute | solution.py:56
  249.7 16.0 %collective-permute-start.20 = (f32[2,1,256,128]{3,2,1,0:T(8,128)S(1)}, f32[2,1,256,128]{3,2,1,0:T(8,128)S(1)}, u32[]{:S(2)}, u32[]{:S(2)}) collective-permute-start(f32[2,1,256,128]{3,2,1,0:T(8,128)S(1)} %add_add_fusion.1), channel_id=1, source_target_pairs={{16,0},{48,32},{80,64},{112,96},{144,128},{176,160},{208,192},{240... | collective-permute-start | bytes 786440 | tf_op jit(solution)/shard_map/ppermute | solution.py:56
  251.0 14.7 %collective-permute-start.19 = (f32[2,1,256,128]{3,2,1,0:T(8,128)S(1)}, f32[2,1,256,128]{3,2,1,0:T(8,128)S(1)}, u32[]{:S(2)}, u32[]{:S(2)}) collective-permute-start(f32[2,1,256,128]{3,2,1,0:T(8,128)S(1)} %add_add_fusion.1), channel_id=1, source_target_pairs={{12,0},{44,32},{76,64},{108,96},{140,128},{172,160},{204,192},{236... | collective-permute-start | bytes 786440 | tf_op jit(solution)/shard_map/ppermute | solution.py:56
  255.0 13.6 %collective-permute-start.18 = (f32[2,1,256,128]{3,2,1,0:T(8,128)S(1)}, f32[2,1,256,128]{3,2,1,0:T(8,128)S(1)}, u32[]{:S(2)}, u32[]{:S(2)}) collective-permute-start(f32[2,1,256,128]{3,2,1,0:T(8,128)S(1)} %add_add_fusion.1), channel_id=1, source_target_pairs={{8,0},{40,32},{72,64},{104,96},{136,128},{168,160},{200,192},{232,... | collective-permute-start | bytes 786440 | tf_op jit(solution)/shard_map/ppermute | solution.py:56
  256.3 17.9 %collective-permute-start.17 = (f32[2,1,256,128]{3,2,1,0:T(8,128)S(1)}, f32[2,1,256,128]{3,2,1,0:T(8,128)S(1)}, u32[]{:S(2)}, u32[]{:S(2)}) collective-permute-start(f32[2,1,256,128]{3,2,1,0:T(8,128)S(1)} %add_add_fusion.1), channel_id=1, source_target_pairs={{4,0},{36,32},{68,64},{100,96},{132,128},{164,160},{196,192},{228,... | collective-permute-start | bytes 786440 | tf_op jit(solution)/shard_map/ppermute | solution.py:56
  283.1 98.9 %all-to-all-start.3 = ((bf16[32,2,2,1,128,128]{5,1,4,2,3,0:T(2,128)(2,1)}), bf16[32,2,2,1,128,128]{5,1,4,2,3,0:T(2,128)(2,1)}, u32[]{:S(2)}, u32[]{:S(2)}) async-start(bf16[32,2,2,1,128,128]{5,1,4,2,3,0:T(2,128)(2,1)} %copy.133), calls=%async_computation.3 | async-start | bytes 8388608 | tf_op jit(solution)/shard_map/all_to_all | solution.py:210
  288.8 2.1 copy-start.3
  289.0 2.8 copy-start.12
  289.0 2.5 copy-start.1
  289.0 2.9 copy-start.5
  291.5 1.2 copy-start.11
  292.7 1.4 copy-start.9
  293.8 1.5 slice-start
  293.8 1.5 copy-start.13
  295.3 0.9 slice-start.1
  299.6 89.3 %copy-start.18 = (s32[64]{0:T(128)S(1)}, s32[64]{0:T(128)}, u32[]{:S(2)}) copy-start(s32[64]{0:T(128)} %reshape.967) | copy-start | bytes 772
  389.6 1.0 copy-start.14
  389.6 1.0 copy-start.15

commit v4 on v2

--- a/solution.py
+++ b/solution.py
@@ -32,16 +32,13 @@
 def broadcast(value, axis):
     count = lax.axis_size(axis)
     me = lax.axis_index(axis)
-    width = row_width(count)
-    got = jnp.zeros_like(value)
-    for row in range(1, count // width):
-        got = got + lax.ppermute(value, axis, [(0, row * width)])
-    value = jnp.where(me == 0, value, got)
-    got = jnp.zeros_like(value)
-    for col in range(1, width):
-        pairs = [(row * width, row * width + col) for row in range(count // width)]
-        got = got + lax.ppermute(value, axis, pairs)
-    return jnp.where(me % width == 0, value, got)
+    step = 1
+    while step < count:
+        pairs = [(i, i + step) for i in range(step) if i + step < count]
+        got = lax.ppermute(value, axis, pairs)
+        value = jnp.where((me >= step) & (me < 2 * step), got, value)
+        step *= 2
+    return value
 
 
 def reduce_to_first(value, axis):

time: 410 us -> 412 us (level)
    ppermute x10 -> x5, starting transfers between devices: 21.7 us -> 7.53 us  [broadcast(): got = lax.ppermute(value, axis, pairs)]
    all_to_all x1, starting transfers between devices: 4.86 us -> 13.3 us  [shards(): lax.all_to_all(served, 'seq', split_axis=0, concat_axis=0, tiled=True)]
    ppermute x10 -> x5, waiting for transfers between devices: 1 us -> 5.2 us  [broadcast(): got = lax.ppermute(value, axis, pairs)]
  transfers between devices with their start and end apart: 28 -> 23, of which waited for: 11 -> 12; matrix products, arithmetic and copies ran while one was open for 6% -> 6% of each run, Pallas kernels for 0% -> 0%
where the time goes in v4:
time: 412 us; the launch traced here: 411 us
  waiting for transfers between devices  225 us (55%)
  starting transfers between devices  75.4 us (18%)
  local copies, waits for them, and re-layouts  48.9 us (12%)
  blocking collectives  31.3 us (8%)
  other arithmetic  16.7 us (4%)
  matrix products  12.4 us (3%)
    ppermute x7, waiting for transfers between devices, reduce_to_first(): total = total + lax.ppermute(value, axis, [(row * width, 0)])  76.4 us
    all_to_all x1, waiting for transfers between devices, shards(): lax.all_to_all(served, 'seq', split_axis=0, concat_axis=0, tiled=True)  75.4 us
    all_to_all x1, blocking collectives, shards(): lax.all_to_all(jnp.stack([by_token(attended.reshape(flat)), by_token(grad...  31.3 us
    all_to_all x1, waiting for transfers between devices, shards(): lax.all_to_all(jnp.stack([queries, keys, values, grad_out]), 'head', spli...  26.7 us
    ppermute x3, waiting for transfers between devices, reduce_to_first(): total = total + lax.ppermute(value, axis, pairs)  25.2 us
    all_to_all x1, starting transfers between devices, shards(): lax.all_to_all(outgoing.reshape(groups, capacity, 2, head_count, BLK, HD)...  14.3 us
    all_to_all x1, starting transfers between devices, shards(): lax.all_to_all(served, 'seq', split_axis=0, concat_axis=0, tiled=True)  13.3 us
    unnamed x38, local copies, waits for them, and re-layouts  11.4 us
  transfers between devices with their start and end apart: 23, of which 12 were waited for; matrix products, arithmetic and copies ran while one was open for 6% of the time, Pallas kernels for 0%

profile of v4, /device:TPU:1, one launch (start us, length us, event | category | flops | bytes accessed | tf_op | source)
XLA Modules:
  0.0 411.0 jit_solution(5440115248499398418)
XLA Ops:
  0.6 1.3 pad_maximum_fusion.3
  2.0 1.4 copy.106
  3.4 2.3 reshape.1010
  5.6 10.3 %all-to-all-start = ((bf16[16,2,16384]{2,1,0:T(2,128)(2,1)}), bf16[16,2,16384]{2,1,0:T(2,128)(2,1)S(1)}, u32[]{:S(2)}, u32[]{:S(2)}) async-start(bf16[16,2,16384]{2,1,0:T(2,128)(2,1)} %reshape.1010), calls=%async_computation | async-start | bytes 2097152 | tf_op jit(solution)/shard_map/all_to_all | solution.py:137
  17.3 26.7 %all-to-all-done = bf16[16,2,16384]{2,1,0:T(2,128)(2,1)S(1)} async-done(((bf16[16,2,16384]{2,1,0:T(2,128)(2,1)}), bf16[16,2,16384]{2,1,0:T(2,128)(2,1)S(1)}, u32[]{:S(2)}, u32[]{:S(2)}) %all-to-all-start) | async-done | bytes 1048608 | tf_op jit(solution)/shard_map/all_to_all | solution.py:137
  43.9 1.3 reshape.1011
  45.3 2.4 copy.107
  47.6 1.3 fusion.48
  48.9 1.4 collective-permute-start
  50.3 2.6 collective-permute-done
  52.9 1.3 collective-permute-start.1
  54.2 7.3 %all-to-all-start.1 = ((s32[32,1,2]{2,1,0:T(1,128)}), s32[32,1,2]{2,1,0:T(1,128)S(1)}, u32[]{:S(2)}, u32[]{:S(2)}) async-start(s32[32,1,2]{2,1,0:T(1,128)} %bitcast.86), calls=%async_computation.1 | async-start | bytes 32768 | tf_op jit(solution)/shard_map/all_to_all | solution.py:159
  61.6 8.4 %all-to-all-done.1 = s32[32,1,2]{2,1,0:T(1,128)S(1)} async-done(((s32[32,1,2]{2,1,0:T(1,128)}), s32[32,1,2]{2,1,0:T(1,128)S(1)}, u32[]{:S(2)}, u32[]{:S(2)}) %all-to-all-start.1) | async-done | bytes 288 | tf_op jit(solution)/shard_map/all_to_all | solution.py:159
  71.4 2.3 collective-permute-start.2
  73.7 2.6 collective-permute-done.2
  76.4 1.3 collective-permute-start.3
  77.8 3.0 gather_fusion
  80.8 1.3 collective-permute-start.4
  82.1 4.6 %broadcast_select_fusion = bf16[32,2,2,1,128,128]{5,4,2,1,3,0:T(8,128)(2,1)} fusion(bf16[32,2,2,1,128,128]{5,4,2,1,3,0:T(8,128)(2,1)} %bitcast.210, pred[32,2]{1,0:T(8,128)(4,1)S(1)} %copy.112), kind=kLoop, calls=%fused_computation.8 | loop fusion | flops 2097152 | bytes 8388672 | tf_op jit(solution)/shard_map/jit(_take)/select_n | solution.py:160
  86.8 13.3 %all-to-all-start.2 = ((bf16[32,2,2,1,128,128]{5,4,2,1,3,0:T(8,128)(2,1)}), bf16[32,2,2,1,128,128]{5,4,2,1,3,0:T(8,128)(2,1)}, u32[]{:S(2)}, u32[]{:S(2)}) async-start(bf16[32,2,2,1,128,128]{5,4,2,1,3,0:T(8,128)(2,1)} %broadcast_select_fusion), calls=%async_computation.2 | async-start | bytes 8388608 | tf_op jit(solution)/shard_map/all_to_all | solution.py:163
  100.5 3.1 collective-permute-start.5
  103.6 1.5 collective-permute-start.6
  105.1 6.1 %collective-permute-done.5 = bf16[2,1,128,128]{3,2,0,1:T(8,128)(2,1)S(1)} collective-permute-done((bf16[2,1,128,128]{3,2,0,1:T(8,128)(2,1)S(1)}, bf16[2,1,128,128]{3,2,0,1:T(8,128)(2,1)S(1)}, u32[]{:S(2)}, u32[]{:S(2)}) %collective-permute-start.5) | collective-permute-done | bytes 65568 | tf_op jit(solution)/shard_map/ppermute | solution.py:19
  111.2 1.4 collective-permute-done.6
  113.6 1.7 convolution_bitcast_fusion.1
  115.5 1.3 convolution_bitcast_fusion.5
  116.8 75.4 %all-to-all-done.2 = bf16[32,2,2,1,128,128]{5,4,2,1,3,0:T(8,128)(2,1)} async-done(((bf16[32,2,2,1,128,128]{5,4,2,1,3,0:T(8,128)(2,1)}), bf16[32,2,2,1,128,128]{5,4,2,1,3,0:T(8,128)(2,1)}, u32[]{:S(2)}, u32[]{:S(2)}) %all-to-all-start.2) | async-done | bytes 4194336 | tf_op jit(solution)/shard_map/all_to_all | solution.py:163
  192.2 4.1 %gather_fusion.1 = bf16[24,2,128,128]{3,2,1,0:T(8,128)(2,1)} fusion(bf16[64,2,128,128]{3,2,1,0:T(8,128)(2,1)} %bitcast.26, s32[1024]{0:T(1024)S(1)} %pad_clamp_fusion), kind=kCustom, calls=%fused_computation.1 | custom fusion | bytes 3145824 | tf_op jit(solution)/shard_map/jit(_take)/gather | solution.py:164
  196.4 1.6 fusion.5
  198.2 0.9 copy-done.10
  200.0 1.2 fusion.2
  201.8 0.9 copy-done.6
  203.0 1.7 multiply_reduce_fusion
  204.6 1.8 multiply_convert_fusion
  208.9 1.4 convolution_convert_fusion
  210.3 6.7 %copy.133 = bf16[32,2,2,1,128,128]{5,1,4,2,3,0:T(2,128)(2,1)} copy(bf16[32,2,2,1,128,128]{5,1,0,4,2,3:T(2,128)(2,1)S(1)} %bitcast.208) | data formatting | bytes 8388608 | tf_op jit(solution)/shard_map/reshape | solution.py:210
  217.0 14.3 %all-to-all-start.3 = ((bf16[32,2,2,1,128,128]{5,1,4,2,3,0:T(2,128)(2,1)}), bf16[32,2,2,1,128,128]{5,1,4,2,3,0:T(2,128)(2,1)}, u32[]{:S(2)}, u32[]{:S(2)}) async-start(bf16[32,2,2,1,128,128]{5,1,4,2,3,0:T(2,128)(2,1)} %copy.133), calls=%async_computation.3 | async-start | bytes 8388608 | tf_op jit(solution)/shard_map/all_to_all | solution.py:209
  231.4 1.5 convolution_bitcast_fusion.8
  233.3 1.3 collective-permute-start.10
  234.6 1.3 collective-permute-start.11
  235.9 1.3 collective-permute-start.9
  239.1 0.8 copy-done.5
  240.9 0.9 copy-done.11
  242.2 8.4 %collective-permute-done.10 = f32[2,1,256,128]{3,2,1,0:T(8,128)S(1)} collective-permute-done((f32[2,1,256,128]{3,2,1,0:T(8,128)S(1)}, f32[2,1,256,128]{3,2,1,0:T(8,128)S(1)}, u32[]{:S(2)}, u32[]{:S(2)}) %collective-permute-start.10) | collective-permute-done | bytes 262176 | tf_op jit(solution)/shard_map/ppermute | solution.py:50
  250.5 16.8 %collective-permute-done.11 = f32[2,1,256,128]{3,2,1,0:T(8,128)S(1)} collective-permute-done((f32[2,1,256,128]{3,2,1,0:T(8,128)S(1)}, f32[2,1,256,128]{3,2,1,0:T(8,128)S(1)}, u32[]{:S(2)}, u32[]{:S(2)}) %collective-permute-start.11) | collective-permute-done | bytes 262176 | tf_op jit(solution)/shard_map/ppermute | solution.py:50
  267.4 1.3 collective-permute-start.18
  268.7 1.3 collective-permute-start.17
  270.5 1.3 collective-permute-start.8
  271.8 4.0 collective-permute-start.7
  276.0 1.3 collective-permute-start.16
  277.3 1.3 collective-permute-start.15
  278.7 1.3 collective-permute-start.14
  280.0 66.2 %collective-permute-done.18 = f32[2,1,256,128]{3,2,1,0:T(8,128)S(1)} collective-permute-done((f32[2,1,256,128]{3,2,1,0:T(8,128)S(1)}, f32[2,1,256,128]{3,2,1,0:T(8,128)S(1)}, u32[]{:S(2)}, u32[]{:S(2)}) %collective-permute-start.18) | collective-permute-done | bytes 262176 | tf_op jit(solution)/shard_map/ppermute | solution.py:53
  346.2 1.3 collective-permute-start.13
  347.5 1.3 collective-permute-start.12
  349.7 3.0 scatter-add.11
  352.7 2.8 collective-permute-done.13
  355.5 7.4 %collective-permute-done.12 = f32[2,1,256,128]{3,2,1,0:T(8,128)} collective-permute-done((f32[2,1,256,128]{3,2,1,0:T(8,128)S(1)}, f32[2,1,256,128]{3,2,1,0:T(8,128)}, u32[]{:S(2)}, u32[]{:S(2)}) %collective-permute-start.12) | collective-permute-done | bytes 262176 | tf_op jit(solution)/shard_map/ppermute | solution.py:53
  362.9 1.1 add_select_fusion
  364.4 7.0 %copy.134 = bf16[32,2,2,1,128,128]{5,1,0,4,2,3:T(2,128)(2,1)S(1)} copy(bf16[32,2,2,1,128,128]{5,1,4,2,3,0:T(2,128)(2,1)} %all-to-all-done.3) | data formatting | bytes 8388608 | tf_op jit(solution)/shard_map/all_to_all | solution.py:209
  372.3 0.8 copy.137
  373.1 31.3 %all_to_all.49 = bf16[4,1024,128]{2,0,1:T(4,128)(2,1)S(1)} all-to-all(bf16[4,1024,128]{2,0,1:T(4,128)(2,1)S(1)} %copy.137), channel_id=1, replica_groups=mesh['head'=16,'seq'=32] {'head'}, dimensions={1} | all-to-all | bytes 2097152 | tf_op jit(solution)/shard_map/all_to_all | solution.py:229
  404.4 2.2 fusion.47
  406.9 0.8 copy.172
  (120 shorter events, 19.1 us)
Async XLA Ops:
  3.4 12.6 %copy-start.12 = (s32[8,3]{0,1:T(4,128)S(1)}, s32[8,3]{0,1:T(4,128)}, u32[]{:S(2)}) copy-start(s32[8,3]{0,1:T(4,128)} %param.15) | copy-start | bytes 292
  5.6 38.3 %all-to-all-start = ((bf16[16,2,16384]{2,1,0:T(2,128)(2,1)}), bf16[16,2,16384]{2,1,0:T(2,128)(2,1)S(1)}, u32[]{:S(2)}, u32[]{:S(2)}) async-start(bf16[16,2,16384]{2,1,0:T(2,128)(2,1)} %reshape.1010), calls=%async_computation | async-start | bytes 2097152 | tf_op jit(solution)/shard_map/all_to_all | solution.py:137
  48.9 4.0 collective-permute-start
  52.9 18.5 %collective-permute-start.1 = (bf16[2,1,256,128]{3,2,1,0:T(8,128)(2,1)S(1)}, bf16[2,1,256,128]{3,2,1,0:T(8,128)(2,1)S(1)}, u32[]{:S(2)}, u32[]{:S(2)}) collective-permute-start(bf16[2,1,256,128]{3,2,1,0:T(8,128)(2,1)S(1)} %broadcast_select_fusion.1), channel_id=1, source_target_pairs={{0,2},{1,3},{32,34},{33,35},{64,66},{65,67},{96,98},{97,99},{128,1... | collective-permute-start | bytes 393224 | tf_op jit(solution)/shard_map/ppermute | solution.py:38
  54.2 15.8 %all-to-all-start.1 = ((s32[32,1,2]{2,1,0:T(1,128)}), s32[32,1,2]{2,1,0:T(1,128)S(1)}, u32[]{:S(2)}, u32[]{:S(2)}) async-start(s32[32,1,2]{2,1,0:T(1,128)} %bitcast.86), calls=%async_computation.1 | async-start | bytes 32768 | tf_op jit(solution)/shard_map/all_to_all | solution.py:159
  71.4 4.9 %collective-permute-start.2 = (bf16[2,1,256,128]{3,2,1,0:T(8,128)(2,1)S(1)}, bf16[2,1,256,128]{3,2,1,0:T(8,128)(2,1)S(1)}, u32[]{:S(2)}, u32[]{:S(2)}) collective-permute-start(bf16[2,1,256,128]{3,2,1,0:T(8,128)(2,1)S(1)} %broadcast_select_fusion.2), channel_id=1, source_target_pairs={{0,4},{1,5},{2,6},{3,7},{32,36},{33,37},{34,38},{35,39},{64,68},{6... | collective-permute-start | bytes 393224 | tf_op jit(solution)/shard_map/ppermute | solution.py:38
  76.4 4.5 %collective-permute-start.3 = (bf16[2,1,256,128]{3,2,1,0:T(8,128)(2,1)S(1)}, bf16[2,1,256,128]{3,2,1,0:T(8,128)(2,1)S(1)}, u32[]{:S(2)}, u32[]{:S(2)}) collective-permute-start(bf16[2,1,256,128]{3,2,1,0:T(8,128)(2,1)S(1)} %broadcast_select_fusion.3), channel_id=1, source_target_pairs={{0,8},{1,9},{2,10},{3,11},{4,12},{5,13},{6,14},{7,15},{32,40},{33,... | collective-permute-start | bytes 393224 | tf_op jit(solution)/shard_map/ppermute | solution.py:38
  80.8 6.0 %collective-permute-start.4 = (bf16[2,1,256,128]{3,2,1,0:T(8,128)(2,1)S(1)}, bf16[2,1,256,128]{3,2,1,0:T(8,128)(2,1)S(1)}, u32[]{:S(2)}, u32[]{:S(2)}) collective-permute-start(bf16[2,1,256,128]{3,2,1,0:T(8,128)(2,1)S(1)} %broadcast_select_fusion.4), channel_id=1, source_target_pairs={{0,16},{1,17},{2,18},{3,19},{4,20},{5,21},{6,22},{7,23},{8,24},{9,... | collective-permute-start | bytes 393224 | tf_op jit(solution)/shard_map/ppermute | solution.py:38
  86.8 105.4 %all-to-all-start.2 = ((bf16[32,2,2,1,128,128]{5,4,2,1,3,0:T(8,128)(2,1)}), bf16[32,2,2,1,128,128]{5,4,2,1,3,0:T(8,128)(2,1)}, u32[]{:S(2)}, u32[]{:S(2)}) async-start(bf16[32,2,2,1,128,128]{5,4,2,1,3,0:T(8,128)(2,1)} %broadcast_select_fusion), calls=%async_computation.2 | async-start | bytes 8388608 | tf_op jit(solution)/shard_map/all_to_all | solution.py:163
  100.5 10.6 %collective-permute-start.5 = (bf16[2,1,128,128]{3,2,0,1:T(8,128)(2,1)S(1)}, bf16[2,1,128,128]{3,2,0,1:T(8,128)(2,1)S(1)}, u32[]{:S(2)}, u32[]{:S(2)}) collective-permute-start(bf16[2,1,128,128]{3,2,0,1:T(8,128)(2,1)S(1)} %get-tuple-element.70), channel_id=1, source_target_pairs={{0,1},{1,2},{2,3},{3,4},{4,5},{5,6},{6,7},{7,8},{8,9},{9,10},{10,1... | collective-permute-start | bytes 196616 | tf_op jit(solution)/shard_map/ppermute | solution.py:19
  103.6 8.9 %collective-permute-start.6 = (bf16[2,1,128,128]{3,2,0,1:T(8,128)(2,1)S(1)}, bf16[2,1,128,128]{3,2,0,1:T(8,128)(2,1)S(1)}, u32[]{:S(2)}, u32[]{:S(2)}) collective-permute-start(bf16[2,1,128,128]{3,2,0,1:T(8,128)(2,1)S(1)} %get-tuple-element.71), channel_id=1, source_target_pairs={{1,0},{2,1},{3,2},{4,3},{5,4},{6,5},{7,6},{8,7},{9,8},{10,9},{11,1... | collective-permute-start | bytes 196616 | tf_op jit(solution)/shard_map/ppermute | solution.py:21
  113.1 2.2 copy-start.4
  198.1 0.9 copy-start.10
  198.2 3.1 copy-start.8
  201.3 1.4 copy-start.6
  201.3 1.7 copy-start.7
  206.4 1.4 copy-start
  206.4 2.0 copy-start.2
  217.0 16.0 %copy-start.1 = (bf16[1,8,128,1024]{3,2,1,0:T(8,128)(2,1)S(1)}, bf16[1,8,128,1024]{3,2,1,0:T(8,128)(2,1)}, u32[]{:S(2)}) copy-start(bf16[1,8,128,1024]{3,2,1,0:T(8,128)(2,1)} %copy-done) | copy-start | bytes 6291460
  217.0 147.4 %all-to-all-start.3 = ((bf16[32,2,2,1,128,128]{5,1,4,2,3,0:T(2,128)(2,1)}), bf16[32,2,2,1,128,128]{5,1,4,2,3,0:T(2,128)(2,1)}, u32[]{:S(2)}, u32[]{:S(2)}) async-start(bf16[32,2,2,1,128,128]{5,1,4,2,3,0:T(2,128)(2,1)} %copy.133), calls=%async_computation.3 | async-start | bytes 8388608 | tf_op jit(solution)/shard_map/all_to_all | solution.py:209
  231.4 5.8 %copy-start.3 = (bf16[1,8,128,1024]{3,2,1,0:T(8,128)(2,1)S(1)}, bf16[1,8,128,1024]{3,2,1,0:T(8,128)(2,1)}, u32[]{:S(2)}) copy-start(bf16[1,8,128,1024]{3,2,1,0:T(8,128)(2,1)} %copy-done.2) | copy-start | bytes 6291460
  233.3 17.2 %collective-permute-start.10 = (f32[2,1,256,128]{3,2,1,0:T(8,128)S(1)}, f32[2,1,256,128]{3,2,1,0:T(8,128)S(1)}, u32[]{:S(2)}, u32[]{:S(2)}) collective-permute-start(f32[2,1,256,128]{3,2,1,0:T(8,128)S(1)} %pad_maximum_fusion.7), channel_id=1, source_target_pairs={{2,0},{6,4},{10,8},{14,12},{18,16},{22,20},{26,24},{30,28},{34,32}... | collective-permute-start | bytes 786440 | tf_op jit(solution)/shard_map/ppermute | solution.py:50
  234.6 32.7 %collective-permute-start.11 = (f32[2,1,256,128]{3,2,1,0:T(8,128)S(1)}, f32[2,1,256,128]{3,2,1,0:T(8,128)S(1)}, u32[]{:S(2)}, u32[]{:S(2)}) collective-permute-start(f32[2,1,256,128]{3,2,1,0:T(8,128)S(1)} %pad_maximum_fusion.7), channel_id=1, source_target_pairs={{3,0},{7,4},{11,8},{15,12},{19,16},{23,20},{27,24},{31,28},{35,32}... | collective-permute-start | bytes 786440 | tf_op jit(solution)/shard_map/ppermute | solution.py:50
  235.9 31.4 %collective-permute-start.9 = (f32[2,1,256,128]{3,2,1,0:T(8,128)S(1)}, f32[2,1,256,128]{3,2,1,0:T(8,128)S(1)}, u32[]{:S(2)}, u32[]{:S(2)}) collective-permute-start(f32[2,1,256,128]{3,2,1,0:T(8,128)S(1)} %pad_maximum_fusion.7), channel_id=1, source_target_pairs={{1,0},{5,4},{9,8},{13,12},{17,16},{21,20},{25,24},{29,28},{33,32},... | collective-permute-start | bytes 786440 | tf_op jit(solution)/shard_map/ppermute | solution.py:50
  238.4 1.4 copy-start.5
  240.6 1.1 copy-start.11
  241.8 28.3 %copy-start.9 = (bf16[1,1,8,3,128,128]{5,4,3,2,1,0:T(8,128)(2,1)S(1)}, bf16[1,1,8,3,128,128]{5,4,3,2,1,0:T(8,128)(2,1)}, u32[]{:S(2)}) copy-start(bf16[1,1,8,3,128,128]{5,4,3,2,1,0:T(8,128)(2,1)} %copy-done.8) | copy-start | bytes 2359300
  267.4 78.7 %collective-permute-start.18 = (f32[2,1,256,128]{3,2,1,0:T(8,128)S(1)}, f32[2,1,256,128]{3,2,1,0:T(8,128)S(1)}, u32[]{:S(2)}, u32[]{:S(2)}) collective-permute-start(f32[2,1,256,128]{3,2,1,0:T(8,128)S(1)} %add_add_fusion), channel_id=1, source_target_pairs={{28,0},{60,32},{92,64},{124,96},{156,128},{188,160},{220,192},{252... | collective-permute-start | bytes 786440 | tf_op jit(solution)/shard_map/ppermute | solution.py:53
  268.7 78.7 %collective-permute-start.17 = (f32[2,1,256,128]{3,2,1,0:T(8,128)S(1)}, f32[2,1,256,128]{3,2,1,0:T(8,128)S(1)}, u32[]{:S(2)}, u32[]{:S(2)}) collective-permute-start(f32[2,1,256,128]{3,2,1,0:T(8,128)S(1)} %add_add_fusion), channel_id=1, source_target_pairs={{24,0},{56,32},{88,64},{120,96},{152,128},{184,160},{216,192},{248... | collective-permute-start | bytes 786440 | tf_op jit(solution)/shard_map/ppermute | solution.py:53
  270.5 6.8 %collective-permute-start.8 = (bf16[2,1,128,128]{3,2,0,1:T(8,128)(2,1)S(1)}, bf16[2,1,128,128]{3,2,0,1:T(8,128)(2,1)S(1)}, u32[]{:S(2)}, u32[]{:S(2)}) collective-permute-start(bf16[2,1,128,128]{3,2,0,1:T(8,128)(2,1)S(1)} %bitcast.264), channel_id=1, source_target_pairs={{1,0},{2,1},{3,2},{4,3},{5,4},{6,5},{7,6},{8,7},{9,8},{10,9},{11,1... | collective-permute-start | bytes 196616 | tf_op jit(solution)/shard_map/ppermute | solution.py:21
  271.8 6.8 %collective-permute-start.7 = (bf16[2,1,128,128]{3,2,0,1:T(8,128)(2,1)S(1)}, bf16[2,1,128,128]{3,2,0,1:T(8,128)(2,1)S(1)}, u32[]{:S(2)}, u32[]{:S(2)}) collective-permute-start(bf16[2,1,128,128]{3,2,0,1:T(8,128)(2,1)S(1)} %bitcast.262), channel_id=1, source_target_pairs={{0,1},{1,2},{2,3},{3,4},{4,5},{5,6},{6,7},{7,8},{8,9},{9,10},{10,1... | collective-permute-start | bytes 196616 | tf_op jit(solution)/shard_map/ppermute | solution.py:19
  276.0 76.6 %collective-permute-start.16 = (f32[2,1,256,128]{3,2,1,0:T(8,128)S(1)}, f32[2,1,256,128]{3,2,1,0:T(8,128)S(1)}, u32[]{:S(2)}, u32[]{:S(2)}) collective-permute-start(f32[2,1,256,128]{3,2,1,0:T(8,128)S(1)} %add_add_fusion), channel_id=1, source_target_pairs={{20,0},{52,32},{84,64},{116,96},{148,128},{180,160},{212,192},{244... | collective-permute-start | bytes 786440 | tf_op jit(solution)/shard_map/ppermute | solution.py:53
  277.3 75.3 %collective-permute-start.15 = (f32[2,1,256,128]{3,2,1,0:T(8,128)S(1)}, f32[2,1,256,128]{3,2,1,0:T(8,128)S(1)}, u32[]{:S(2)}, u32[]{:S(2)}) collective-permute-start(f32[2,1,256,128]{3,2,1,0:T(8,128)S(1)} %add_add_fusion), channel_id=1, source_target_pairs={{16,0},{48,32},{80,64},{112,96},{144,128},{176,160},{208,192},{240... | collective-permute-start | bytes 786440 | tf_op jit(solution)/shard_map/ppermute | solution.py:53
  278.7 74.0 %collective-permute-start.14 = (f32[2,1,256,128]{3,2,1,0:T(8,128)S(1)}, f32[2,1,256,128]{3,2,1,0:T(8,128)S(1)}, u32[]{:S(2)}, u32[]{:S(2)}) collective-permute-start(f32[2,1,256,128]{3,2,1,0:T(8,128)S(1)} %add_add_fusion), channel_id=1, source_target_pairs={{12,0},{44,32},{76,64},{108,96},{140,128},{172,160},{204,192},{236... | collective-permute-start | bytes 786440 | tf_op jit(solution)/shard_map/ppermute | solution.py:53
  346.2 9.3 %collective-permute-start.13 = (f32[2,1,256,128]{3,2,1,0:T(8,128)S(1)}, f32[2,1,256,128]{3,2,1,0:T(8,128)}, u32[]{:S(2)}, u32[]{:S(2)}) collective-permute-start(f32[2,1,256,128]{3,2,1,0:T(8,128)S(1)} %add_add_fusion), channel_id=1, source_target_pairs={{8,0},{40,32},{72,64},{104,96},{136,128},{168,160},{200,192},{232,... | collective-permute-start | bytes 786440 | tf_op jit(solution)/shard_map/ppermute | solution.py:53
  347.5 15.4 %collective-permute-start.12 = (f32[2,1,256,128]{3,2,1,0:T(8,128)S(1)}, f32[2,1,256,128]{3,2,1,0:T(8,128)}, u32[]{:S(2)}, u32[]{:S(2)}) collective-permute-start(f32[2,1,256,128]{3,2,1,0:T(8,128)S(1)} %add_add_fusion), channel_id=1, source_target_pairs={{4,0},{36,32},{68,64},{100,96},{132,128},{164,160},{196,192},{228,... | collective-permute-start | bytes 786440 | tf_op jit(solution)/shard_map/ppermute | solution.py:53

commit v5 on v2

--- a/solution.py
+++ b/solution.py
@@ -71,6 +71,31 @@
     return table.reshape(groups, capacity)
 
 
+def mirror_shift(groups):
+    return max(1, groups * 27 // 32) % groups
+
+
+def route(list_rows, query_count, groups, capacity):
+    flat_rows = list_rows.reshape(-1)
+    owners = flat_rows // query_count
+    places = slot_places(owners, groups, capacity)
+    rank = places - owners * capacity
+    source = jnp.where(rank == 0, owners, (owners + mirror_shift(groups)) % groups)
+    held_id = jnp.where(rank == 0, flat_rows % query_count, query_count + flat_rows % query_count)
+    hits = (source[None, :] == jnp.arange(groups, dtype=jnp.int32)[:, None]).astype(jnp.int32)
+    fits = jnp.logical_and(jnp.all(jnp.sum(hits, axis=1) <= 1), jnp.all(rank <= 1))
+    fast_table = jnp.sum(hits * held_id[None, :], axis=1)
+    table = jnp.concatenate(
+        [
+            request_table(list_rows, query_count, groups, capacity),
+            fast_table[:, None],
+            jnp.broadcast_to(fits.astype(jnp.int32), (groups, 1)),
+        ],
+        axis=1,
+    )
+    return table, places, source
+
+
 def window_valid(my_group, query_count, groups):
     block_ids = jnp.arange(query_count, dtype=jnp.int32)
     left_ok = jnp.logical_not(jnp.logical_and(my_group == 0, block_ids == 0))
@@ -145,9 +170,9 @@
     query_count = group_tokens // BLK
     capacity = max(2, 3 * query_count * RAND // (2 * groups))
     score_scale = HD ** (-0.5)
-    ordered_table, head_k = lax.optimization_barrier(
-        (request_table(random_blocks, query_count, groups, capacity), head_k)
-    )
+    ordered_table, places, source = route(random_blocks, query_count, groups, capacity)
+    ordered_table, head_k = lax.optimization_barrier((ordered_table, head_k))
+    shift = mirror_shift(groups)
     key_value = jnp.stack([by_head(head_k, head_count), by_head(head_v, head_count)])
     kv_blocks = key_value.reshape(2, head_count, query_count, BLK, HD)
     edged = with_halo(key_value, (("seq", 2),), BLK)
@@ -157,14 +182,26 @@
         axis=3,
     )
     global_kv = broadcast(kv_blocks[:, :, 0:2].reshape(2, head_count, 2 * BLK, HD), "seq")
-    flat_ids = random_blocks.reshape(-1)
-    places = slot_places(flat_ids // query_count, groups, capacity)
-    wanted = lax.all_to_all(ordered_table, "seq", split_axis=0, concat_axis=0, tiled=True)
-    served = jnp.take(jnp.transpose(kv_blocks, (2, 0, 1, 3, 4)), wanted.reshape(-1), axis=0)
-    served = served.reshape(groups, capacity, 2, head_count, BLK, HD)
-    served, global_kv = lax.optimization_barrier((served, global_kv))
-    fetched = lax.all_to_all(served, "seq", split_axis=0, concat_axis=0, tiled=True)
-    chosen = jnp.take(fetched.reshape(groups * capacity, 2, head_count, BLK, HD), places, axis=0)
+    received = lax.all_to_all(ordered_table, "seq", split_axis=0, concat_axis=0, tiled=True)
+    wanted = received[:, :capacity]
+    wanted_fast = received[:, capacity]
+    take_fast = jnp.all(received[:, capacity + 1] == 1)
+    mirror = lax.ppermute(kv_blocks, "seq", [(i, (i + shift) % groups) for i in range(groups)])
+    held = jnp.transpose(jnp.concatenate([kv_blocks, mirror], axis=2), (2, 0, 1, 3, 4))
+    held, global_kv = lax.optimization_barrier((held, global_kv))
+
+    def fetch_fast(held):
+        served = jnp.take(held, wanted_fast, axis=0)
+        fetched = lax.all_to_all(served, "seq", split_axis=0, concat_axis=0, tiled=True)
+        return jnp.take(fetched, source, axis=0)
+
+    def fetch_all(held):
+        served = jnp.take(held[:query_count], wanted.reshape(-1), axis=0)
+        served = served.reshape(groups, capacity, 2, head_count, BLK, HD)
+        fetched = lax.all_to_all(served, "seq", split_axis=0, concat_axis=0, tiled=True)
+        return jnp.take(fetched.reshape(groups * capacity, 2, head_count, BLK, HD), places, axis=0)
+
+    chosen = lax.cond(take_fast, fetch_fast, fetch_all, held)
     remote_kv = jnp.transpose(
         chosen.reshape(query_count, RAND, 2, head_count, BLK, HD), (2, 3, 0, 1, 4, 5)
     ).reshape(2, head_count, query_count, RAND * BLK, HD)
@@ -203,28 +240,49 @@
         jnp.stack([key_random, value_random]).reshape(2, head_count, query_count * RAND, BLK, HD),
         (2, 0, 1, 3, 4),
     ).astype(jnp.bfloat16)
-    send_pick = (places[None, :] == jnp.arange(groups * capacity, dtype=jnp.int32)[:, None]).astype(
-        jnp.bfloat16
-    )
-    outgoing = jnp.einsum(
-        "pj,jxhid->pxhid", send_pick, random_terms, preferred_element_type=jnp.float32
-    ).astype(jnp.bfloat16)
-    incoming = lax.all_to_all(
-        outgoing.reshape(groups, capacity, 2, head_count, BLK, HD),
-        "seq",
-        split_axis=0,
-        concat_axis=0,
-        tiled=True,
-    )
-    take_pick = (
-        wanted.reshape(-1)[None, :] == jnp.arange(query_count, dtype=jnp.int32)[:, None]
-    ).astype(jnp.bfloat16)
-    random_sum = jnp.einsum(
-        "qp,pxhid->xhqid",
-        take_pick,
-        incoming.reshape(groups * capacity, 2, head_count, BLK, HD),
-        preferred_element_type=jnp.float32,
-    )
+
+    def return_fast(random_terms):
+        send_pick = (source[None, :] == jnp.arange(groups, dtype=jnp.int32)[:, None]).astype(
+            jnp.bfloat16
+        )
+        outgoing = jnp.einsum(
+            "pj,jxhid->pxhid", send_pick, random_terms, preferred_element_type=jnp.float32
+        ).astype(jnp.bfloat16)
+        incoming = lax.all_to_all(outgoing, "seq", split_axis=0, concat_axis=0, tiled=True)
+        take_pick = (
+            wanted_fast[None, :] == jnp.arange(2 * query_count, dtype=jnp.int32)[:, None]
+        ).astype(jnp.bfloat16)
+        sums = jnp.einsum("qp,pxhid->xhqid", take_pick, incoming, preferred_element_type=jnp.float32)
+        back = lax.ppermute(
+            sums[:, :, query_count:], "seq", [((i + shift) % groups, i) for i in range(groups)]
+        )
+        return sums[:, :, :query_count] + back
+
+    def return_all(random_terms):
+        send_pick = (
+            places[None, :] == jnp.arange(groups * capacity, dtype=jnp.int32)[:, None]
+        ).astype(jnp.bfloat16)
+        outgoing = jnp.einsum(
+            "pj,jxhid->pxhid", send_pick, random_terms, preferred_element_type=jnp.float32
+        ).astype(jnp.bfloat16)
+        incoming = lax.all_to_all(
+            outgoing.reshape(groups, capacity, 2, head_count, BLK, HD),
+            "seq",
+            split_axis=0,
+            concat_axis=0,
+            tiled=True,
+        )
+        take_pick = (
+            wanted.reshape(-1)[None, :] == jnp.arange(query_count, dtype=jnp.int32)[:, None]
+        ).astype(jnp.bfloat16)
+        return jnp.einsum(
+            "qp,pxhid->xhqid",
+            take_pick,
+            incoming.reshape(groups * capacity, 2, head_count, BLK, HD),
+            preferred_element_type=jnp.float32,
+        )
+
+    random_sum = lax.cond(take_fast, return_fast, return_all, random_terms)
     global_sum = global_sum.reshape(2, head_count, 2, BLK, HD)
     own_grad = own_grad.at[:, :, 0:2].add(jnp.where(my_group == 0, global_sum, 0.0))
     total_grad = (own_grad + random_sum).astype(jnp.bfloat16)

time: 410 us -> 428 us (1.044); the launches traced: 409 us -> 419 us
  blocking collectives: 31.3 us -> 87.7 us
  waiting for transfers between devices: 221 us -> 166 us
  local copies, waits for them, and re-layouts: 48.9 us -> 32.4 us
  loops' own time: 0 us -> 12.3 us
  other arithmetic: 16.7 us -> 24.3 us
    all_to_all x0 -> x1, blocking collectives: none -> 55.8 us  [return_fast(): lax.all_to_all(outgoing, 'seq', split_axis=0, concat_axis=0, tiled=True)]
    ppermute x0 -> x2, waiting for transfers between devices: none -> 52.6 us  [the longest x1 47 us: return_fast(): lax.ppermute(sums[:, :, query_count:], 'seq', [((i + shift) % groups, i)...]
    ppermute x7, waiting for transfers between devices: 76.3 us -> 31.3 us  [reduce_to_first(): total = total + lax.ppermute(value, axis, [(row * width, 0)])]
    all_to_all x2 -> x1, waiting for transfers between devices: 73.5 us -> 47.8 us  [fetch_fast(): lax.all_to_all(served, 'seq', split_axis=0, concat_axis=0, tiled=True)]
    ppermute x3, waiting for transfers between devices: 25.3 us -> 0.01 us  [reduce_to_first(): total = total + lax.ppermute(value, axis, pairs)]
    another operation x0 -> x2, loops' own time: none -> 12.3 us  [the longest x1 12 us: shards(): chosen = lax.cond(take_fast, fetch_fast, fetch_all, held)]
    all_to_all x2 -> x1, starting transfers between devices: 19.1 us -> 10.8 us  [fetch_fast(): lax.all_to_all(served, 'seq', split_axis=0, concat_axis=0, tiled=True)]
    all_to_all x1 -> x0, local copies, waits for them, and re-layouts: 6.97 us -> none  [shards(): lax.all_to_all(outgoing.reshape(groups, capacity, 2, head_count, BLK, HD)...]
  transfers between devices with their start and end apart: 28 -> 29, of which waited for: 11 -> 12; matrix products, arithmetic and copies ran while one was open for 6% -> 6% of each run, Pallas kernels for 0% -> 0%
where the time goes in v5:
time: 428 us; the launch traced here: 419 us
  waiting for transfers between devices  166 us (39%)
  blocking collectives  87.7 us (20%)
  starting transfers between devices  77.5 us (18%)
  local copies, waits for them, and re-layouts  32.4 us (8%)
  other arithmetic  24.3 us (6%)
  matrix products  15.2 us (4%)
  loops' own time  12.3 us (3%)
    all_to_all x1, blocking collectives, return_fast(): lax.all_to_all(outgoing, 'seq', split_axis=0, concat_axis=0, tiled=True)  55.8 us
    all_to_all x1, waiting for transfers between devices, fetch_fast(): lax.all_to_all(served, 'seq', split_axis=0, concat_axis=0, tiled=True)  47.8 us
    ppermute x1, waiting for transfers between devices, return_fast(): lax.ppermute(sums[:, :, query_count:], 'seq', [((i + shift) % groups, i)...  47 us
    all_to_all x1, blocking collectives, shards(): lax.all_to_all(jnp.stack([by_token(attended.reshape(flat)), by_token(grad...  31.9 us
    ppermute x7, waiting for transfers between devices, reduce_to_first(): total = total + lax.ppermute(value, axis, [(row * width, 0)])  31.3 us
    all_to_all x1, waiting for transfers between devices, shards(): lax.all_to_all(jnp.stack([queries, keys, values, grad_out]), 'head', spli...  23.6 us
    ppermute x7, starting transfers between devices, broadcast(): got = got + lax.ppermute(value, axis, [(0, row * width)])  23.4 us
    another operation x1, loops' own time, shards(): chosen = lax.cond(take_fast, fetch_fast, fetch_all, held)  12 us
  transfers between devices with their start and end apart: 29, of which 12 were waited for; matrix products, arithmetic and copies ran while one was open for 6% of the time, Pallas kernels for 0%

profile of v5, /device:TPU:1, one launch (start us, length us, event | category | flops | bytes accessed | tf_op | source)
XLA Modules:
  0.0 419.3 jit_solution(5291259325900883388)
XLA Ops:
  0.6 1.3 pad_maximum_fusion.3
  2.0 1.4 copy.134
  3.4 2.3 reshape.1006
  5.6 10.3 %all-to-all-start.4 = ((bf16[16,2,16384]{2,1,0:T(2,128)(2,1)}), bf16[16,2,16384]{2,1,0:T(2,128)(2,1)S(1)}, u32[]{:S(2)}, u32[]{:S(2)}) async-start(bf16[16,2,16384]{2,1,0:T(2,128)(2,1)} %reshape.1006), calls=%async_computation.4 | async-start | bytes 2097152 | tf_op jit(solution)/shard_map/all_to_all | solution.py:165
  20.4 23.6 %all-to-all-done.4 = bf16[16,2,16384]{2,1,0:T(2,128)(2,1)S(1)} async-done(((bf16[16,2,16384]{2,1,0:T(2,128)(2,1)}), bf16[16,2,16384]{2,1,0:T(2,128)(2,1)S(1)}, u32[]{:S(2)}, u32[]{:S(2)}) %all-to-all-start.4) | async-done | bytes 1048608 | tf_op jit(solution)/shard_map/all_to_all | solution.py:165
  43.9 1.3 reshape.1007
  45.3 2.3 copy.135
  48.9 8.9 %collective-permute-start.8 = (bf16[2,1,256,128]{3,2,1,0:T(8,128)(2,1)S(1)}, bf16[2,1,256,128]{3,2,1,0:T(8,128)(2,1)S(1)}, u32[]{:S(2)}, u32[]{:S(2)}) collective-permute-start(bf16[2,1,256,128]{3,2,1,0:T(8,128)(2,1)S(1)} %bitcast.292), channel_id=1, source_target_pairs={{0,28},{32,60},{64,92},{96,124},{128,156},{160,188},{192,220},{224... | collective-permute-start | bytes 393224 | tf_op jit(solution)/shard_map/ppermute | solution.py:38
  57.8 1.3 collective-permute-start.7
  59.1 2.0 collective-permute-start.6
  62.6 3.8 all-to-all-start.5
  66.5 3.0 collective-permute-start.12
  69.5 1.3 collective-permute-start.13
  70.8 4.1 all-to-all-done.5
  76.9 7.2 %collective-permute-start.5 = (bf16[2,1,256,128]{3,2,1,0:T(8,128)(2,1)S(1)}, bf16[2,1,256,128]{3,2,1,0:T(8,128)(2,1)S(1)}, u32[]{:S(2)}, u32[]{:S(2)}) collective-permute-start(bf16[2,1,256,128]{3,2,1,0:T(8,128)(2,1)S(1)} %bitcast.295), channel_id=1, source_target_pairs={{0,16},{32,48},{64,80},{96,112},{128,144},{160,176},{192,208},{224... | collective-permute-start | bytes 393224 | tf_op jit(solution)/shard_map/ppermute | solution.py:38
  84.1 1.3 collective-permute-start.4
  86.0 1.4 collective-permute-start.3
  87.4 1.3 collective-permute-start.2
  89.3 1.9 collective-permute-start.1
  91.2 1.4 collective-permute-done.3
  92.7 2.8 collective-permute-done.2
  96.5 1.3 collective-permute-start.11
  97.8 1.3 collective-permute-start.10
  99.1 1.3 collective-permute-start.9
  100.4 1.6 convolution_bitcast_fusion.2
  102.2 2.1 collective-permute-done.9
  104.3 5.6 %collective-permute-done.1 = bf16[2,1,8,128,128]{4,3,1,0,2:T(8,128)(2,1)S(1)} collective-permute-done((bf16[2,1,8,128,128]{4,3,1,0,2:T(8,128)(2,1)S(1)}, bf16[2,1,8,128,128]{4,3,1,0,2:T(8,128)(2,1)S(1)}, u32[]{:S(2)}, u32[]{:S(2)}) %collective-permute-start.1) | collective-permute-done | bytes 524320 | tf_op jit(solution)/shard_map/ppermute | solution.py:189
  111.3 1.3 convolution_bitcast_fusion.5
  112.6 84.7 %conditional.2 = (bf16[24,2,1,128,128]{4,3,1,0,2:T(8,128)(2,1)}) conditional(s32[]{:T(128)} %convert_element_type.101, (s32[24]{0:T(128)}, s32[32,2]{0,1:T(2,128)S(1)}, bf16[16,2,1,128,128]{4,3,2,1,0:T(8,128)(2,1)}) %tuple.80, (s32[24]{0:T(128)}, s32[32,1]{0,1:T(1,128)}, bf16[16,2,1,128,128]{4,3,2,1,0:T(8,128)(2,1)}) %tuple.78), branch_computations={%region_8.9_spmd, %region_9.10_spmd} | conditional | flops 2886424 | bytes 36711764 | solution.py:204
  113.9 3.4 gather_fusion.2
  117.2 3.2 bitcast_select_fusion.1
  120.4 10.8 %all-to-all-start.2 = ((bf16[32,2,1,128,128]{4,3,1,2,0:T(8,128)(2,1)}), bf16[32,2,1,128,128]{4,3,1,2,0:T(8,128)(2,1)}, u32[]{:S(2)}, u32[]{:S(2)}) async-start(bf16[32,2,1,128,128]{4,3,1,2,0:T(8,128)(2,1)} %bitcast_select_fusion.1), calls=%async_computation.2 | async-start | bytes 4194304 | tf_op jit(solution)/shard_map/cond/branch_1_fun/all_to_all | solution.py:195
  131.2 47.8 %all-to-all-done.2 = bf16[32,2,1,128,128]{4,3,1,2,0:T(8,128)(2,1)} async-done(((bf16[32,2,1,128,128]{4,3,1,2,0:T(8,128)(2,1)}), bf16[32,2,1,128,128]{4,3,1,2,0:T(8,128)(2,1)}, u32[]{:S(2)}, u32[]{:S(2)}) %all-to-all-start.2) | async-done | bytes 2097184 | tf_op jit(solution)/shard_map/cond/branch_1_fun/all_to_all | solution.py:195
  179.0 3.5 gather_fusion.3
  182.5 2.8 bitcast_select_fusion.2
  197.3 1.5 copy.198
  203.7 1.7 multiply_reduce_fusion
  205.4 1.8 multiply_convert_fusion
  207.9 1.3 pad_maximum_fusion.7
  209.2 1.3 collective-permute-start.17
  210.5 1.3 collective-permute-start.18
  211.8 1.3 collective-permute-start.16
  217.3 1.3 pad_add_fusion
  221.5 1.3 collective-permute-start.15
  222.8 109.7 %conditional.3 = (f32[2,1,8,128,128]{4,3,2,1,0:T(8,128)S(1)}) conditional(s32[]{:T(128)} %convert_element_type.101, (s32[24]{0:T(128)S(1)}, bf16[24,2,1,128,128]{4,0,3,1,2:T(8,128)(2,1)S(1)}, s32[32,2]{0,1:T(2,128)S(1)}) %tuple.81, (s32[24]{0:T(128)S(1)}, bf16[24,2,1,128,128]{4,0,3,1,2:T(8,128)(2,1)S(1)}, s32[32,1]{0,1:T(1,128)S(1)}) %tuple.82), branch_computations={%region_13.14_spmd, %region_14.15_spmd} | conditional | flops 136316928 | bytes 42468744 | solution.py:285
  224.6 55.8 %all_to_all.58 = bf16[32,2,1,128,128]{4,3,1,2,0:T(8,128)(2,1)S(1)} all-to-all(bf16[32,2,1,128,128]{4,3,1,2,0:T(8,128)(2,1)S(1)} %copy.132), channel_id=1, replica_groups=mesh['head'=16,'seq'=32] {'seq'}, dimensions={0} | all-to-all | bytes 4194304 | tf_op jit(solution)/shard_map/cond/branch_1_fun/all_to_all | solution.py:251
  280.4 1.3 fusion.10
  281.8 3.4 collective-permute-start
  285.2 47.0 %collective-permute-done = f32[2,1,8,128,128]{4,2,3,0,1:T(8,128)S(1)} collective-permute-done((f32[2,1,8,128,128]{4,2,3,0,1:T(8,128)S(1)}, f32[2,1,8,128,128]{4,2,3,0,1:T(8,128)S(1)}, u32[]{:S(2)}, u32[]{:S(2)}) %collective-permute-start) | collective-permute-done | bytes 1048608 | tf_op jit(solution)/shard_map/cond/branch_1_fun/ppermute | solution.py:256
  332.6 1.4 collective-permute-start.14
  334.0 1.6 fusion.26
  336.9 1.3 collective-permute-start.25
  338.2 1.3 collective-permute-start.24
  339.6 1.5 fusion.25
  341.1 1.3 collective-permute-start.23
  342.4 1.3 collective-permute-start.22
  343.7 1.3 collective-permute-start.21
  345.0 17.9 %collective-permute-done.25 = f32[2,1,256,128]{3,2,1,0:T(8,128)S(1)} collective-permute-done((f32[2,1,256,128]{3,2,1,0:T(8,128)S(1)}, f32[2,1,256,128]{3,2,1,0:T(8,128)S(1)}, u32[]{:S(2)}, u32[]{:S(2)}) %collective-permute-start.25) | collective-permute-done | bytes 262176 | tf_op jit(solution)/shard_map/ppermute | solution.py:56
  362.9 1.3 collective-permute-start.20
  364.2 1.3 collective-permute-start.19
  365.7 5.3 %collective-permute-done.20 = f32[2,1,256,128]{3,2,1,0:T(8,128)S(1)} collective-permute-done((f32[2,1,256,128]{3,2,1,0:T(8,128)S(1)}, f32[2,1,256,128]{3,2,1,0:T(8,128)S(1)}, u32[]{:S(2)}, u32[]{:S(2)}) %collective-permute-start.20) | collective-permute-done | bytes 262176 | tf_op jit(solution)/shard_map/ppermute | solution.py:56
  371.0 8.1 %collective-permute-done.19 = f32[2,1,256,128]{3,2,1,0:T(8,128)S(1)} collective-permute-done((f32[2,1,256,128]{3,2,1,0:T(8,128)S(1)}, f32[2,1,256,128]{3,2,1,0:T(8,128)S(1)}, u32[]{:S(2)}, u32[]{:S(2)}) %collective-permute-start.19) | collective-permute-done | bytes 262176 | tf_op jit(solution)/shard_map/ppermute | solution.py:56
  380.4 31.9 %all_to_all.59 = bf16[4,1024,128]{2,0,1:T(4,128)(2,1)S(1)} all-to-all(bf16[4,1024,128]{2,0,1:T(4,128)(2,1)S(1)} %copy.159), channel_id=1, replica_groups=mesh['head'=16,'seq'=32] {'head'}, dimensions={1} | all-to-all | bytes 2097152 | tf_op jit(solution)/shard_map/all_to_all | solution.py:290
  412.3 2.2 fusion.52
  (168 shorter events, 33.6 us)
Async XLA Ops:
  3.4 12.6 %copy-start.27 = (s32[8,3]{0,1:T(4,128)S(1)}, s32[8,3]{0,1:T(4,128)}, u32[]{:S(2)}) copy-start(s32[8,3]{0,1:T(4,128)} %param.19) | copy-start | bytes 292
  5.6 38.3 %all-to-all-start.4 = ((bf16[16,2,16384]{2,1,0:T(2,128)(2,1)}), bf16[16,2,16384]{2,1,0:T(2,128)(2,1)S(1)}, u32[]{:S(2)}, u32[]{:S(2)}) async-start(bf16[16,2,16384]{2,1,0:T(2,128)(2,1)} %reshape.1006), calls=%async_computation.4 | async-start | bytes 2097152 | tf_op jit(solution)/shard_map/all_to_all | solution.py:165
  17.1 0.6 copy-start.21
  17.1 2.7 copy-start.24
  48.9 62.1 %copy-start.5 = (bf16[1,16,64,128]{3,2,1,0:T(8,128)(2,1)}, bf16[1,16,64,128]{3,2,1,0:T(8,128)(2,1)S(1)}, u32[]{:S(2)}) copy-start(bf16[1,16,64,128]{3,2,1,0:T(8,128)(2,1)S(1)} %get-tuple-element.142) | copy-start | bytes 786436
  48.9 37.1 %collective-permute-start.8 = (bf16[2,1,256,128]{3,2,1,0:T(8,128)(2,1)S(1)}, bf16[2,1,256,128]{3,2,1,0:T(8,128)(2,1)S(1)}, u32[]{:S(2)}, u32[]{:S(2)}) collective-permute-start(bf16[2,1,256,128]{3,2,1,0:T(8,128)(2,1)S(1)} %bitcast.292), channel_id=1, source_target_pairs={{0,28},{32,60},{64,92},{96,124},{128,156},{160,188},{192,220},{224... | collective-permute-start | bytes 393224 | tf_op jit(solution)/shard_map/ppermute | solution.py:38
  57.8 29.6 %collective-permute-start.7 = (bf16[2,1,256,128]{3,2,1,0:T(8,128)(2,1)S(1)}, bf16[2,1,256,128]{3,2,1,0:T(8,128)(2,1)S(1)}, u32[]{:S(2)}, u32[]{:S(2)}) collective-permute-start(bf16[2,1,256,128]{3,2,1,0:T(8,128)(2,1)S(1)} %bitcast.293), channel_id=1, source_target_pairs={{0,24},{32,56},{64,88},{96,120},{128,152},{160,184},{192,216},{224... | collective-permute-start | bytes 393224 | tf_op jit(solution)/shard_map/ppermute | solution.py:38
  59.1 30.1 %collective-permute-start.6 = (bf16[2,1,256,128]{3,2,1,0:T(8,128)(2,1)S(1)}, bf16[2,1,256,128]{3,2,1,0:T(8,128)(2,1)}, u32[]{:S(2)}, u32[]{:S(2)}) collective-permute-start(bf16[2,1,256,128]{3,2,1,0:T(8,128)(2,1)S(1)} %bitcast.294), channel_id=1, source_target_pairs={{0,20},{32,52},{64,84},{96,116},{128,148},{160,180},{192,212},{224... | collective-permute-start | bytes 393224 | tf_op jit(solution)/shard_map/ppermute | solution.py:38
  62.6 12.3 %all-to-all-start.5 = ((s32[32,1,4]{2,1,0:T(1,128)}), s32[32,1,4]{2,1,0:T(1,128)S(1)}, u32[]{:S(2)}, u32[]{:S(2)}) async-start(s32[32,1,4]{2,1,0:T(1,128)} %copy.140), calls=%async_computation.5 | async-start | bytes 32768 | tf_op jit(solution)/shard_map/all_to_all | solution.py:185
  66.5 10.4 %collective-permute-start.12 = (bf16[2,1,128,128]{3,2,0,1:T(8,128)(2,1)S(1)}, bf16[2,1,128,128]{3,2,0,1:T(8,128)(2,1)S(1)}, u32[]{:S(2)}, u32[]{:S(2)}) collective-permute-start(bf16[2,1,128,128]{3,2,0,1:T(8,128)(2,1)S(1)} %get-tuple-element.148), channel_id=1, source_target_pairs={{0,1},{1,2},{2,3},{3,4},{4,5},{5,6},{6,7},{7,8},{8,9},{9,10},{10,1... | collective-permute-start | bytes 196616 | tf_op jit(solution)/shard_map/ppermute | solution.py:19
  69.5 14.6 %collective-permute-start.13 = (bf16[2,1,128,128]{3,2,0,1:T(8,128)(2,1)S(1)}, bf16[2,1,128,128]{3,2,0,1:T(8,128)(2,1)S(1)}, u32[]{:S(2)}, u32[]{:S(2)}) collective-permute-start(bf16[2,1,128,128]{3,2,0,1:T(8,128)(2,1)S(1)} %get-tuple-element.149), channel_id=1, source_target_pairs={{1,0},{2,1},{3,2},{4,3},{5,4},{6,5},{7,6},{8,7},{9,8},{10,9},{11,1... | collective-permute-start | bytes 196616 | tf_op jit(solution)/shard_map/ppermute | solution.py:21
  76.9 14.3 %collective-permute-start.5 = (bf16[2,1,256,128]{3,2,1,0:T(8,128)(2,1)S(1)}, bf16[2,1,256,128]{3,2,1,0:T(8,128)(2,1)S(1)}, u32[]{:S(2)}, u32[]{:S(2)}) collective-permute-start(bf16[2,1,256,128]{3,2,1,0:T(8,128)(2,1)S(1)} %bitcast.295), channel_id=1, source_target_pairs={{0,16},{32,48},{64,80},{96,112},{128,144},{160,176},{192,208},{224... | collective-permute-start | bytes 393224 | tf_op jit(solution)/shard_map/ppermute | solution.py:38
  84.1 7.1 %collective-permute-start.4 = (bf16[2,1,256,128]{3,2,1,0:T(8,128)(2,1)S(1)}, bf16[2,1,256,128]{3,2,1,0:T(8,128)(2,1)S(1)}, u32[]{:S(2)}, u32[]{:S(2)}) collective-permute-start(bf16[2,1,256,128]{3,2,1,0:T(8,128)(2,1)S(1)} %bitcast.296), channel_id=1, source_target_pairs={{0,12},{32,44},{64,76},{96,108},{128,140},{160,172},{192,204},{224... | collective-permute-start | bytes 393224 | tf_op jit(solution)/shard_map/ppermute | solution.py:38
  86.0 16.0 %copy-start.2 = (bf16[2,1,8,384,128]{4,3,2,1,0:T(8,128)(2,1)}, bf16[2,1,8,384,128]{4,3,2,1,0:T(8,128)(2,1)S(1)}, u32[]{:S(2)}) copy-start(bf16[2,1,8,384,128]{4,3,2,1,0:T(8,128)(2,1)S(1)} %pad_maximum_fusion.1) | copy-start | bytes 4718596
  86.0 3.3 copy-start.14
  86.0 6.7 %collective-permute-start.3 = (bf16[2,1,256,128]{3,2,1,0:T(8,128)(2,1)S(1)}, bf16[2,1,256,128]{3,2,1,0:T(8,128)(2,1)S(1)}, u32[]{:S(2)}, u32[]{:S(2)}) collective-permute-start(bf16[2,1,256,128]{3,2,1,0:T(8,128)(2,1)S(1)} %bitcast.297), channel_id=1, source_target_pairs={{0,8},{32,40},{64,72},{96,104},{128,136},{160,168},{192,200},{224,... | collective-permute-start | bytes 393224 | tf_op jit(solution)/shard_map/ppermute | solution.py:38
  87.4 1.3 copy-start.19
  87.4 8.0 %collective-permute-start.2 = (bf16[2,1,256,128]{3,2,1,0:T(8,128)(2,1)S(1)}, bf16[2,1,256,128]{3,2,1,0:T(8,128)(2,1)S(1)}, u32[]{:S(2)}, u32[]{:S(2)}) collective-permute-start(bf16[2,1,256,128]{3,2,1,0:T(8,128)(2,1)S(1)} %bitcast.298), channel_id=1, source_target_pairs={{0,4},{32,36},{64,68},{96,100},{128,132},{160,164},{192,196},{224,... | collective-permute-start | bytes 393224 | tf_op jit(solution)/shard_map/ppermute | solution.py:38
  88.8 6.7 %copy-start.20 = (bf16[2,1,256,128]{3,2,1,0:T(8,128)(2,1)S(1)}, bf16[2,1,256,128]{3,2,1,0:T(8,128)(2,1)}, u32[]{:S(2)}) copy-start(bf16[2,1,256,128]{3,2,1,0:T(8,128)(2,1)} %copy-done.19) | copy-start | bytes 393220
  89.3 20.6 %collective-permute-start.1 = (bf16[2,1,8,128,128]{4,3,1,0,2:T(8,128)(2,1)S(1)}, bf16[2,1,8,128,128]{4,3,1,0,2:T(8,128)(2,1)S(1)}, u32[]{:S(2)}, u32[]{:S(2)}) collective-permute-start(bf16[2,1,8,128,128]{4,3,1,0,2:T(8,128)(2,1)S(1)} %copy-done.14), channel_id=1, source_target_pairs={{0,27},{1,28},{2,29},{3,30},{4,31},{5,0},{6,1},{7,2},{8,3},{9,4},{... | collective-permute-start | bytes 1572872 | tf_op jit(solution)/shard_map/ppermute | solution.py:189
  96.5 5.7 %collective-permute-start.11 = (bf16[2,1,256,128]{3,2,1,0:T(8,128)(2,1)S(1)}, bf16[2,1,256,128]{3,2,1,0:T(8,128)(2,1)S(1)}, u32[]{:S(2)}, u32[]{:S(2)}) collective-permute-start(bf16[2,1,256,128]{3,2,1,0:T(8,128)(2,1)S(1)} %add_select_fusion.2), channel_id=1, source_target_pairs={{0,3},{4,7},{8,11},{12,15},{16,19},{20,23},{24,27},{28,31},{32,35}... | collective-permute-start | bytes 393224 | tf_op jit(solution)/shard_map/ppermute | solution.py:43
  97.8 4.4 %collective-permute-start.10 = (bf16[2,1,256,128]{3,2,1,0:T(8,128)(2,1)S(1)}, bf16[2,1,256,128]{3,2,1,0:T(8,128)(2,1)S(1)}, u32[]{:S(2)}, u32[]{:S(2)}) collective-permute-start(bf16[2,1,256,128]{3,2,1,0:T(8,128)(2,1)S(1)} %add_select_fusion.2), channel_id=1, source_target_pairs={{0,2},{4,6},{8,10},{12,14},{16,18},{20,22},{24,26},{28,30},{32,34}... | collective-permute-start | bytes 393224 | tf_op jit(solution)/shard_map/ppermute | solution.py:43
  99.1 5.2 %collective-permute-start.9 = (bf16[2,1,256,128]{3,2,1,0:T(8,128)(2,1)S(1)}, bf16[2,1,256,128]{3,2,1,0:T(8,128)(2,1)S(1)}, u32[]{:S(2)}, u32[]{:S(2)}) collective-permute-start(bf16[2,1,256,128]{3,2,1,0:T(8,128)(2,1)S(1)} %add_select_fusion.2), channel_id=1, source_target_pairs={{0,1},{4,5},{8,9},{12,13},{16,17},{20,21},{24,25},{28,29},{32,33},... | collective-permute-start | bytes 393224 | tf_op jit(solution)/shard_map/ppermute | solution.py:43
  120.4 10.8 %copy-start.23 = (s32[24]{0:T(128)S(1)}, s32[24]{0:T(128)}, u32[]{:S(2)}) copy-start(s32[24]{0:T(128)} %get-tuple-element.70) | copy-start | bytes 292 | tf_op jit(solution)/shard_map/cond
  120.4 58.6 %all-to-all-start.2 = ((bf16[32,2,1,128,128]{4,3,1,2,0:T(8,128)(2,1)}), bf16[32,2,1,128,128]{4,3,1,2,0:T(8,128)(2,1)}, u32[]{:S(2)}, u32[]{:S(2)}) async-start(bf16[32,2,1,128,128]{4,3,1,2,0:T(8,128)(2,1)} %bitcast_select_fusion.1), calls=%async_computation.2 | async-start | bytes 4194304 | tf_op jit(solution)/shard_map/cond/branch_1_fun/all_to_all | solution.py:195
  198.8 1.0 copy-start.6
  198.9 1.9 copy-start.10
  199.0 3.1 copy-start.8
  202.0 1.4 copy-start.4
  202.0 1.7 copy-start.7
  207.2 11.3 %copy-start.1 = (bf16[1,8,128,1024]{3,2,1,0:T(8,128)(2,1)}, bf16[1,8,128,1024]{3,2,1,0:T(8,128)(2,1)S(1)}, u32[]{:S(2)}) copy-start(bf16[1,8,128,1024]{3,2,1,0:T(8,128)(2,1)S(1)} %get-tuple-element.126) | copy-start | bytes 6291460
  207.2 13.1 %copy-start = (bf16[1,8,128,1024]{3,2,1,0:T(8,128)(2,1)}, bf16[1,8,128,1024]{3,2,1,0:T(8,128)(2,1)S(1)}, u32[]{:S(2)}) copy-start(bf16[1,8,128,1024]{3,2,1,0:T(8,128)(2,1)S(1)} %get-tuple-element.127) | copy-start | bytes 6291460
  207.6 6.6 %copy-start.15 = (f32[1,1,256,128]{3,2,1,0:T(8,128)}, f32[1,1,256,128]{3,2,1,0:T(8,128)S(1)}, u32[]{:S(2)}) copy-start(f32[1,1,256,128]{3,2,1,0:T(8,128)S(1)} %convolution_bitcast_fusion.8) | copy-start | bytes 393220
  207.9 6.2 %copy-start.17 = (f32[1,1,256,128]{3,2,1,0:T(8,128)}, f32[1,1,256,128]{3,2,1,0:T(8,128)S(1)}, u32[]{:S(2)}) copy-start(f32[1,1,256,128]{3,2,1,0:T(8,128)S(1)} %convolution_bitcast_fusion.7) | copy-start | bytes 393220
  209.2 126.5 %collective-permute-start.17 = (f32[2,1,256,128]{3,2,1,0:T(8,128)}, f32[2,1,256,128]{3,2,1,0:T(8,128)}, u32[]{:S(2)}, u32[]{:S(2)}) collective-permute-start(f32[2,1,256,128]{3,2,1,0:T(8,128)} %pad_maximum_fusion.7), channel_id=1, source_target_pairs={{2,0},{6,4},{10,8},{14,12},{18,16},{22,20},{26,24},{30,28},{34,32}... | collective-permute-start | bytes 786440 | tf_op jit(solution)/shard_map/ppermute | solution.py:53
  210.5 125.2 %collective-permute-start.18 = (f32[2,1,256,128]{3,2,1,0:T(8,128)}, f32[2,1,256,128]{3,2,1,0:T(8,128)}, u32[]{:S(2)}, u32[]{:S(2)}) collective-permute-start(f32[2,1,256,128]{3,2,1,0:T(8,128)} %pad_maximum_fusion.7), channel_id=1, source_target_pairs={{3,0},{7,4},{11,8},{15,12},{19,16},{23,20},{27,24},{31,28},{35,32}... | collective-permute-start | bytes 786440 | tf_op jit(solution)/shard_map/ppermute | solution.py:53
  211.8 123.9 %collective-permute-start.16 = (f32[2,1,256,128]{3,2,1,0:T(8,128)}, f32[2,1,256,128]{3,2,1,0:T(8,128)}, u32[]{:S(2)}, u32[]{:S(2)}) collective-permute-start(f32[2,1,256,128]{3,2,1,0:T(8,128)} %pad_maximum_fusion.7), channel_id=1, source_target_pairs={{1,0},{5,4},{9,8},{13,12},{17,16},{21,20},{25,24},{29,28},{33,32},... | collective-permute-start | bytes 786440 | tf_op jit(solution)/shard_map/ppermute | solution.py:53
  217.2 1.9 copy-start.3
  219.1 2.4 copy-start.22
  219.1 2.4 copy-start.25
  219.1 2.4 copy-start.28
  221.5 120.9 %collective-permute-start.15 = (bf16[2,1,128,128]{3,2,0,1:T(8,128)(2,1)S(1)}, bf16[2,1,128,128]{3,2,0,1:T(8,128)(2,1)S(1)}, u32[]{:S(2)}, u32[]{:S(2)}) collective-permute-start(bf16[2,1,128,128]{3,2,0,1:T(8,128)(2,1)S(1)} %bitcast.306), channel_id=1, source_target_pairs={{1,0},{2,1},{3,2},{4,3},{5,4},{6,5},{7,6},{8,7},{9,8},{10,9},{11,1... | collective-permute-start | bytes 196616 | tf_op jit(solution)/shard_map/ppermute | solution.py:21
  281.8 50.4 %collective-permute-start = (f32[2,1,8,128,128]{4,2,3,0,1:T(8,128)S(1)}, f32[2,1,8,128,128]{4,2,3,0,1:T(8,128)S(1)}, u32[]{:S(2)}, u32[]{:S(2)}) collective-permute-start(f32[2,1,8,128,128]{4,2,3,0,1:T(8,128)S(1)} %slice.284), channel_id=1, source_target_pairs={{27,0},{28,1},{29,2},{30,3},{31,4},{0,5},{1,6},{2,7},{3,8},{4,9},{... | collective-permute-start | bytes 3145736 | tf_op jit(solution)/shard_map/cond/branch_1_fun/ppermute | solution.py:256
  332.5 1.5 copy-start.11
  332.5 1.5 copy-start.13
  332.5 3.2 copy-start.16
  332.5 3.2 copy-start.18
  332.6 11.1 %collective-permute-start.14 = (bf16[2,1,128,128]{3,2,0,1:T(8,128)(2,1)S(1)}, bf16[2,1,128,128]{3,2,0,1:T(8,128)(2,1)S(1)}, u32[]{:S(2)}, u32[]{:S(2)}) collective-permute-start(bf16[2,1,128,128]{3,2,0,1:T(8,128)(2,1)S(1)} %bitcast.304), channel_id=1, source_target_pairs={{0,1},{1,2},{2,3},{3,4},{4,5},{5,6},{6,7},{7,8},{8,9},{9,10},{10,1... | collective-permute-start | bytes 196616 | tf_op jit(solution)/shard_map/ppermute | solution.py:19
  334.0 5.5 %copy-start.9 = (bf16[1,1,8,3,128,128]{5,4,3,2,1,0:T(8,128)(2,1)S(1)}, bf16[1,1,8,3,128,128]{5,4,3,2,1,0:T(8,128)(2,1)}, u32[]{:S(2)}) copy-start(bf16[1,1,8,3,128,128]{5,4,3,2,1,0:T(8,128)(2,1)} %copy-done.8) | copy-start | bytes 2359300
  334.0 5.5 %copy-start.12 = (f32[8,128,128]{2,1,0:T(8,128)S(1)}, f32[8,128,128]{2,1,0:T(8,128)}, u32[]{:S(2)}) copy-start(f32[8,128,128]{2,1,0:T(8,128)} %convolution_add_fusion.3) | copy-start | bytes 1572868
  335.6 29.8 %slice-start = ((f32[2,1,10,128,128]{4,3,0,2,1:T(8,128)}), f32[2,1,8,128,128]{4,3,0,2,1:T(8,128)S(1)}, s32[]{:S(2)}) async-start(f32[2,1,10,128,128]{4,3,0,2,1:T(8,128)} %pad_add_fusion), calls=%async_computation.7 | async-start | bytes 2097152 | tf_op jit(solution)/shard_map/slice | solution.py:236
  336.9 25.9 %collective-permute-start.25 = (f32[2,1,256,128]{3,2,1,0:T(8,128)S(1)}, f32[2,1,256,128]{3,2,1,0:T(8,128)S(1)}, u32[]{:S(2)}, u32[]{:S(2)}) collective-permute-start(f32[2,1,256,128]{3,2,1,0:T(8,128)S(1)} %add_add_fusion), channel_id=1, source_target_pairs={{28,0},{60,32},{92,64},{124,96},{156,128},{188,160},{220,192},{252... | collective-permute-start | bytes 786440 | tf_op jit(solution)/shard_map/ppermute | solution.py:56
  338.2 25.9 %collective-permute-start.24 = (f32[2,1,256,128]{3,2,1,0:T(8,128)S(1)}, f32[2,1,256,128]{3,2,1,0:T(8,128)S(1)}, u32[]{:S(2)}, u32[]{:S(2)}) collective-permute-start(f32[2,1,256,128]{3,2,1,0:T(8,128)S(1)} %add_add_fusion), channel_id=1, source_target_pairs={{24,0},{56,32},{88,64},{120,96},{152,128},{184,160},{216,192},{248... | collective-permute-start | bytes 786440 | tf_op jit(solution)/shard_map/ppermute | solution.py:56
  341.1 24.5 %collective-permute-start.23 = (f32[2,1,256,128]{3,2,1,0:T(8,128)S(1)}, f32[2,1,256,128]{3,2,1,0:T(8,128)S(1)}, u32[]{:S(2)}, u32[]{:S(2)}) collective-permute-start(f32[2,1,256,128]{3,2,1,0:T(8,128)S(1)} %add_add_fusion), channel_id=1, source_target_pairs={{20,0},{52,32},{84,64},{116,96},{148,128},{180,160},{212,192},{244... | collective-permute-start | bytes 786440 | tf_op jit(solution)/shard_map/ppermute | solution.py:56
  342.4 23.2 %collective-permute-start.22 = (f32[2,1,256,128]{3,2,1,0:T(8,128)S(1)}, f32[2,1,256,128]{3,2,1,0:T(8,128)S(1)}, u32[]{:S(2)}, u32[]{:S(2)}) collective-permute-start(f32[2,1,256,128]{3,2,1,0:T(8,128)S(1)} %add_add_fusion), channel_id=1, source_target_pairs={{16,0},{48,32},{80,64},{112,96},{144,128},{176,160},{208,192},{240... | collective-permute-start | bytes 786440 | tf_op jit(solution)/shard_map/ppermute | solution.py:56
  343.7 21.9 %collective-permute-start.21 = (f32[2,1,256,128]{3,2,1,0:T(8,128)S(1)}, f32[2,1,256,128]{3,2,1,0:T(8,128)S(1)}, u32[]{:S(2)}, u32[]{:S(2)}) collective-permute-start(f32[2,1,256,128]{3,2,1,0:T(8,128)S(1)} %add_add_fusion), channel_id=1, source_target_pairs={{12,0},{44,32},{76,64},{108,96},{140,128},{172,160},{204,192},{236... | collective-permute-start | bytes 786440 | tf_op jit(solution)/shard_map/ppermute | solution.py:56
  362.9 8.1 %collective-permute-start.20 = (f32[2,1,256,128]{3,2,1,0:T(8,128)S(1)}, f32[2,1,256,128]{3,2,1,0:T(8,128)S(1)}, u32[]{:S(2)}, u32[]{:S(2)}) collective-permute-start(f32[2,1,256,128]{3,2,1,0:T(8,128)S(1)} %add_add_fusion), channel_id=1, source_target_pairs={{8,0},{40,32},{72,64},{104,96},{136,128},{168,160},{200,192},{232,... | collective-permute-start | bytes 786440 | tf_op jit(solution)/shard_map/ppermute | solution.py:56
  364.2 14.9 %collective-permute-start.19 = (f32[2,1,256,128]{3,2,1,0:T(8,128)S(1)}, f32[2,1,256,128]{3,2,1,0:T(8,128)S(1)}, u32[]{:S(2)}, u32[]{:S(2)}) collective-permute-start(f32[2,1,256,128]{3,2,1,0:T(8,128)S(1)} %add_add_fusion), channel_id=1, source_target_pairs={{4,0},{36,32},{68,64},{100,96},{132,128},{164,160},{196,192},{228,... | collective-permute-start | bytes 786440 | tf_op jit(solution)/shard_map/ppermute | solution.py:56
